TPU v7x, 256 devices: a whole 4x4x8 slice. The times are simulated.
256 devices in a mesh: dp: 2 (over core), ctx: 32 (over y, z), tensor: 4 (over x).
Axes of the slice: x: 4, y: 4, z: 8, core: 2. Of those that a mesh axis runs over, the one named last changes fastest.
Arguments:
- query_in: bfloat16 [2, 8192, 8192], P('dp', 'ctx', 'tensor'), may hold values from -6 to 6
- key_in: bfloat16 [2, 8192, 8192], P('dp', 'ctx', 'tensor'), may hold values from -6 to 6
- value_in: bfloat16 [2, 8192, 8192], P('dp', 'ctx', 'tensor'), may hold values from -6 to 6
- grad_out: bfloat16 [2, 8192, 8192], P('dp', 'ctx', 'tensor'), may hold values from -6 to 6
- seq_lengths: int32 [2, 64], P('dp'), may hold values from 1 to 512, 8192 in all within a row
- filters: bfloat16 [512, 128], P('tensor'), may hold values from -0.5 to 0.5
Outputs:
- mixed_out: bfloat16 [2, 8192, 8192], P('dp', 'ctx', 'tensor')
- grad_query: bfloat16 [2, 8192, 8192], P('dp', 'ctx', 'tensor')
- grad_key: bfloat16 [2, 8192, 8192], P('dp', 'ctx', 'tensor')
- grad_value: bfloat16 [2, 8192, 8192], P('dp', 'ctx', 'tensor')
- grad_filters: float32 [512, 128], P('tensor')
All inputs are finite; a program needn't handle non-finite values.
Results may differ from a plain program's by a relative error of at most 0.005.
Values may be sent and summed in bfloat16 or wider, within the bound.
No kernel may reach another device: no remote copies, remote signals or barrier semaphores. Data moves between devices by JAX's collectives and lax.ppermute only.
A program may use at most 192 MiB of HBM per device.

v0:
```python
import math

import jax
import jax.numpy as jnp
from jax import lax
from jax.sharding import PartitionSpec as P

GROUP = 16
FLEN = 128
GROUPS = 512


def passed_along(value, axis, steps):
    count = lax.axis_size(axis)
    initial, last = (max(0, -steps), min(count, count - steps))
    return lax.ppermute(value, axis, [(source, source + steps) for source in range(initial, last)])


def on_device(query_in, key_in, value_in, grad_out, seq_lengths, filters):
    query = query_in[0].astype(jnp.float32)
    keys = key_in[0].astype(jnp.float32)
    values = value_in[0].astype(jnp.float32)
    upstream = grad_out[0].astype(jnp.float32)
    lengths = seq_lengths[0]
    starts = jnp.cumsum(lengths) - lengths
    rows_dev, channels = query.shape
    blocks = rows_dev // FLEN
    local_groups = channels // GROUP
    offset = lax.axis_index("ctx") * rows_dev
    gated = (keys * values).astype(jnp.bfloat16)
    cotangent = (upstream * query).astype(jnp.bfloat16)
    gated_cols = gated.reshape(rows_dev, local_groups, GROUP).transpose(1, 2, 0)
    cot_cols = cotangent.reshape(rows_dev, local_groups, GROUP).transpose(1, 2, 0)
    prev_tail = passed_along(gated_cols[:, :, rows_dev - FLEN :], "ctx", 1)
    u_joined = jnp.concatenate([prev_tail, gated_cols], axis=2)
    row_ids = jnp.arange(FLEN, dtype=jnp.int32)[:, None]
    col_ids = jnp.arange(2 * FLEN, dtype=jnp.int32)[None, :]
    lag_table = row_ids - col_ids + FLEN
    inside = (lag_table >= 0) & (lag_table < FLEN)
    reversed_taps = filters[:, ::-1]
    row_pattern = jnp.concatenate(
        [
            jnp.zeros((local_groups, 1), jnp.bfloat16),
            reversed_taps,
            jnp.zeros((local_groups, FLEN), jnp.bfloat16),
        ],
        axis=1,
    )
    tiled = jnp.broadcast_to(row_pattern[:, None, :], (local_groups, FLEN, 2 * FLEN + 1))
    toeplitz = tiled.reshape(local_groups, FLEN * (2 * FLEN + 1))[:, : FLEN * 2 * FLEN].reshape(
        local_groups, FLEN, 2 * FLEN
    )

    def operator_of(block_id):
        tpos = offset + block_id * FLEN + jnp.arange(FLEN, dtype=jnp.int32)
        rpos = offset + (block_id - 1) * FLEN + jnp.arange(2 * FLEN, dtype=jnp.int32)
        doc_begin = jnp.max(jnp.where(starts[None, :] <= tpos[:, None], starts[None, :], 0), axis=1)
        inside_doc = (rpos[None, :] >= doc_begin[:, None]) & inside
        return (toeplitz * inside_doc.astype(jnp.bfloat16)[None], inside_doc.astype(jnp.float32))

    def per_block(accum, block_id):
        operator, valid = operator_of(block_id)
        window = lax.dynamic_slice_in_dim(u_joined, block_id * FLEN, 2 * FLEN, 2)
        cot_block = lax.dynamic_slice_in_dim(cot_cols, block_id * FLEN, FLEN, 2)
        mixed_rows = jnp.einsum(
            "gtr,gcr->gct", operator, window, preferred_element_type=jnp.float32
        )
        back_rows = jnp.einsum(
            "gtr,gct->gcr", operator, cot_block, preferred_element_type=jnp.float32
        )
        products = jnp.einsum("gct,gcr->gtr", cot_block, window, preferred_element_type=jnp.float32)
        accum = accum + products * valid[None]
        return (accum, (mixed_rows, back_rows))

    start_accum = jnp.zeros((local_groups, FLEN, 2 * FLEN), jnp.float32)
    accum, (mixed_blocks, back_blocks) = lax.scan(
        per_block, start_accum, jnp.arange(blocks, dtype=jnp.int32)
    )
    flat = accum.reshape(local_groups, FLEN * 2 * FLEN)
    flat = jnp.pad(flat, ((0, 0), (0, FLEN)))
    skewed = flat.reshape(local_groups, FLEN, 2 * FLEN + 1)
    lag_sums = jnp.sum(skewed, axis=1)[:, 1 : FLEN + 1]
    local_raw = lag_sums[:, ::-1]
    next_head = passed_along(cot_cols[:, :, :FLEN], "ctx", -1)
    next_operator, next_valid = operator_of(blocks)
    spill_last = jnp.einsum(
        "gtr,gct->gcr", next_operator, next_head, preferred_element_type=jnp.float32
    )[:, :, :FLEN]
    own_rows = back_blocks[:, :, :, FLEN:]
    spill_rows = jnp.concatenate([back_blocks[1:, :, :, :FLEN], spill_last[None]], axis=0)
    grad_gated = (own_rows + spill_rows).transpose(0, 3, 1, 2).reshape(rows_dev, channels)
    mixed = mixed_blocks.transpose(0, 3, 1, 2).reshape(rows_dev, channels)
    mixed_out = (query * mixed).astype(jnp.bfloat16)
    grad_query = (upstream * mixed).astype(jnp.bfloat16)
    grad_key = (grad_gated * values).astype(jnp.bfloat16)
    grad_value = (grad_gated * keys).astype(jnp.bfloat16)
    clip_limit = math.sqrt(GROUPS * FLEN)
    summed = lax.psum(local_raw, ("dp", "ctx"))
    squares = lax.psum(jnp.sum(summed * summed), "tensor")
    factor = jnp.minimum(1.0, clip_limit / jnp.sqrt(squares))
    grad_filters = summed * factor
    return (mixed_out[None], grad_query[None], grad_key[None], grad_value[None], grad_filters)


def solution(mesh):
    in_specs = (
        P("dp", "ctx", "tensor"),
        P("dp", "ctx", "tensor"),
        P("dp", "ctx", "tensor"),
        P("dp", "ctx", "tensor"),
        P("dp", None),
        P("tensor", None),
    )
    out_specs = (
        P("dp", "ctx", "tensor"),
        P("dp", "ctx", "tensor"),
        P("dp", "ctx", "tensor"),
        P("dp", "ctx", "tensor"),
        P("tensor", None),
    )
    return jax.shard_map(
        on_device, mesh=mesh, in_specs=in_specs, out_specs=out_specs, check_vma=False
    )
```

profile of v0, /device:TPU:32, one launch (start us, length us, event | category | flops | bytes accessed | tf_op | source)
XLA Modules:
  0.0 368.9 jit_solution(4789059327670511102)
XLA Ops:
  7.2 0.0 all-reduce.3.cloned.1.call-start
  7.2 1.5 copy.48
  8.7 1.9 copy.49
  10.6 0.3 fusion.34
  10.9 1.1 slice.29
  12.0 0.1 copy-done.8
  12.1 3.8 %collective-permute-start = (bf16[128,16,128]{2,1,0:T(8,128)(2,1)}, bf16[128,16,128]{2,1,0:T(8,128)(2,1)}, u32[]{:S(2)}, u32[]{:S(2)}) collective-permute-start(bf16[128,16,128]{2,1,0:T(8,128)(2,1)} %slice.29), channel_id=1, source_target_pairs={{0,4},{4,8},{8,12},{12,16},{16,20},{20,24},{24,28},{28,32},{32,36}... | collective-permute-start | bytes 1572872 | tf_op jit(solution)/shard_map/ppermute | solution.py:16
  15.9 0.5 copy.46
  16.5 2.6 copy.47
  19.1 1.5 fusion.31
  20.6 0.1 slice.31
  20.7 2.8 collective-permute-start.1
  23.6 0.1 rev.6
  23.7 0.1 pad.9.clone
  23.8 0.1 maximum_maximum_fusion
  23.9 0.1 copy.51
  24.0 4.4 %broadcast_in_dim.81 = bf16[128,128,257]{0,2,1:T(8,128)(2,1)} broadcast(bf16[128,257]{0,1:T(8,128)(2,1)S(1)} %copy.51), dimensions={0,2} | broadcast | bytes 8487168 | tf_op jit(solution)/shard_map/broadcast_in_dim | solution.py:49
  28.4 12.9 %reshape.186 = bf16[128,32896]{0,1:T(8,128)(2,1)} reshape(bf16[128,128,257]{0,2,1:T(8,128)(2,1)} %broadcast_in_dim.81) | data formatting | bytes 16842752 | tf_op jit(solution)/shard_map/reshape | solution.py:50
  41.4 7.1 %slice.30 = bf16[128,32768]{0,1:T(8,128)(2,1)} slice(bf16[128,32896]{0,1:T(8,128)(2,1)} %reshape.186), slice={[0:128], [0:32768]} | slice | bytes 16777216 | tf_op jit(solution)/shard_map/slice | solution.py:50
  48.4 12.5 %copy.52 = bf16[128,128,256]{2,1,0:T(8,128)(2,1)} copy(bf16[128,128,256]{0,2,1:T(8,128)(2,1)} %bitcast.51) | data formatting | bytes 16777216
  60.9 0.1 copy.50
  61.0 0.1 reduce-window.4
  61.1 0.1 reduce
  61.2 0.1 select_reduce_fusion.1
  61.3 0.1 fusion.43
  61.5 1.6 pad_maximum_fusion
  63.0 37.5 %while.17 = (s32[]{:T(128)}, f32[128,128,256]{2,1,0:T(8,128)}, f32[2,128,16,128]{3,2,1,0:T(8,128)}, f32[2,128,16,256]{3,2,1,0:T(8,128)}, s32[2]{0:T(128)S(1)}, /...) while((s32[]{:T(128)}, f32[128,128,256]{2,1,0:T(8,128)}, ...), condition=%wide.region_3.4_spmd.clone, body=%wide.region_1.3_spmd.clone.sunk | while | flops 423944448 | bytes 90641992 | solution.py:76
  63.1 0.6 dynamic_slice.39
  64.3 0.1 select_reduce_fusion.3
  65.1 0.1 fusion.60
  65.2 7.9 %select_add_fusion.2 = f32[128,128,256]{2,1,0:T(8,128)} fusion(f32[128,128,256]{2,1,0:T(8,128)} %get-tuple-element.335, f32[128,256]{1,0:T(8,128)S(1)} %get-tuple-element.316, pred[]{:T(512)S(6)} %compare.4, bf16[128,16,384]{2,1,0:T(8,128)(2,1)S(1)} %get-tuple-element.356, s32[]{:T(128)S(6)} %select_n.32, ...), kind=kOutput, calls=%fused_computation.1.clone.1 | convolution fusion | flops 146800640 | bytes 35258376 | tf_op jit(solution)/shard_map/while/body/eval_jaxpr/gct,gcr->gtr/dot_general | solution.py:71
  73.1 2.7 bitcast_dynamic-update-slice_fusion.2
  75.7 3.3 fusion.61
  79.0 0.6 dynamic_slice.39
  80.3 0.1 select_reduce_fusion.3
  81.1 0.1 fusion.60
  81.2 12.9 %select_add_fusion.2 = f32[128,128,256]{2,1,0:T(8,128)} fusion(f32[128,128,256]{2,1,0:T(8,128)} %get-tuple-element.335, f32[128,256]{1,0:T(8,128)S(1)} %get-tuple-element.316, pred[]{:T(512)S(6)} %compare.4, bf16[128,16,384]{2,1,0:T(8,128)(2,1)S(1)} %get-tuple-element.356, s32[]{:T(128)S(6)} %select_n.32, ...), kind=kOutput, calls=%fused_computation.1.clone.1 | convolution fusion | flops 146800640 | bytes 35258376 | tf_op jit(solution)/shard_map/while/body/eval_jaxpr/gct,gcr->gtr/dot_general | solution.py:71
  94.1 0.5 copy-done
  94.6 2.6 bitcast_dynamic-update-slice_fusion.2
  97.2 3.3 fusion.61
  100.5 1.3 slice.24
  101.8 3.6 fusion.38
  105.4 1.9 fusion.37
  107.3 2.9 copy.55
  110.3 4.1 %reshape.190 = f32[1,256,2048]{1,2,0:T(8,128)} reshape(f32[2,128,128,16]{1,0,3,2:T(2,128)} %copy.55) | data formatting | bytes 4194304 | tf_op jit(solution)/shard_map/reshape | solution.py:91
  114.4 2.9 fusion.33
  117.3 17.8 %copy.62 = f32[128,128,256]{0,2,1:T(8,128)} copy(f32[128,128,256]{2,1,0:T(8,128)} %get-tuple-element.146) | data formatting | bytes 33554432 | tf_op jit(solution)/shard_map/reshape | solution.py:79
  135.1 13.3 %pad.4 = f32[128,32896]{0,1:T(8,128)} pad(f32[128,32768]{0,1:T(8,128)} %bitcast.48, f32[]{:T(128)} %constant.68.clone.1), padding=0_0x0_128 | pad | bytes 33619972 | tf_op jit(solution)/shard_map/jit(_pad)/pad | solution.py:80
  148.4 17.5 %reshape.192 = f32[128,128,257]{0,2,1:T(8,128)} reshape(f32[128,32896]{0,1:T(8,128)} %pad.4) | data formatting | bytes 33685504 | tf_op jit(solution)/shard_map/reshape | solution.py:81
  165.9 6.7 %reduce_sum.18 = f32[128,257]{0,1:T(8,128)S(1)} reduce(f32[128,128,257]{0,2,1:T(8,128)} %reshape.192, f32[]{:T(128)} %constant.68.clone.1), dimensions={1}, to_apply=%region_5.6 | reduce | flops 4177792 | bytes 16974340 | tf_op jit(solution)/shard_map/reduce_sum | solution.py:82
  172.7 0.6 rev.7
  173.3 0.0 all-reduce.3.cloned.1.call-update
  173.3 4.6 %copy.53 = f32[2,128,128,16]{1,0,3,2:T(2,128)} copy(f32[2,128,128,16]{1,3,2,0:T(8,128)} %bitcast.7) | data formatting | bytes 4194304 | tf_op jit(solution)/shard_map/transpose | solution.py:92
  177.9 4.0 %reshape.188 = f32[1,256,2048]{1,2,0:T(8,128)} reshape(f32[2,128,128,16]{1,0,3,2:T(2,128)} %copy.53) | data formatting | bytes 4194304 | tf_op jit(solution)/shard_map/reshape | solution.py:92
  182.0 3.3 fusion.32
  185.2 2.4 copy.59
  187.7 1.4 copy.60
  189.1 1.4 copy.57
  190.5 155.3 %all-reduce.3.cloned.1.call-done = f32[128,128]{0,1:T(8,128)} async-done(((f32[128,128]{0,1:T(8,128)}), f32[128,128]{0,1:T(8,128)}) %all-reduce.3.cloned.1.call-update) | async-done | bytes 65552 | tf_op jit(solution)/shard_map/psum | solution.py:98
  345.8 1.5 multiply_reduce_fusion
  347.3 1.4 copy.58
  348.7 11.0 %psum.15 = f32[]{:T(128)} all-reduce(f32[]{:T(128)} %multiply_reduce_fusion), channel_id=1, replica_groups=mesh['dp'=2,'ctx'=32,'tensor'=4] {'tensor'}, use_global_device_ids=true, to_apply=%region_8.9 | all-reduce | flops 1 | bytes 8 | tf_op jit(solution)/shard_map/psum | solution.py:99
  360.4 0.8 broadcast_multiply_fusion
  361.3 0.7 copy.61
  (46 shorter events, 0.1 us)
Async XLA Ops:
  7.2 338.7 %all-reduce.3.cloned.1.call-start = ((), (), s32[]{:S(2)}) async-start(), calls=%async_computation | async-start | bytes 131072 | tf_op jit(solution)/shard_map/psum | solution.py:98
  8.7 3.3 copy-start.4
  8.7 7.2 %copy-start.11 = (bf16[1,256,2048]{2,1,0:T(8,128)(2,1)S(1)}, bf16[1,256,2048]{2,1,0:T(8,128)(2,1)}, u32[]{:S(2)}) copy-start(bf16[1,256,2048]{2,1,0:T(8,128)(2,1)} %param.8) | copy-start | bytes 3145732
  10.6 5.9 %copy-start.6 = (bf16[1,256,2048]{1,2,0:T(8,128)(2,1)}, bf16[1,256,2048]{1,2,0:T(8,128)(2,1)S(1)}, u32[]{:S(2)}) copy-start(bf16[1,256,2048]{1,2,0:T(8,128)(2,1)S(1)} %copy.49) | copy-start | bytes 3145732
  10.9 1.2 copy-start.8
  12.1 49.4 %collective-permute-start = (bf16[128,16,128]{2,1,0:T(8,128)(2,1)}, bf16[128,16,128]{2,1,0:T(8,128)(2,1)}, u32[]{:S(2)}, u32[]{:S(2)}) collective-permute-start(bf16[128,16,128]{2,1,0:T(8,128)(2,1)} %slice.29), channel_id=1, source_target_pairs={{0,4},{4,8},{8,12},{12,16},{16,20},{20,24},{24,28},{28,32},{32,36}... | collective-permute-start | bytes 1572872 | tf_op jit(solution)/shard_map/ppermute | solution.py:16
  16.5 4.3 %copy-start.1 = (bf16[1,256,2048]{1,2,0:T(8,128)(2,1)}, bf16[1,256,2048]{1,2,0:T(8,128)(2,1)S(1)}, u32[]{:S(2)}) copy-start(bf16[1,256,2048]{1,2,0:T(8,128)(2,1)S(1)} %copy.46) | copy-start | bytes 3145732
  16.5 7.1 %copy-start.12 = (bf16[128,128]{1,0:T(8,128)(2,1)S(1)}, bf16[128,128]{1,0:T(8,128)(2,1)}, u32[]{:S(2)}) copy-start(bf16[128,128]{1,0:T(8,128)(2,1)} %param.13) | copy-start | bytes 98308
  20.7 81.1 %collective-permute-start.1 = (bf16[128,16,128]{2,1,0:T(8,128)(2,1)S(1)}, bf16[128,16,128]{2,1,0:T(8,128)(2,1)}, u32[]{:S(2)}, u32[]{:S(2)}) collective-permute-start(bf16[128,16,128]{2,1,0:T(8,128)(2,1)S(1)} %slice.31), channel_id=1, source_target_pairs={{4,0},{8,4},{12,8},{16,12},{20,16},{24,20},{28,24},{32,28},{36,32}... | collective-permute-start | bytes 1572872 | tf_op jit(solution)/shard_map/ppermute | solution.py:16
  48.4 12.5 %copy-start.13 = (s32[1,64]{1,0:T(1,128)S(1)}, s32[1,64]{1,0:T(1,128)}, u32[]{:S(2)}) copy-start(s32[1,64]{1,0:T(1,128)} %param.12) | copy-start | bytes 772
  65.2 7.9 %copy-start = (bf16[128,128,256]{2,1,0:T(8,128)(2,1)S(1)}, bf16[128,128,256]{2,1,0:T(8,128)(2,1)}, u32[]{:S(2)}) copy-start(bf16[128,128,256]{2,1,0:T(8,128)(2,1)} %get-tuple-element.359) | copy-start | bytes 25165828 | tf_op jit(solution)/shard_map/while
  81.2 13.5 %copy-start = (bf16[128,128,256]{2,1,0:T(8,128)(2,1)S(1)}, bf16[128,128,256]{2,1,0:T(8,128)(2,1)}, u32[]{:S(2)}) copy-start(bf16[128,128,256]{2,1,0:T(8,128)(2,1)} %get-tuple-element.359) | copy-start | bytes 25165828 | tf_op jit(solution)/shard_map/while
  110.3 4.1 %copy-start.5 = (bf16[1,256,2048]{1,2,0:T(8,128)(2,1)S(1)}, bf16[1,256,2048]{1,2,0:T(8,128)(2,1)}, u32[]{:S(2)}) copy-start(bf16[1,256,2048]{1,2,0:T(8,128)(2,1)} %copy-done.4) | copy-start | bytes 3145732
  110.3 4.1 %copy-start.7 = (bf16[1,256,2048]{1,2,0:T(8,128)(2,1)S(1)}, bf16[1,256,2048]{1,2,0:T(8,128)(2,1)}, u32[]{:S(2)}) copy-start(bf16[1,256,2048]{1,2,0:T(8,128)(2,1)} %copy-done.6) | copy-start | bytes 3145732
  177.9 4.1 %copy-start.2 = (bf16[1,256,2048]{1,2,0:T(8,128)(2,1)S(1)}, bf16[1,256,2048]{1,2,0:T(8,128)(2,1)}, u32[]{:S(2)}) copy-start(bf16[1,256,2048]{1,2,0:T(8,128)(2,1)} %copy-done.1) | copy-start | bytes 3145732
  177.9 4.1 %copy-start.3 = (bf16[1,256,2048]{1,2,0:T(8,128)(2,1)S(1)}, bf16[1,256,2048]{1,2,0:T(8,128)(2,1)}, u32[]{:S(2)}) copy-start(bf16[1,256,2048]{1,2,0:T(8,128)(2,1)} %copy.47) | copy-start | bytes 3145732
  185.2 3.8 %copy-start.10 = (bf16[1,256,2048]{1,2,0:T(8,128)(2,1)S(1)}, bf16[1,256,2048]{1,2,0:T(8,128)(2,1)}, u32[]{:S(2)}) copy-start(bf16[1,256,2048]{1,2,0:T(8,128)(2,1)} %get-tuple-element.252) | copy-start | bytes 3145732
  185.2 162.1 %copy-start.9 = (bf16[1,256,2048]{1,2,0:T(8,128)(2,1)S(1)}, bf16[1,256,2048]{1,2,0:T(8,128)(2,1)}, u32[]{:S(2)}) copy-start(bf16[1,256,2048]{1,2,0:T(8,128)(2,1)} %get-tuple-element.251) | copy-start | bytes 3145732
Sparse Core Ops, SparseCore 0:
  173.4 172.3 all-reduce.2
where the time goes:
time: 372 us; the launch traced here: 369 us
  waiting for transfers between devices  155 us (42%)
  local copies, waits for them, and re-layouts  120 us (32%)
  matrix products  36.2 us (10%)
  other arithmetic  21.4 us (6%)
  between operations  15 us (4%)
  blocking collectives  11 us (3%)
  starting transfers between devices  6.66 us (2%)
    psum x1, waiting for transfers between devices, on_device(): summed = lax.psum(local_raw, ('dp', 'ctx'))  155 us
    unnamed x36, local copies, waits for them, and re-layouts  26.6 us
    dot_general x2, matrix products, per_block(): jnp.einsum('gct,gcr->gtr', cot_block, window, preferred_element_type=jnp....  20.8 us
    reshape x1, local copies, waits for them, and re-layouts, on_device(): flat = accum.reshape(local_groups, FLEN * 2 * FLEN)  17.8 us
    reshape x1, local copies, waits for them, and re-layouts, on_device(): skewed = flat.reshape(local_groups, FLEN, 2 * FLEN + 1)  17.5 us
    pad x1, local copies, waits for them, and re-layouts, on_device(): flat = jnp.pad(flat, ((0, 0), (0, FLEN)))  13.3 us
    reshape x1, local copies, waits for them, and re-layouts, on_device(): tiled.reshape(local_groups, FLEN * (2 * FLEN + 1))[:, :FLEN * 2 * FLEN]  12.9 us
    psum x1, blocking collectives, on_device(): squares = lax.psum(jnp.sum(summed * summed), 'tensor')  11 us
  transfers between devices with their start and end apart: 3, of which 1 were waited for; matrix products, arithmetic and copies ran while one was open for 26% of the time, Pallas kernels for 0%

commit v1 on v0

--- a/solution.py
+++ b/solution.py
@@ -14,6 +14,16 @@
     count = lax.axis_size(axis)
     initial, last = (max(0, -steps), min(count, count - steps))
     return lax.ppermute(value, axis, [(source, source + steps) for source in range(initial, last)])
+
+
+def doubling_sum(value, axis):
+    count = lax.axis_size(axis)
+    step = 1
+    while step < count:
+        partner = lax.ppermute(value, axis, [(i, i ^ step) for i in range(count)])
+        value = value + partner
+        step *= 2
+    return value
 
 
 def on_device(query_in, key_in, value_in, grad_out, seq_lengths, filters):
@@ -95,8 +105,8 @@
     grad_key = (grad_gated * values).astype(jnp.bfloat16)
     grad_value = (grad_gated * keys).astype(jnp.bfloat16)
     clip_limit = math.sqrt(GROUPS * FLEN)
-    summed = lax.psum(local_raw, ("dp", "ctx"))
-    squares = lax.psum(jnp.sum(summed * summed), "tensor")
+    summed = doubling_sum(doubling_sum(local_raw, "dp"), "ctx")
+    squares = doubling_sum(jnp.sum(summed * summed), "tensor")
     factor = jnp.minimum(1.0, clip_limit / jnp.sqrt(squares))
     grad_filters = summed * factor
     return (mixed_out[None], grad_query[None], grad_key[None], grad_value[None], grad_filters)

time: 372 us -> 217 us (0.58)
  waiting for transfers between devices: 155 us -> 8.23 us
  starting transfers between devices: 6.66 us -> 25.5 us
  between operations: 15 us -> 2.92 us
  blocking collectives: 11 us -> 0 us
    psum x1 -> x0, waiting for transfers between devices: 155 us -> none  [on_device(): summed = lax.psum(local_raw, ('dp', 'ctx'))]
    ppermute x0 -> x8, starting transfers between devices: none -> 18.9 us  [doubling_sum(): partner = lax.ppermute(value, axis, [(i, i ^ step) for i in range(count)])]
    psum x1 -> x0, blocking collectives: 11 us -> none  [on_device(): squares = lax.psum(jnp.sum(summed * summed), 'tensor')]
    ppermute x0 -> x8, waiting for transfers between devices: none -> 8.23 us  [doubling_sum(): partner = lax.ppermute(value, axis, [(i, i ^ step) for i in range(count)])]
  transfers between devices with their start and end apart: 3 -> 10, of which waited for: 1 -> 4; matrix products, arithmetic and copies ran while one was open for 26% -> 79% of each run, Pallas kernels for 0% -> 0%
where the time goes in v1:
time: 217 us; the launch traced here: 215 us
  local copies, waits for them, and re-layouts  120 us (55%)
  matrix products  36.3 us (17%)
  starting transfers between devices  25.5 us (12%)
  other arithmetic  19.8 us (9%)
  waiting for transfers between devices  8.23 us (4%)
  between operations  2.92 us (1%)
  loops' own time  2.72 us (1%)
    unnamed x36, local copies, waits for them, and re-layouts  26.2 us
    dot_general x2, matrix products, per_block(): jnp.einsum('gct,gcr->gtr', cot_block, window, preferred_element_type=jnp....  20.8 us
    ppermute x8, starting transfers between devices, doubling_sum(): partner = lax.ppermute(value, axis, [(i, i ^ step) for i in range(count)])  18.9 us
    reshape x1, local copies, waits for them, and re-layouts, on_device(): flat = accum.reshape(local_groups, FLEN * 2 * FLEN)  17.8 us
    reshape x1, local copies, waits for them, and re-layouts, on_device(): skewed = flat.reshape(local_groups, FLEN, 2 * FLEN + 1)  17.5 us
    pad x1, local copies, waits for them, and re-layouts, on_device(): flat = jnp.pad(flat, ((0, 0), (0, FLEN)))  13.3 us
    reshape x1, local copies, waits for them, and re-layouts, on_device(): tiled.reshape(local_groups, FLEN * (2 * FLEN + 1))[:, :FLEN * 2 * FLEN]  12.9 us
    ppermute x8, waiting for transfers between devices, doubling_sum(): partner = lax.ppermute(value, axis, [(i, i ^ step) for i in range(count)])  8.23 us
  transfers between devices with their start and end apart: 10, of which 4 were waited for; matrix products, arithmetic and copies ran while one was open for 79% of the time, Pallas kernels for 0%

profile of v1, /device:TPU:32, one launch (start us, length us, event | category | flops | bytes accessed | tf_op | source)
XLA Modules:
  0.0 214.9 jit_solution(792294957339892621)
XLA Ops:
  0.6 1.5 copy.48
  2.1 1.9 copy.49
  4.0 0.3 fusion.34
  4.3 1.1 slice.29
  5.4 0.1 copy-done.8
  5.5 3.8 %collective-permute-start = (bf16[128,16,128]{2,1,0:T(8,128)(2,1)}, bf16[128,16,128]{2,1,0:T(8,128)(2,1)}, u32[]{:S(2)}, u32[]{:S(2)}) collective-permute-start(bf16[128,16,128]{2,1,0:T(8,128)(2,1)} %slice.29), channel_id=1, source_target_pairs={{0,4},{4,8},{8,12},{12,16},{16,20},{20,24},{24,28},{28,32},{32,36}... | collective-permute-start | bytes 1572872 | tf_op jit(solution)/shard_map/ppermute | solution.py:16
  9.3 0.5 copy.46
  9.9 2.6 %copy.47 = bf16[1,256,2048]{1,2,0:T(8,128)(2,1)} copy(bf16[1,256,2048]{2,1,0:T(8,128)(2,1)} %param.11) | data formatting | bytes 2097152 | tf_op args[3]
  12.6 1.5 fusion.31
  14.2 2.8 %collective-permute-start.1 = (bf16[128,16,128]{2,1,0:T(8,128)(2,1)S(1)}, bf16[128,16,128]{2,1,0:T(8,128)(2,1)}, u32[]{:S(2)}, u32[]{:S(2)}) collective-permute-start(bf16[128,16,128]{2,1,0:T(8,128)(2,1)S(1)} %slice.31), channel_id=1, source_target_pairs={{4,0},{8,4},{12,8},{16,12},{20,16},{24,20},{28,24},{32,28},{36,32}... | collective-permute-start | bytes 1572872 | tf_op jit(solution)/shard_map/ppermute | solution.py:16
  17.0 0.1 rev.6
  17.3 0.1 copy.51
  17.4 4.5 %broadcast_in_dim.81 = bf16[128,128,257]{0,2,1:T(8,128)(2,1)} broadcast(bf16[128,257]{0,1:T(8,128)(2,1)S(1)} %copy.51), dimensions={0,2} | broadcast | bytes 8487168 | tf_op jit(solution)/shard_map/broadcast_in_dim | solution.py:59
  21.9 12.9 %reshape.186 = bf16[128,32896]{0,1:T(8,128)(2,1)} reshape(bf16[128,128,257]{0,2,1:T(8,128)(2,1)} %broadcast_in_dim.81) | data formatting | bytes 16842752 | tf_op jit(solution)/shard_map/reshape | solution.py:60
  34.8 7.1 %slice.30 = bf16[128,32768]{0,1:T(8,128)(2,1)} slice(bf16[128,32896]{0,1:T(8,128)(2,1)} %reshape.186), slice={[0:128], [0:32768]} | slice | bytes 16777216 | tf_op jit(solution)/shard_map/slice | solution.py:60
  41.9 12.2 %copy.52 = bf16[128,128,256]{2,1,0:T(8,128)(2,1)} copy(bf16[128,128,256]{0,2,1:T(8,128)(2,1)} %bitcast.51) | data formatting | bytes 16777216
  54.1 0.1 copy.50
  54.1 0.1 reduce-window.4
  54.2 0.1 reduce
  54.4 0.1 select_reduce_fusion.1
  54.5 1.6 pad_maximum_fusion
  56.1 37.5 %while.17 = (s32[]{:T(128)}, f32[128,128,256]{2,1,0:T(8,128)}, f32[2,128,16,128]{3,2,1,0:T(8,128)}, f32[2,128,16,256]{3,2,1,0:T(8,128)}, s32[2]{0:T(128)S(1)}, /...) while((s32[]{:T(128)}, f32[128,128,256]{2,1,0:T(8,128)}, ...), condition=%wide.region_3.4_spmd.clone, body=%wide.region_1.3_spmd.clone.sunk | while | flops 423944448 | bytes 90641992 | solution.py:86
  56.1 0.6 dynamic_slice.39
  57.3 0.1 select_reduce_fusion.3
  58.1 0.1 fusion.60
  58.2 7.9 %select_add_fusion.2 = f32[128,128,256]{2,1,0:T(8,128)} fusion(f32[128,128,256]{2,1,0:T(8,128)} %get-tuple-element.337, f32[128,256]{1,0:T(8,128)S(1)} %get-tuple-element.318, pred[]{:T(512)S(6)} %compare.4, bf16[128,16,384]{2,1,0:T(8,128)(2,1)S(1)} %get-tuple-element.358, s32[]{:T(128)S(6)} %select_n.32, ...), kind=kOutput, calls=%fused_computation.1.clone.1 | convolution fusion | flops 146800640 | bytes 35258376 | tf_op jit(solution)/shard_map/while/body/eval_jaxpr/gct,gcr->gtr/dot_general | solution.py:81
  66.1 2.7 %bitcast_dynamic-update-slice_fusion.2 = f32[2,128,16,256]{3,2,1,0:T(8,128)} fusion(f32[2,128,16,256]{3,2,1,0:T(8,128)} %get-tuple-element.339, s32[]{:T(128)} %get-tuple-element.336, bf16[128,128,256]{2,1,0:T(8,128)(2,1)S(1)} %copy-done, bf16[128,256]{1,0:T(8,128)(2,1)S(1)} %get-tuple-element.319, bf16[128,16,256]{2,1,0:T(8,128)(2,1)S(1)} %get-tuple-element.357, ...), kind=kOutput, calls=%fused_computation.8.clone.1 | convolution fusion | flops 138412032 | bytes 11076100 | tf_op jit(solution)/shard_map/while/body/eval_jaxpr/gtr,gct->gcr/dot_general | solution.py:78
  68.8 3.3 %fusion.61 = f32[2,128,16,128]{3,2,1,0:T(8,128)} fusion(f32[2,128,16,128]{3,2,1,0:T(8,128)} %get-tuple-element.338, s32[]{:T(128)} %get-tuple-element.336, bf16[128,128,256]{2,1,0:T(8,128)(2,1)S(1)} %copy-done, bf16[128,256]{1,0:T(8,128)(2,1)S(1)} %get-tuple-element.319, bf16[128,16,384]{2,1,0:T(8,128)(2,1)S(1)} %get-tuple-element.358, s32[]{:T(128)S(6)} %select_n.32), kind=kOutput, calls=%fused_computation.10.clone.1 | convolution fusion | flops 138412032 | bytes 10551812 | tf_op jit(solution)/shard_map/while/body/eval_jaxpr/gtr,gcr->gct/dot_general | solution.py:75
  72.1 0.6 dynamic_slice.39
  73.3 0.1 select_reduce_fusion.3
  74.1 0.1 fusion.60
  74.2 12.9 %select_add_fusion.2 = f32[128,128,256]{2,1,0:T(8,128)} fusion(f32[128,128,256]{2,1,0:T(8,128)} %get-tuple-element.337, f32[128,256]{1,0:T(8,128)S(1)} %get-tuple-element.318, pred[]{:T(512)S(6)} %compare.4, bf16[128,16,384]{2,1,0:T(8,128)(2,1)S(1)} %get-tuple-element.358, s32[]{:T(128)S(6)} %select_n.32, ...), kind=kOutput, calls=%fused_computation.1.clone.1 | convolution fusion | flops 146800640 | bytes 35258376 | tf_op jit(solution)/shard_map/while/body/eval_jaxpr/gct,gcr->gtr/dot_general | solution.py:81
  87.1 0.5 copy-done
  87.7 2.7 %bitcast_dynamic-update-slice_fusion.2 = f32[2,128,16,256]{3,2,1,0:T(8,128)} fusion(f32[2,128,16,256]{3,2,1,0:T(8,128)} %get-tuple-element.339, s32[]{:T(128)} %get-tuple-element.336, bf16[128,128,256]{2,1,0:T(8,128)(2,1)S(1)} %copy-done, bf16[128,256]{1,0:T(8,128)(2,1)S(1)} %get-tuple-element.319, bf16[128,16,256]{2,1,0:T(8,128)(2,1)S(1)} %get-tuple-element.357, ...), kind=kOutput, calls=%fused_computation.8.clone.1 | convolution fusion | flops 138412032 | bytes 11076100 | tf_op jit(solution)/shard_map/while/body/eval_jaxpr/gtr,gct->gcr/dot_general | solution.py:78
  90.3 3.3 %fusion.61 = f32[2,128,16,128]{3,2,1,0:T(8,128)} fusion(f32[2,128,16,128]{3,2,1,0:T(8,128)} %get-tuple-element.338, s32[]{:T(128)} %get-tuple-element.336, bf16[128,128,256]{2,1,0:T(8,128)(2,1)S(1)} %copy-done, bf16[128,256]{1,0:T(8,128)(2,1)S(1)} %get-tuple-element.319, bf16[128,16,384]{2,1,0:T(8,128)(2,1)S(1)} %get-tuple-element.358, s32[]{:T(128)S(6)} %select_n.32), kind=kOutput, calls=%fused_computation.10.clone.1 | convolution fusion | flops 138412032 | bytes 10551812 | tf_op jit(solution)/shard_map/while/body/eval_jaxpr/gtr,gcr->gct/dot_general | solution.py:75
  93.6 17.8 %copy.62 = f32[128,128,256]{0,2,1:T(8,128)} copy(f32[128,128,256]{2,1,0:T(8,128)} %get-tuple-element.146) | data formatting | bytes 33554432 | tf_op jit(solution)/shard_map/reshape | solution.py:89
  111.4 13.3 %pad.4 = f32[128,32896]{0,1:T(8,128)} pad(f32[128,32768]{0,1:T(8,128)} %bitcast.48, f32[]{:T(128)} %constant.68.clone.1), padding=0_0x0_128 | pad | bytes 33619972 | tf_op jit(solution)/shard_map/jit(_pad)/pad | solution.py:90
  124.8 17.5 %reshape.192 = f32[128,128,257]{0,2,1:T(8,128)} reshape(f32[128,32896]{0,1:T(8,128)} %pad.4) | data formatting | bytes 33685504 | tf_op jit(solution)/shard_map/reshape | solution.py:91
  142.2 6.7 %reduce_sum.18 = f32[128,257]{0,1:T(8,128)S(1)} reduce(f32[128,128,257]{0,2,1:T(8,128)} %reshape.192, f32[]{:T(128)} %constant.68.clone.1), dimensions={1}, to_apply=%region_5.6 | reduce | flops 4177792 | bytes 16974340 | tf_op jit(solution)/shard_map/reduce_sum | solution.py:92
  149.1 1.2 collective-permute-done.2
  150.5 4.1 %collective-permute-done.3 = f32[128,128]{0,1:T(8,128)S(1)} collective-permute-done((f32[128,128]{0,1:T(8,128)S(1)}, f32[128,128]{0,1:T(8,128)S(1)}, u32[]{:S(2)}, u32[]{:S(2)}) %collective-permute-start.3) | collective-permute-done | bytes 65568 | tf_op jit(solution)/shard_map/ppermute | solution.py:23
  154.7 3.9 %collective-permute-start.4 = (f32[128,128]{0,1:T(8,128)S(1)}, f32[128,128]{0,1:T(8,128)S(1)}, u32[]{:S(2)}, u32[]{:S(2)}) collective-permute-start(f32[128,128]{0,1:T(8,128)S(1)} %add.140), channel_id=1, source_target_pairs={{0,8},{4,12},{8,0},{12,4},{16,24},{20,28},{24,16},{28,20},{32,40},... | collective-permute-start | bytes 196616 | tf_op jit(solution)/shard_map/ppermute | solution.py:23
  158.6 3.6 %fusion.38 = f32[1,128,16,128]{3,2,1,0:T(8,128)S(1)} fusion(bf16[128,16,128]{2,1,0:T(8,128)(2,1)} %collective-permute-done.1, bf16[128,128,256]{2,1,0:T(8,128)(2,1)} %get-tuple-element.368, bf16[128,128]{1,0:T(8,128)(2,1)S(1)} %slice.33), kind=kOutput, calls=%fused_computation.46 | convolution fusion | flops 69206016 | bytes 5799936 | tf_op jit(solution)/shard_map/gtr,gct->gcr/dot_general | solution.py:96
  162.1 1.3 slice.24
  163.5 3.5 %collective-permute-start.5 = (f32[128,128]{0,1:T(8,128)S(1)}, f32[128,128]{0,1:T(8,128)S(1)}, u32[]{:S(2)}, u32[]{:S(2)}) collective-permute-start(f32[128,128]{0,1:T(8,128)S(1)} %add.141), channel_id=1, source_target_pairs={{0,16},{4,20},{8,24},{12,28},{16,0},{20,4},{24,8},{28,12},{32,48},... | collective-permute-start | bytes 196616 | tf_op jit(solution)/shard_map/ppermute | solution.py:23
  166.9 1.9 fusion.37
  168.9 3.0 %copy.55 = f32[2,128,128,16]{1,0,3,2:T(2,128)} copy(f32[2,128,128,16]{1,3,2,0:T(8,128)S(1)} %fusion.37) | data formatting | bytes 4194304 | tf_op jit(solution)/shard_map/transpose | solution.py:101
  171.8 4.1 %reshape.190 = f32[1,256,2048]{1,2,0:T(8,128)} reshape(f32[2,128,128,16]{1,0,3,2:T(2,128)} %copy.55) | data formatting | bytes 4194304 | tf_op jit(solution)/shard_map/reshape | solution.py:101
  175.9 1.7 collective-permute-start.6
  177.6 2.9 %fusion.33 = (bf16[1,256,2048]{1,2,0:T(8,128)(2,1)S(1)}, bf16[1,256,2048]{1,2,0:T(8,128)(2,1)}) fusion(f32[1,256,2048]{1,2,0:T(8,128)} %reshape.190, bf16[1,256,2048]{1,2,0:T(8,128)(2,1)S(1)} %copy-done.5, bf16[1,256,2048]{1,2,0:T(8,128)(2,1)S(1)} %copy-done.7), kind=kLoop, calls=%fused_computation.39 | loop fusion | flops 3145728 | bytes 6291456 | tf_op jit(solution)/shard_map/convert_element_type | solution.py:106
  180.5 4.6 %copy.53 = f32[2,128,128,16]{1,0,3,2:T(2,128)} copy(f32[2,128,128,16]{1,3,2,0:T(8,128)} %bitcast.7) | data formatting | bytes 4194304 | tf_op jit(solution)/shard_map/transpose | solution.py:102
  185.1 4.1 %reshape.188 = f32[1,256,2048]{1,2,0:T(8,128)} reshape(f32[2,128,128,16]{1,0,3,2:T(2,128)} %copy.53) | data formatting | bytes 4194304 | tf_op jit(solution)/shard_map/reshape | solution.py:102
  189.2 3.7 %collective-permute-start.7 = (f32[128,128]{0,1:T(8,128)S(1)}, f32[128,128]{0,1:T(8,128)S(1)}, u32[]{:S(2)}, u32[]{:S(2)}) collective-permute-start(f32[128,128]{0,1:T(8,128)S(1)} %add.143), channel_id=1, source_target_pairs={{0,64},{4,68},{8,72},{12,76},{16,80},{20,84},{24,88},{28,92},{32,9... | collective-permute-start | bytes 196616 | tf_op jit(solution)/shard_map/ppermute | solution.py:23
  192.9 3.3 %fusion.32 = (bf16[1,256,2048]{1,2,0:T(8,128)(2,1)}, bf16[1,256,2048]{1,2,0:T(8,128)(2,1)}) fusion(f32[1,256,2048]{1,2,0:T(8,128)} %reshape.188, bf16[1,256,2048]{1,2,0:T(8,128)(2,1)S(1)} %copy-done.3, bf16[1,256,2048]{1,2,0:T(8,128)(2,1)S(1)} %copy-done.2), kind=kLoop, calls=%fused_computation.38 | loop fusion | flops 3145728 | bytes 6291456 | tf_op jit(solution)/shard_map/convert_element_type | solution.py:104
  196.2 2.4 %copy.59 = bf16[1,256,2048]{2,1,0:T(8,128)(2,1)} copy(bf16[1,256,2048]{1,2,0:T(8,128)(2,1)} %get-tuple-element.252) | data formatting | bytes 2097152
  198.6 1.4 copy.60
  200.0 1.4 copy.57
  201.4 1.4 copy.58
  202.9 0.6 multiply_reduce_fusion
  203.5 1.5 collective-permute-start.8
  205.0 2.1 collective-permute-done.8
  208.4 4.4 %collective-permute-start.9 = (f32[]{:T(128)}, f32[]{:T(128)}, u32[]{:S(2)}, u32[]{:S(2)}) collective-permute-start(f32[]{:T(128)} %add.145), channel_id=1, source_target_pairs={{0,2},{1,3},{2,0},{3,1},{4,6},{5,7},{6,4},{7,5},{8,10},{9,11},{10,... | collective-permute-start | bytes 20 | tf_op jit(solution)/shard_map/ppermute | solution.py:23
  212.8 0.7 collective-permute-done.9
  214.2 0.7 copy.61
  (63 shorter events, 0.7 us)
Async XLA Ops:
  2.1 3.3 %copy-start.4 = (bf16[1,256,2048]{1,2,0:T(8,128)(2,1)}, bf16[1,256,2048]{1,2,0:T(8,128)(2,1)S(1)}, u32[]{:S(2)}) copy-start(bf16[1,256,2048]{1,2,0:T(8,128)(2,1)S(1)} %copy.48) | copy-start | bytes 3145732
  2.1 7.2 %copy-start.11 = (bf16[1,256,2048]{2,1,0:T(8,128)(2,1)S(1)}, bf16[1,256,2048]{2,1,0:T(8,128)(2,1)}, u32[]{:S(2)}) copy-start(bf16[1,256,2048]{2,1,0:T(8,128)(2,1)} %param.8) | copy-start | bytes 3145732
  4.0 5.9 %copy-start.6 = (bf16[1,256,2048]{1,2,0:T(8,128)(2,1)}, bf16[1,256,2048]{1,2,0:T(8,128)(2,1)S(1)}, u32[]{:S(2)}) copy-start(bf16[1,256,2048]{1,2,0:T(8,128)(2,1)S(1)} %copy.49) | copy-start | bytes 3145732
  4.3 1.2 copy-start.8
  5.5 49.0 %collective-permute-start = (bf16[128,16,128]{2,1,0:T(8,128)(2,1)}, bf16[128,16,128]{2,1,0:T(8,128)(2,1)}, u32[]{:S(2)}, u32[]{:S(2)}) collective-permute-start(bf16[128,16,128]{2,1,0:T(8,128)(2,1)} %slice.29), channel_id=1, source_target_pairs={{0,4},{4,8},{8,12},{12,16},{16,20},{20,24},{24,28},{28,32},{32,36}... | collective-permute-start | bytes 1572872 | tf_op jit(solution)/shard_map/ppermute | solution.py:16
  9.9 4.3 %copy-start.1 = (bf16[1,256,2048]{1,2,0:T(8,128)(2,1)}, bf16[1,256,2048]{1,2,0:T(8,128)(2,1)S(1)}, u32[]{:S(2)}) copy-start(bf16[1,256,2048]{1,2,0:T(8,128)(2,1)S(1)} %copy.46) | copy-start | bytes 3145732
  9.9 7.1 %copy-start.12 = (bf16[128,128]{1,0:T(8,128)(2,1)S(1)}, bf16[128,128]{1,0:T(8,128)(2,1)}, u32[]{:S(2)}) copy-start(bf16[128,128]{1,0:T(8,128)(2,1)} %param.13) | copy-start | bytes 98308
  14.2 144.4 %collective-permute-start.1 = (bf16[128,16,128]{2,1,0:T(8,128)(2,1)S(1)}, bf16[128,16,128]{2,1,0:T(8,128)(2,1)}, u32[]{:S(2)}, u32[]{:S(2)}) collective-permute-start(bf16[128,16,128]{2,1,0:T(8,128)(2,1)S(1)} %slice.31), channel_id=1, source_target_pairs={{4,0},{8,4},{12,8},{16,12},{20,16},{24,20},{28,24},{32,28},{36,32}... | collective-permute-start | bytes 1572872 | tf_op jit(solution)/shard_map/ppermute | solution.py:16
  41.9 12.2 %copy-start.13 = (s32[1,64]{1,0:T(1,128)S(1)}, s32[1,64]{1,0:T(1,128)}, u32[]{:S(2)}) copy-start(s32[1,64]{1,0:T(1,128)} %param.12) | copy-start | bytes 772
  58.2 7.9 %copy-start = (bf16[128,128,256]{2,1,0:T(8,128)(2,1)S(1)}, bf16[128,128,256]{2,1,0:T(8,128)(2,1)}, u32[]{:S(2)}) copy-start(bf16[128,128,256]{2,1,0:T(8,128)(2,1)} %get-tuple-element.361) | copy-start | bytes 25165828 | tf_op jit(solution)/shard_map/while
  74.2 13.5 %copy-start = (bf16[128,128,256]{2,1,0:T(8,128)(2,1)S(1)}, bf16[128,128,256]{2,1,0:T(8,128)(2,1)}, u32[]{:S(2)}) copy-start(bf16[128,128,256]{2,1,0:T(8,128)(2,1)} %get-tuple-element.361) | copy-start | bytes 25165828 | tf_op jit(solution)/shard_map/while
  149.0 1.3 collective-permute-start.2
  150.3 4.4 %collective-permute-start.3 = (f32[128,128]{0,1:T(8,128)S(1)}, f32[128,128]{0,1:T(8,128)S(1)}, u32[]{:S(2)}, u32[]{:S(2)}) collective-permute-start(f32[128,128]{0,1:T(8,128)S(1)} %add.139), channel_id=1, source_target_pairs={{0,4},{4,0},{8,12},{12,8},{16,20},{20,16},{24,28},{28,24},{32,36},... | collective-permute-start | bytes 196616 | tf_op jit(solution)/shard_map/ppermute | solution.py:23
  154.7 8.7 %collective-permute-start.4 = (f32[128,128]{0,1:T(8,128)S(1)}, f32[128,128]{0,1:T(8,128)S(1)}, u32[]{:S(2)}, u32[]{:S(2)}) collective-permute-start(f32[128,128]{0,1:T(8,128)S(1)} %add.140), channel_id=1, source_target_pairs={{0,8},{4,12},{8,0},{12,4},{16,24},{20,28},{24,16},{28,20},{32,40},... | collective-permute-start | bytes 196616 | tf_op jit(solution)/shard_map/ppermute | solution.py:23
  163.5 12.4 %collective-permute-start.5 = (f32[128,128]{0,1:T(8,128)S(1)}, f32[128,128]{0,1:T(8,128)S(1)}, u32[]{:S(2)}, u32[]{:S(2)}) collective-permute-start(f32[128,128]{0,1:T(8,128)S(1)} %add.141), channel_id=1, source_target_pairs={{0,16},{4,20},{8,24},{12,28},{16,0},{20,4},{24,8},{28,12},{32,48},... | collective-permute-start | bytes 196616 | tf_op jit(solution)/shard_map/ppermute | solution.py:23
  171.8 5.8 %copy-start.5 = (bf16[1,256,2048]{1,2,0:T(8,128)(2,1)S(1)}, bf16[1,256,2048]{1,2,0:T(8,128)(2,1)}, u32[]{:S(2)}) copy-start(bf16[1,256,2048]{1,2,0:T(8,128)(2,1)} %copy-done.4) | copy-start | bytes 3145732
  171.8 5.8 %copy-start.7 = (bf16[1,256,2048]{1,2,0:T(8,128)(2,1)S(1)}, bf16[1,256,2048]{1,2,0:T(8,128)(2,1)}, u32[]{:S(2)}) copy-start(bf16[1,256,2048]{1,2,0:T(8,128)(2,1)} %copy-done.6) | copy-start | bytes 3145732
  175.9 13.2 %collective-permute-start.6 = (f32[128,128]{0,1:T(8,128)S(1)}, f32[128,128]{0,1:T(8,128)S(1)}, u32[]{:S(2)}, u32[]{:S(2)}) collective-permute-start(f32[128,128]{0,1:T(8,128)S(1)} %add.142), channel_id=1, source_target_pairs={{0,32},{4,36},{8,40},{12,44},{16,48},{20,52},{24,56},{28,60},{32,0... | collective-permute-start | bytes 196616 | tf_op jit(solution)/shard_map/ppermute | solution.py:23
  185.1 7.8 %copy-start.2 = (bf16[1,256,2048]{1,2,0:T(8,128)(2,1)S(1)}, bf16[1,256,2048]{1,2,0:T(8,128)(2,1)}, u32[]{:S(2)}) copy-start(bf16[1,256,2048]{1,2,0:T(8,128)(2,1)} %copy-done.1) | copy-start | bytes 3145732
  185.1 7.8 %copy-start.3 = (bf16[1,256,2048]{1,2,0:T(8,128)(2,1)S(1)}, bf16[1,256,2048]{1,2,0:T(8,128)(2,1)}, u32[]{:S(2)}) copy-start(bf16[1,256,2048]{1,2,0:T(8,128)(2,1)} %copy.47) | copy-start | bytes 3145732
  189.2 13.7 %collective-permute-start.7 = (f32[128,128]{0,1:T(8,128)S(1)}, f32[128,128]{0,1:T(8,128)S(1)}, u32[]{:S(2)}, u32[]{:S(2)}) collective-permute-start(f32[128,128]{0,1:T(8,128)S(1)} %add.143), channel_id=1, source_target_pairs={{0,64},{4,68},{8,72},{12,76},{16,80},{20,84},{24,88},{28,92},{32,9... | collective-permute-start | bytes 196616 | tf_op jit(solution)/shard_map/ppermute | solution.py:23
  196.2 3.8 %copy-start.10 = (bf16[1,256,2048]{1,2,0:T(8,128)(2,1)S(1)}, bf16[1,256,2048]{1,2,0:T(8,128)(2,1)}, u32[]{:S(2)}) copy-start(bf16[1,256,2048]{1,2,0:T(8,128)(2,1)} %get-tuple-element.254) | copy-start | bytes 3145732
  196.2 5.2 %copy-start.9 = (bf16[1,256,2048]{1,2,0:T(8,128)(2,1)S(1)}, bf16[1,256,2048]{1,2,0:T(8,128)(2,1)}, u32[]{:S(2)}) copy-start(bf16[1,256,2048]{1,2,0:T(8,128)(2,1)} %get-tuple-element.253) | copy-start | bytes 3145732
  203.5 3.7 %collective-permute-start.8 = (f32[]{:T(128)}, f32[]{:T(128)}, u32[]{:S(2)}, u32[]{:S(2)}) collective-permute-start(f32[]{:T(128)} %get-tuple-element.247), channel_id=1, source_target_pairs={{0,1},{1,0},{2,3},{3,2},{4,5},{5,4},{6,7},{7,6},{8,9},{9,8},{10,11... | collective-permute-start | bytes 20 | tf_op jit(solution)/shard_map/ppermute | solution.py:23
  208.4 5.1 %collective-permute-start.9 = (f32[]{:T(128)}, f32[]{:T(128)}, u32[]{:S(2)}, u32[]{:S(2)}) collective-permute-start(f32[]{:T(128)} %add.145), channel_id=1, source_target_pairs={{0,2},{1,3},{2,0},{3,1},{4,6},{5,7},{6,4},{7,5},{8,10},{9,11},{10,... | collective-permute-start | bytes 20 | tf_op jit(solution)/shard_map/ppermute | solution.py:23

commit v2 on v1

v2 whole, which is shorter than its diff:
```python
import math

import jax
import jax.numpy as jnp
from jax import lax
from jax.experimental import pallas as pl
from jax.experimental.pallas import tpu as pltpu
from jax.sharding import PartitionSpec as P

GROUP = 16
FLEN = 128
GROUPS = 512
LANES = 128


def passed_along(value, axis, steps):
    count = lax.axis_size(axis)
    initial, last = (max(0, -steps), min(count, count - steps))
    return lax.ppermute(value, axis, [(source, source + steps) for source in range(initial, last)])


def doubling_sum(value, axis):
    count = lax.axis_size(axis)
    step = 1
    while step < count:
        partner = lax.ppermute(value, axis, [(i, i ^ step) for i in range(count)])
        value = value + partner
        step *= 2
    return value


def conv_kernel(q_ref, k_ref, v_ref, go_ref, prev_ref, next_ref, fp_ref, fq_ref, m_ref, mt_ref, mr_ref,
                mo_ref, gq_ref, gk_ref, gv_ref, raw_ref):
    f32, bf16 = jnp.float32, jnp.bfloat16
    rows = q_ref.shape[0]
    blocks = rows // FLEN
    query = q_ref[...].astype(f32)
    keys = k_ref[...].astype(f32)
    values = v_ref[...].astype(f32)
    upstream = go_ref[...].astype(f32)
    gated = (keys * values).astype(bf16)
    cot = (upstream * query).astype(bf16)
    u_all = jnp.concatenate([prev_ref[...], gated], axis=0)
    c_all = jnp.concatenate([cot, next_ref[...]], axis=0)
    lane_group = lax.broadcasted_iota(jnp.int32, (1, LANES), 1) // GROUP
    windows = [u_all[b * FLEN:(b + 2) * FLEN] for b in range(blocks)]
    cots = [c_all[b * FLEN:(b + 1) * FLEN] for b in range(blocks + 1)]
    masks = [m_ref[b] for b in range(blocks + 1)]
    masks_t = [mt_ref[b] for b in range(blocks + 1)]
    masks_r = [mr_ref[b].astype(f32) for b in range(blocks)]
    flip = (lax.broadcasted_iota(jnp.int32, (FLEN, FLEN), 0)
            + lax.broadcasted_iota(jnp.int32, (FLEN, FLEN), 1) == FLEN - 1).astype(bf16)
    cots_r = [jnp.dot(flip, cots[b], preferred_element_type=f32).astype(bf16) for b in range(blocks)]
    mixed = [jnp.zeros((FLEN, LANES), f32) for _ in range(blocks)]
    back = [jnp.zeros((FLEN, LANES), f32) for _ in range(blocks)]
    nt = (((1,), (1,)), ((), ()))
    sums = []
    for k in range(LANES // GROUP):
        prow = jnp.broadcast_to(fp_ref[k:k + 1, :], (FLEN, 2 * FLEN))
        taps = pltpu.roll(prow, 0, 1, stride=1, stride_axis=0).astype(bf16)
        qrow = jnp.broadcast_to(fq_ref[k:k + 1, :], (2 * FLEN, 2 * FLEN))
        taps_t = pltpu.roll(qrow, FLEN, 1, stride=1, stride_axis=0)[:, :FLEN].astype(bf16)
        in_group = lane_group == k
        group_cots = [jnp.where(in_group, c, jnp.zeros_like(c)) for c in cots]
        group_cots_r = [jnp.where(in_group, c, jnp.zeros_like(c)) for c in cots_r]
        acc = jnp.zeros((FLEN, 2 * FLEN), f32)
        for b in range(blocks):
            window = jnp.where(in_group, windows[b], jnp.zeros_like(windows[b]))
            mixed[b] = mixed[b] + jnp.dot(taps * masks[b], window, preferred_element_type=f32)
            prods = lax.dot_general(group_cots_r[b], windows[b], nt, preferred_element_type=f32)
            acc = acc + prods * masks_r[b]
        for b in range(blocks + 1):
            spread = jnp.dot(taps_t * masks_t[b], group_cots[b], preferred_element_type=f32)
            if b < blocks:
                back[b] = back[b] + spread[FLEN:]
            if b > 0:
                back[b - 1] = back[b - 1] + spread[:FLEN]
        skewed = pltpu.roll(acc, 0, 1, stride=1, stride_axis=0)
        sums.append(jnp.sum(skewed, axis=0, keepdims=True))
    raw_ref[0] = jnp.concatenate(sums, axis=0)
    mixed_all = jnp.concatenate(mixed, axis=0)
    back_all = jnp.concatenate(back, axis=0)
    mo_ref[...] = (query * mixed_all).astype(bf16)
    gq_ref[...] = (upstream * mixed_all).astype(bf16)
    gk_ref[...] = (back_all * values).astype(bf16)
    gv_ref[...] = (back_all * keys).astype(bf16)


def grouped_conv(q2, k2, v2, g2, prev_tail, next_head, fp, fq, mask, mask_t, interpret=False):
    mask_r = mask[:-1, ::-1, :]
    rows, channels = q2.shape
    tiles = channels // LANES
    per_tile = LANES // GROUP
    nb = rows // FLEN
    tok = pl.BlockSpec((rows, LANES), lambda j: (0, j))
    halo = pl.BlockSpec((FLEN, LANES), lambda j: (0, j))
    filt = pl.BlockSpec((per_tile, 2 * FLEN), lambda j: (j, 0))
    mspec = pl.BlockSpec((nb + 1, FLEN, 2 * FLEN), lambda j: (0, 0, 0))
    mtspec = pl.BlockSpec((nb + 1, 2 * FLEN, FLEN), lambda j: (0, 0, 0))
    mrspec = pl.BlockSpec((nb, FLEN, 2 * FLEN), lambda j: (0, 0, 0))
    out_tok = jax.ShapeDtypeStruct((rows, channels), jnp.bfloat16)
    return pl.pallas_call(
        conv_kernel,
        grid=(tiles,),
        in_specs=[tok, tok, tok, tok, halo, halo, filt, filt, mspec, mtspec, mrspec],
        out_specs=[tok, tok, tok, tok, pl.BlockSpec((1, per_tile, 2 * FLEN), lambda j: (j, 0, 0))],
        out_shape=[out_tok, out_tok, out_tok, out_tok,
                   jax.ShapeDtypeStruct((tiles, per_tile, 2 * FLEN), jnp.float32)],
        interpret=interpret,
    )(q2, k2, v2, g2, prev_tail, next_head, fp, fq, mask, mask_t, mask_r)


def doc_masks(lengths, offset, rows):
    starts = jnp.cumsum(lengths) - lengths
    nb = rows // FLEN
    b_ids = jnp.arange(nb + 1, dtype=jnp.int32)[:, None]
    tpos = offset + b_ids * FLEN + jnp.arange(FLEN, dtype=jnp.int32)[None, :]
    doc_begin = jnp.max(jnp.where(starts[None, None, :] <= tpos[:, :, None], starts[None, None, :], 0), axis=2)
    rpos = offset + (b_ids - 1) * FLEN + jnp.arange(2 * FLEN, dtype=jnp.int32)[None, :]
    lag = jnp.arange(FLEN, dtype=jnp.int32)[:, None] + FLEN - jnp.arange(2 * FLEN, dtype=jnp.int32)[None, :]
    inside = (lag >= 0) & (lag < FLEN)
    mask = ((rpos[:, None, :] >= doc_begin[:, :, None]) & inside[None]).astype(jnp.bfloat16)
    return mask, mask.transpose(0, 2, 1)


def filter_rows(filters):
    taps = filters.astype(jnp.float32)
    groups = taps.shape[0]
    fp = jnp.concatenate([jnp.zeros((groups, 1), jnp.float32), taps[:, ::-1],
                          jnp.zeros((groups, FLEN - 1), jnp.float32)], axis=1)
    fq = jnp.concatenate([taps, jnp.zeros((groups, FLEN), jnp.float32)], axis=1)
    return fp, fq


def on_device(query_in, key_in, value_in, grad_out, seq_lengths, filters):
    f32, bf16 = jnp.float32, jnp.bfloat16
    q2, k2, v2, g2 = query_in[0], key_in[0], value_in[0], grad_out[0]
    rows = q2.shape[0]
    tail = (k2[rows - FLEN:].astype(f32) * v2[rows - FLEN:].astype(f32)).astype(bf16)
    head = (g2[:FLEN].astype(f32) * q2[:FLEN].astype(f32)).astype(bf16)
    prev_tail = passed_along(tail, "ctx", 1)
    next_head = passed_along(head, "ctx", -1)
    mask, mask_t = doc_masks(seq_lengths[0], lax.axis_index("ctx") * rows, rows)
    fp, fq = filter_rows(filters)
    mixed_out, grad_query, grad_key, grad_value, cols = grouped_conv(
        q2, k2, v2, g2, prev_tail, next_head, fp, fq, mask, mask_t)
    local_raw = cols.reshape(-1, 2 * FLEN)[:, 2 * FLEN - 1:FLEN - 1:-1]
    summed = doubling_sum(doubling_sum(local_raw, "dp"), "ctx")
    squares = doubling_sum(jnp.sum(summed * summed), "tensor")
    factor = jnp.minimum(1.0, math.sqrt(GROUPS * FLEN) / jnp.sqrt(squares))
    grad_filters = summed * factor
    return (mixed_out[None], grad_query[None], grad_key[None], grad_value[None], grad_filters)


def solution(mesh):
    tok = P("dp", "ctx", "tensor")
    in_specs = (tok, tok, tok, tok, P("dp", None), P("tensor", None))
    out_specs = (tok, tok, tok, tok, P("tensor", None))
    return jax.shard_map(
        on_device, mesh=mesh, in_specs=in_specs, out_specs=out_specs, check_vma=False
    )
```

time: 217 us -> 93.2 us (0.43)
  local copies, waits for them, and re-layouts: 120 us -> 5.35 us
  matrix products: 36.3 us -> 0 us
  Pallas kernels: 0 us -> 23 us
  waiting for transfers between devices: 8.23 us -> 29.2 us
  other arithmetic: 19.8 us -> 6.22 us
  loops' own time: 2.72 us -> 0 us
    reshape x6 -> x0, local copies, waits for them, and re-layouts: 56.5 us -> none  [the longest x1 17.8 us: on_device(): flat = accum.reshape(local_groups, FLEN * 2 * FLEN)]
    dot_general x7 -> x0, matrix products: 36.3 us -> none  [the longest x2 20.8 us: per_block(): jnp.einsum('gct,gcr->gtr', cot_block, window, preferred_element_type=jnp....]
    unnamed x36 -> x12, local copies, waits for them, and re-layouts: 26.2 us -> 2.18 us
    pallas_call x0 -> x1, Pallas kernels: none -> 23 us  [grouped_conv(): pl.pallas_call(conv_kernel, grid=(tiles,), in_specs=[tok, tok, tok, tok,...]
    ppermute x8, waiting for transfers between devices: 8.23 us -> 21.9 us  [doubling_sum(): partner = lax.ppermute(value, axis, [(i, i ^ step) for i in range(count)])]
    pad x1 -> x0, local copies, waits for them, and re-layouts: 13.3 us -> none  [on_device(): flat = jnp.pad(flat, ((0, 0), (0, FLEN)))]
    slice x6 -> x2, local copies, waits for them, and re-layouts: 9.53 us -> 0.86 us  [the longest x1 0.85 us: on_device(): local_raw = cols.reshape(-1, 2 * FLEN)[:, 2 * FLEN - 1:FLEN - 1:-1]]
    transpose x2 -> x0, local copies, waits for them, and re-layouts: 7.52 us -> none  [the longest x1 4.55 us: on_device(): mixed = mixed_blocks.transpose(0, 3, 1, 2).reshape(rows_dev, channels)]
  transfers between devices with their start and end apart: 10 -> 10, of which waited for: 4 -> 10; matrix products, arithmetic and copies ran while one was open for 79% -> 6% of each run, Pallas kernels for 0% -> 0%
where the time goes in v2:
time: 93.2 us; the launch traced here: 92.2 us
  waiting for transfers between devices  29.2 us (31%)
  starting transfers between devices  25.7 us (28%)
  Pallas kernels  23 us (25%)
  other arithmetic  6.22 us (7%)
  local copies, waits for them, and re-layouts  5.35 us (6%)
  between operations  2.63 us (3%)
    pallas_call x1, Pallas kernels, grouped_conv(): pl.pallas_call(conv_kernel, grid=(tiles,), in_specs=[tok, tok, tok, tok,...  23 us
    ppermute x8, waiting for transfers between devices, doubling_sum(): partner = lax.ppermute(value, axis, [(i, i ^ step) for i in range(count)])  21.9 us
    ppermute x8, starting transfers between devices, doubling_sum(): partner = lax.ppermute(value, axis, [(i, i ^ step) for i in range(count)])  19.8 us
    ppermute x2, waiting for transfers between devices, passed_along(): lax.ppermute(value, axis, [(source, source + steps) for source in range(i...  7.33 us
    ppermute x2, starting transfers between devices, passed_along(): lax.ppermute(value, axis, [(source, source + steps) for source in range(i...  5.87 us
    unnamed x12, local copies, waits for them, and re-layouts  2.18 us
  transfers between devices with their start and end apart: 10, of which 10 were waited for; matrix products, arithmetic and copies ran while one was open for 6% of the time, Pallas kernels for 0%

profile of v2, /device:TPU:32, one launch (start us, length us, event | category | flops | bytes accessed | tf_op | source)
XLA Modules:
  0.0 92.2 jit_solution(1477669538790558828)
XLA Ops:
  0.6 0.0 copy-start
  0.6 1.4 %fusion = bf16[128,2048]{1,0:T(8,128)(2,1)S(1)} fusion(bf16[1,256,2048]{2,1,0:T(8,128)(2,1)} %param.8, bf16[1,256,2048]{2,1,0:T(8,128)(2,1)} %param.7), kind=kLoop, calls=%fused_computation.2 | loop fusion | flops 1048576 | bytes 1572864 | tf_op jit(solution)/shard_map/convert_element_type | solution.py:139
  2.1 3.8 %collective-permute-start = (bf16[128,2048]{1,0:T(8,128)(2,1)S(1)}, bf16[128,2048]{1,0:T(8,128)(2,1)S(1)}, u32[]{:S(2)}, u32[]{:S(2)}) collective-permute-start(bf16[128,2048]{1,0:T(8,128)(2,1)S(1)} %fusion), channel_id=1, source_target_pairs={{0,4},{4,8},{8,12},{12,16},{16,20},{20,24},{24,28},{28,32},{32,36}... | collective-permute-start | bytes 1572872 | tf_op jit(solution)/shard_map/ppermute | solution.py:19
  5.9 0.0 copy-done
  5.9 1.2 %fusion.1 = bf16[128,2048]{1,0:T(8,128)(2,1)S(1)} fusion(bf16[1,256,2048]{2,1,0:T(8,128)(2,1)S(1)} %copy-done, bf16[1,256,2048]{2,1,0:T(8,128)(2,1)} %param.9), kind=kLoop, calls=%fused_computation.3 | loop fusion | flops 1048576 | bytes 1572864 | tf_op jit(solution)/shard_map/convert_element_type | solution.py:140
  7.1 2.0 %collective-permute-start.1 = (bf16[128,2048]{1,0:T(8,128)(2,1)S(1)}, bf16[128,2048]{1,0:T(8,128)(2,1)S(1)}, u32[]{:S(2)}, u32[]{:S(2)}) collective-permute-start(bf16[128,2048]{1,0:T(8,128)(2,1)S(1)} %fusion.1), channel_id=1, source_target_pairs={{4,0},{8,4},{12,8},{16,12},{20,16},{24,20},{28,24},{32,28},{36,32}... | collective-permute-start | bytes 1572872 | tf_op jit(solution)/shard_map/ppermute | solution.py:19
  9.2 0.1 iota_add_fusion.1
  9.2 0.1 iota_add_fusion
  9.3 0.1 fusion.6
  9.4 0.0 copy-start.5
  9.4 0.6 copy-done.5
  10.1 0.1 copy.13
  10.2 0.1 reduce-window.8
  10.3 0.1 reduce
  10.4 0.1 select_reduce_fusion
  10.5 0.1 and_convert_fusion.1.m_ref
  10.6 0.0 copy-start.1
  10.6 0.0 copy-start.4
  10.7 0.7 copy-done.4
  11.4 0.1 rev.9
  11.5 0.7 concatenate.7.fq_ref
  12.2 0.1 pad.3.clone
  12.3 0.0 copy-done.1
  12.3 1.3 %rev.10.mr_ref = bf16[2,128,256]{2,1,0:T(8,128)(2,1)} reverse(bf16[2,128,256]{2,1,0:T(8,128)(2,1)S(1)} %slice.28), dimensions={1} | reverse | bytes 262144 | tf_op jit(solution)/shard_map/rev | solution.py:90
  13.6 0.7 maximum_maximum_fusion.fp_ref
  14.3 0.9 and_convert_fusion.mt_ref
  15.2 2.4 %collective-permute-done.prev_ref = bf16[128,2048]{1,0:T(8,128)(2,1)S(1)} collective-permute-done((bf16[128,2048]{1,0:T(8,128)(2,1)S(1)}, bf16[128,2048]{1,0:T(8,128)(2,1)S(1)}, u32[]{:S(2)}, u32[]{:S(2)}) %collective-permute-start) | collective-permute-done | bytes 524320 | tf_op jit(solution)/shard_map/ppermute | solution.py:19
  17.6 0.0 copy-start.2
  17.6 4.9 %collective-permute-done.1.next_ref = bf16[128,2048]{1,0:T(8,128)(2,1)S(1)} collective-permute-done((bf16[128,2048]{1,0:T(8,128)(2,1)S(1)}, bf16[128,2048]{1,0:T(8,128)(2,1)S(1)}, u32[]{:S(2)}, u32[]{:S(2)}) %collective-permute-start.1) | collective-permute-done | bytes 524320 | tf_op jit(solution)/shard_map/ppermute | solution.py:19
  22.5 0.0 copy-start.3
  22.5 0.0 copy-done.2
  22.5 0.8 copy-done.3
  23.3 23.0 %shard_map.101 = (bf16[256,2048]{1,0:T(8,128)(2,1)}, bf16[256,2048]{1,0:T(8,128)(2,1)}, bf16[256,2048]{1,0:T(8,128)(2,1)}, bf16[256,2048]{1,0:T(8,128)(2,1)}, f32[16,8,256]{2,1,0:T(8,128)}) custom-call(bf16[256,2048]{1,0:T(8,128)(2,1)} %bitcast.17, bf16[256,2048]{1,0:T(8,128)(2,1)} %bitcast.18, bf16[256,2048]{1,0:T(8,128)(2,1)} %bitcast.19, ...), custom_call_target="tpu_custom_call" | custom-call | tf_op jit(solution)/shard_map/pallas_call | solution.py:102
  46.3 0.8 slice.29
  47.2 0.1 rev.11
  47.3 0.1 collective-permute-start.2
  47.3 1.2 %collective-permute-done.2 = f32[128,128]{1,0:T(8,128)S(1)} collective-permute-done((f32[128,128]{1,0:T(8,128)S(1)}, f32[128,128]{1,0:T(8,128)S(1)}, u32[]{:S(2)}, u32[]{:S(2)}) %collective-permute-start.2) | collective-permute-done | bytes 65568 | tf_op jit(solution)/shard_map/ppermute | solution.py:26
  48.6 0.2 collective-permute-start.3
  48.8 4.2 %collective-permute-done.3 = f32[128,128]{1,0:T(8,128)S(1)} collective-permute-done((f32[128,128]{1,0:T(8,128)S(1)}, f32[128,128]{1,0:T(8,128)S(1)}, u32[]{:S(2)}, u32[]{:S(2)}) %collective-permute-start.3) | collective-permute-done | bytes 65568 | tf_op jit(solution)/shard_map/ppermute | solution.py:26
  53.0 5.6 %collective-permute-start.4 = (f32[128,128]{1,0:T(8,128)S(1)}, f32[128,128]{1,0:T(8,128)S(1)}, u32[]{:S(2)}, u32[]{:S(2)}) collective-permute-start(f32[128,128]{1,0:T(8,128)S(1)} %add.111), channel_id=1, source_target_pairs={{0,8},{4,12},{8,0},{12,4},{16,24},{20,28},{24,16},{28,20},{32,40},... | collective-permute-start | bytes 196616 | tf_op jit(solution)/shard_map/ppermute | solution.py:26
  58.5 2.2 %collective-permute-done.4 = f32[128,128]{1,0:T(8,128)S(1)} collective-permute-done((f32[128,128]{1,0:T(8,128)S(1)}, f32[128,128]{1,0:T(8,128)S(1)}, u32[]{:S(2)}, u32[]{:S(2)}) %collective-permute-start.4) | collective-permute-done | bytes 65568 | tf_op jit(solution)/shard_map/ppermute | solution.py:26
  60.8 2.8 %collective-permute-start.5 = (f32[128,128]{1,0:T(8,128)S(1)}, f32[128,128]{1,0:T(8,128)S(1)}, u32[]{:S(2)}, u32[]{:S(2)}) collective-permute-start(f32[128,128]{1,0:T(8,128)S(1)} %add.112), channel_id=1, source_target_pairs={{0,16},{4,20},{8,24},{12,28},{16,0},{20,4},{24,8},{28,12},{32,48},... | collective-permute-start | bytes 196616 | tf_op jit(solution)/shard_map/ppermute | solution.py:26
  63.6 6.2 %collective-permute-done.5 = f32[128,128]{1,0:T(8,128)S(1)} collective-permute-done((f32[128,128]{1,0:T(8,128)S(1)}, f32[128,128]{1,0:T(8,128)S(1)}, u32[]{:S(2)}, u32[]{:S(2)}) %collective-permute-start.5) | collective-permute-done | bytes 65568 | tf_op jit(solution)/shard_map/ppermute | solution.py:26
  69.8 1.7 %collective-permute-start.6 = (f32[128,128]{1,0:T(8,128)S(1)}, f32[128,128]{1,0:T(8,128)S(1)}, u32[]{:S(2)}, u32[]{:S(2)}) collective-permute-start(f32[128,128]{1,0:T(8,128)S(1)} %add.113), channel_id=1, source_target_pairs={{0,32},{4,36},{8,40},{12,44},{16,48},{20,52},{24,56},{28,60},{32,0... | collective-permute-start | bytes 196616 | tf_op jit(solution)/shard_map/ppermute | solution.py:26
  71.4 2.7 %collective-permute-done.6 = f32[128,128]{1,0:T(8,128)S(1)} collective-permute-done((f32[128,128]{1,0:T(8,128)S(1)}, f32[128,128]{1,0:T(8,128)S(1)}, u32[]{:S(2)}, u32[]{:S(2)}) %collective-permute-start.6) | collective-permute-done | bytes 65568 | tf_op jit(solution)/shard_map/ppermute | solution.py:26
  74.1 3.6 %collective-permute-start.7 = (f32[128,128]{1,0:T(8,128)S(1)}, f32[128,128]{1,0:T(8,128)S(1)}, u32[]{:S(2)}, u32[]{:S(2)}) collective-permute-start(f32[128,128]{1,0:T(8,128)S(1)} %add.114), channel_id=1, source_target_pairs={{0,64},{4,68},{8,72},{12,76},{16,80},{20,84},{24,88},{28,92},{32,9... | collective-permute-start | bytes 196616 | tf_op jit(solution)/shard_map/ppermute | solution.py:26
  77.8 2.2 %collective-permute-done.7 = f32[128,128]{1,0:T(8,128)S(1)} collective-permute-done((f32[128,128]{1,0:T(8,128)S(1)}, f32[128,128]{1,0:T(8,128)S(1)}, u32[]{:S(2)}, u32[]{:S(2)}) %collective-permute-start.7) | collective-permute-done | bytes 65568 | tf_op jit(solution)/shard_map/ppermute | solution.py:26
  80.0 0.6 multiply_reduce_fusion
  80.6 1.5 %collective-permute-start.8 = (f32[]{:T(128)}, f32[]{:T(128)}, u32[]{:S(2)}, u32[]{:S(2)}) collective-permute-start(f32[]{:T(128)} %get-tuple-element.15), channel_id=1, source_target_pairs={{0,1},{1,0},{2,3},{3,2},{4,5},{5,4},{6,7},{7,6},{8,9},{9,8},{10,11... | collective-permute-start | bytes 20 | tf_op jit(solution)/shard_map/ppermute | solution.py:26
  82.1 2.3 %collective-permute-done.8 = f32[]{:T(128)} collective-permute-done((f32[]{:T(128)}, f32[]{:T(128)}, u32[]{:S(2)}, u32[]{:S(2)}) %collective-permute-start.8) | collective-permute-done | bytes 36 | tf_op jit(solution)/shard_map/ppermute | solution.py:26
  85.6 4.4 %collective-permute-start.9 = (f32[]{:T(128)}, f32[]{:T(128)}, u32[]{:S(2)}, u32[]{:S(2)}) collective-permute-start(f32[]{:T(128)} %add.116), channel_id=1, source_target_pairs={{0,2},{1,3},{2,0},{3,1},{4,6},{5,7},{6,4},{7,5},{8,10},{9,11},{10,... | collective-permute-start | bytes 20 | tf_op jit(solution)/shard_map/ppermute | solution.py:26
  90.1 0.9 collective-permute-done.9
  91.5 0.6 broadcast_multiply_fusion
  (12 shorter events, 0.1 us)
Async XLA Ops:
  0.6 5.3 %copy-start = (bf16[1,256,2048]{2,1,0:T(8,128)(2,1)S(1)}, bf16[1,256,2048]{2,1,0:T(8,128)(2,1)}, u32[]{:S(2)}) copy-start(bf16[1,256,2048]{2,1,0:T(8,128)(2,1)} %param.6) | copy-start | bytes 3145732
  2.1 15.6 %collective-permute-start = (bf16[128,2048]{1,0:T(8,128)(2,1)S(1)}, bf16[128,2048]{1,0:T(8,128)(2,1)S(1)}, u32[]{:S(2)}, u32[]{:S(2)}) collective-permute-start(bf16[128,2048]{1,0:T(8,128)(2,1)S(1)} %fusion), channel_id=1, source_target_pairs={{0,4},{4,8},{8,12},{12,16},{16,20},{20,24},{24,28},{28,32},{32,36}... | collective-permute-start | bytes 1572872 | tf_op jit(solution)/shard_map/ppermute | solution.py:19
  7.1 15.5 %collective-permute-start.1 = (bf16[128,2048]{1,0:T(8,128)(2,1)S(1)}, bf16[128,2048]{1,0:T(8,128)(2,1)S(1)}, u32[]{:S(2)}, u32[]{:S(2)}) collective-permute-start(bf16[128,2048]{1,0:T(8,128)(2,1)S(1)} %fusion.1), channel_id=1, source_target_pairs={{4,0},{8,4},{12,8},{16,12},{20,16},{24,20},{28,24},{32,28},{36,32}... | collective-permute-start | bytes 1572872 | tf_op jit(solution)/shard_map/ppermute | solution.py:19
  9.4 0.7 copy-start.5
  10.6 1.6 %copy-start.1 = (bf16[3,128,256]{2,1,0:T(8,128)(2,1)}, bf16[3,128,256]{2,1,0:T(8,128)(2,1)S(1)}, u32[]{:S(2)}) copy-start(bf16[3,128,256]{2,1,0:T(8,128)(2,1)S(1)} %and_convert_fusion.1.m_ref) | copy-start | bytes 589828
  10.6 0.8 copy-start.4
  17.6 4.9 %copy-start.2 = (bf16[128,2048]{1,0:T(8,128)(2,1)}, bf16[128,2048]{1,0:T(8,128)(2,1)S(1)}, u32[]{:S(2)}) copy-start(bf16[128,2048]{1,0:T(8,128)(2,1)S(1)} %collective-permute-done.prev_ref) | copy-start | bytes 1572868
  22.5 0.8 copy-start.3
  47.3 1.3 %collective-permute-start.2 = (f32[128,128]{1,0:T(8,128)S(1)}, f32[128,128]{1,0:T(8,128)S(1)}, u32[]{:S(2)}, u32[]{:S(2)}) collective-permute-start(f32[128,128]{1,0:T(8,128)S(1)} %rev.11), channel_id=1, source_target_pairs={{0,128},{128,0},{1,129},{129,1},{2,130},{130,2},{3,131},{131,3},{4... | collective-permute-start | bytes 196616 | tf_op jit(solution)/shard_map/ppermute | solution.py:26
  48.6 4.4 %collective-permute-start.3 = (f32[128,128]{1,0:T(8,128)S(1)}, f32[128,128]{1,0:T(8,128)S(1)}, u32[]{:S(2)}, u32[]{:S(2)}) collective-permute-start(f32[128,128]{1,0:T(8,128)S(1)} %add.110), channel_id=1, source_target_pairs={{0,4},{4,0},{8,12},{12,8},{16,20},{20,16},{24,28},{28,24},{32,36},... | collective-permute-start | bytes 196616 | tf_op jit(solution)/shard_map/ppermute | solution.py:26
  53.0 7.8 %collective-permute-start.4 = (f32[128,128]{1,0:T(8,128)S(1)}, f32[128,128]{1,0:T(8,128)S(1)}, u32[]{:S(2)}, u32[]{:S(2)}) collective-permute-start(f32[128,128]{1,0:T(8,128)S(1)} %add.111), channel_id=1, source_target_pairs={{0,8},{4,12},{8,0},{12,4},{16,24},{20,28},{24,16},{28,20},{32,40},... | collective-permute-start | bytes 196616 | tf_op jit(solution)/shard_map/ppermute | solution.py:26
  60.8 9.0 %collective-permute-start.5 = (f32[128,128]{1,0:T(8,128)S(1)}, f32[128,128]{1,0:T(8,128)S(1)}, u32[]{:S(2)}, u32[]{:S(2)}) collective-permute-start(f32[128,128]{1,0:T(8,128)S(1)} %add.112), channel_id=1, source_target_pairs={{0,16},{4,20},{8,24},{12,28},{16,0},{20,4},{24,8},{28,12},{32,48},... | collective-permute-start | bytes 196616 | tf_op jit(solution)/shard_map/ppermute | solution.py:26
  69.8 4.4 %collective-permute-start.6 = (f32[128,128]{1,0:T(8,128)S(1)}, f32[128,128]{1,0:T(8,128)S(1)}, u32[]{:S(2)}, u32[]{:S(2)}) collective-permute-start(f32[128,128]{1,0:T(8,128)S(1)} %add.113), channel_id=1, source_target_pairs={{0,32},{4,36},{8,40},{12,44},{16,48},{20,52},{24,56},{28,60},{32,0... | collective-permute-start | bytes 196616 | tf_op jit(solution)/shard_map/ppermute | solution.py:26
  74.1 5.9 %collective-permute-start.7 = (f32[128,128]{1,0:T(8,128)S(1)}, f32[128,128]{1,0:T(8,128)S(1)}, u32[]{:S(2)}, u32[]{:S(2)}) collective-permute-start(f32[128,128]{1,0:T(8,128)S(1)} %add.114), channel_id=1, source_target_pairs={{0,64},{4,68},{8,72},{12,76},{16,80},{20,84},{24,88},{28,92},{32,9... | collective-permute-start | bytes 196616 | tf_op jit(solution)/shard_map/ppermute | solution.py:26
  80.6 3.8 %collective-permute-start.8 = (f32[]{:T(128)}, f32[]{:T(128)}, u32[]{:S(2)}, u32[]{:S(2)}) collective-permute-start(f32[]{:T(128)} %get-tuple-element.15), channel_id=1, source_target_pairs={{0,1},{1,0},{2,3},{3,2},{4,5},{5,4},{6,7},{7,6},{8,9},{9,8},{10,11... | collective-permute-start | bytes 20 | tf_op jit(solution)/shard_map/ppermute | solution.py:26
  85.6 5.3 %collective-permute-start.9 = (f32[]{:T(128)}, f32[]{:T(128)}, u32[]{:S(2)}, u32[]{:S(2)}) collective-permute-start(f32[]{:T(128)} %add.116), channel_id=1, source_target_pairs={{0,2},{1,3},{2,0},{3,1},{4,6},{5,7},{6,4},{7,5},{8,10},{9,11},{10,... | collective-permute-start | bytes 20 | tf_op jit(solution)/shard_map/ppermute | solution.py:26

commit v3 on v2

--- a/solution.py
+++ b/solution.py
@@ -27,6 +27,21 @@
         value = value + partner
         step *= 2
     return value
+
+
+def radix_sum(value, axes, bits):
+    sizes = [lax.axis_size(a) for a in axes]
+    count = math.prod(sizes)
+    linear = 0
+    for a, n in zip(axes, sizes):
+        linear = linear * n + lax.axis_index(a)
+    members = [m for m in range(count) if m & bits == m]
+    received = [value] + [
+        lax.ppermute(value, axes, [(i, i ^ m) for i in range(count)]) for m in members[1:]
+    ]
+    table = jnp.array(members, jnp.int32)
+    picks = jnp.searchsorted(table, (linear & bits) ^ table)
+    return jnp.sum(jnp.take(jnp.stack(received), picks, axis=0), axis=0)
 
 
 def conv_kernel(q_ref, k_ref, v_ref, go_ref, prev_ref, next_ref, fp_ref, fq_ref, m_ref, mt_ref, mr_ref,
@@ -145,8 +160,9 @@
     mixed_out, grad_query, grad_key, grad_value, cols = grouped_conv(
         q2, k2, v2, g2, prev_tail, next_head, fp, fq, mask, mask_t)
     local_raw = cols.reshape(-1, 2 * FLEN)[:, 2 * FLEN - 1:FLEN - 1:-1]
-    summed = doubling_sum(doubling_sum(local_raw, "dp"), "ctx")
-    squares = doubling_sum(jnp.sum(summed * summed), "tensor")
+    near = radix_sum(local_raw, ("ctx",), 7)
+    summed = radix_sum(near, ("dp", "ctx"), 56)
+    squares = radix_sum(jnp.sum(summed * summed), ("tensor",), 3)
     factor = jnp.minimum(1.0, math.sqrt(GROUPS * FLEN) / jnp.sqrt(squares))
     grad_filters = summed * factor
     return (mixed_out[None], grad_query[None], grad_key[None], grad_value[None], grad_filters)

time: 93.2 us -> 102 us (1.094)
  waiting for transfers between devices: 29.2 us -> 15 us
  starting transfers between devices: 25.7 us -> 37 us
  local copies, waits for them, and re-layouts: 5.35 us -> 13.8 us
  other arithmetic: 6.22 us -> 9.91 us
    ppermute x8 -> x17, starting transfers between devices: 19.8 us -> 31.1 us  [radix_sum(): lax.ppermute(value, axes, [(i, i ^ m) for i in range(count)])]
    gather x0 -> x14, local copies, waits for them, and re-layouts: none -> 8.87 us  [the longest x11 7.06 us: radix_sum(): picks = jnp.searchsorted(table, linear & bits ^ table)]
    ppermute x2, waiting for transfers between devices: 7.33 us -> 0.04 us  [passed_along(): lax.ppermute(value, axis, [(source, source + steps) for source in range(i...]
    ppermute x8 -> x17, waiting for transfers between devices: 21.9 us -> 15 us  [radix_sum(): lax.ppermute(value, axes, [(i, i ^ m) for i in range(count)])]
    another operation x2 -> x7, other arithmetic: 0.2 us -> 2.76 us  [the longest x1 2.54 us: radix_sum(): return jnp.sum(jnp.take(jnp.stack(received), picks, axis=0), axis=0)]
    unnamed x12 -> x26, local copies, waits for them, and re-layouts: 2.18 us -> 1.69 us
  transfers between devices with their start and end apart: 10 -> 19, of which waited for: 10 -> 7; matrix products, arithmetic and copies ran while one was open for 6% -> 13% of each run, Pallas kernels for 0% -> 0%
where the time goes in v3:
time: 102 us; the launch traced here: 101 us
  starting transfers between devices  37 us (36%)
  Pallas kernels  23 us (23%)
  waiting for transfers between devices  15 us (15%)
  local copies, waits for them, and re-layouts  13.8 us (14%)
  other arithmetic  9.91 us (10%)
  between operations  1.73 us (2%)
    ppermute x17, starting transfers between devices, radix_sum(): lax.ppermute(value, axes, [(i, i ^ m) for i in range(count)])  31.1 us
    pallas_call x1, Pallas kernels, grouped_conv(): pl.pallas_call(conv_kernel, grid=(tiles,), in_specs=[tok, tok, tok, tok,...  23 us
    ppermute x17, waiting for transfers between devices, radix_sum(): lax.ppermute(value, axes, [(i, i ^ m) for i in range(count)])  15 us
    gather x11, local copies, waits for them, and re-layouts, radix_sum(): picks = jnp.searchsorted(table, linear & bits ^ table)  7.06 us
    ppermute x2, starting transfers between devices, passed_along(): lax.ppermute(value, axis, [(source, source + steps) for source in range(i...  5.87 us
    another operation x1, other arithmetic, radix_sum(): return jnp.sum(jnp.take(jnp.stack(received), picks, axis=0), axis=0)  2.54 us
  transfers between devices with their start and end apart: 19, of which 7 were waited for; matrix products, arithmetic and copies ran while one was open for 13% of the time, Pallas kernels for 0%

profile of v3, /device:TPU:32, one launch (start us, length us, event | category | flops | bytes accessed | tf_op | source)
XLA Modules:
  0.0 100.9 jit_solution(2812269312252553756)
XLA Ops:
  0.6 1.4 %fusion.18 = bf16[128,2048]{1,0:T(8,128)(2,1)S(1)} fusion(bf16[1,256,2048]{2,1,0:T(8,128)(2,1)} %param.19, bf16[1,256,2048]{2,1,0:T(8,128)(2,1)} %param.18), kind=kLoop, calls=%fused_computation.36 | loop fusion | flops 1048576 | bytes 1572864 | tf_op jit(solution)/shard_map/convert_element_type | solution.py:154
  2.1 3.8 %collective-permute-start = (bf16[128,2048]{1,0:T(8,128)(2,1)S(1)}, bf16[128,2048]{1,0:T(8,128)(2,1)S(1)}, u32[]{:S(2)}, u32[]{:S(2)}) collective-permute-start(bf16[128,2048]{1,0:T(8,128)(2,1)S(1)} %fusion.18), channel_id=1, source_target_pairs={{0,4},{4,8},{8,12},{12,16},{16,20},{20,24},{24,28},{28,32},{32,36}... | collective-permute-start | bytes 1572872 | tf_op jit(solution)/shard_map/ppermute | solution.py:19
  5.9 1.2 %fusion.19 = bf16[128,2048]{1,0:T(8,128)(2,1)S(1)} fusion(bf16[1,256,2048]{2,1,0:T(8,128)(2,1)S(1)} %copy-done, bf16[1,256,2048]{2,1,0:T(8,128)(2,1)} %param.20), kind=kLoop, calls=%fused_computation.37 | loop fusion | flops 1048576 | bytes 1572864 | tf_op jit(solution)/shard_map/convert_element_type | solution.py:155
  7.1 2.0 %collective-permute-start.1 = (bf16[128,2048]{1,0:T(8,128)(2,1)S(1)}, bf16[128,2048]{1,0:T(8,128)(2,1)S(1)}, u32[]{:S(2)}, u32[]{:S(2)}) collective-permute-start(bf16[128,2048]{1,0:T(8,128)(2,1)S(1)} %fusion.19), channel_id=1, source_target_pairs={{4,0},{8,4},{12,8},{16,12},{20,16},{24,20},{28,24},{32,28},{36,32}... | collective-permute-start | bytes 1572872 | tf_op jit(solution)/shard_map/ppermute | solution.py:19
  9.2 0.1 fusion.24
  9.3 2.8 %while.61 = (s32[]{:T(128)}, u32[8]{0:T(128)S(1)}, u32[8]{0:T(128)S(1)}, s32[]{:T(128)}, s32[]{:T(128)}, /*index=5*/s32[]{:T(128)}, s32[]{}) while((s32[]{:T(128)}, u32[8]{0:T(128)S(1)}, u32[8]{0:T(128)S(1)}, s32[]{:T(128)}, s32[]{:T(128)}, /*index=5*/s32[]{:T(128)}, s32[]{}) %tuple.94), condition=%wide.region_3.4_spmd.clone, body=%wide.region_2.3_spmd.clone.sunk | while | flops 1140 | bytes 4616 | solution.py:43
  9.4 0.6 gather_fusion
  10.1 0.6 gather_fusion
  10.8 0.6 gather_fusion
  11.5 0.6 gather_fusion
  12.2 2.9 %while.62 = (s32[]{:T(128)}, u32[8]{0:T(128)S(1)}, u32[8]{0:T(128)S(1)}, s32[]{:T(128)}, s32[]{:T(128)}, /*index=5*/s32[]{:T(128)}, s32[]{}) while((s32[]{:T(128)}, u32[8]{0:T(128)S(1)}, u32[8]{0:T(128)S(1)}, s32[]{:T(128)}, s32[]{:T(128)}, /*index=5*/s32[]{:T(128)}, s32[]{}) %tuple.97), condition=%wide.region_6.8_spmd.clone, body=%wide.region_5.7_spmd.clone.sunk | while | flops 1156 | bytes 4616 | solution.py:43
  12.3 0.6 gather_fusion.1
  13.0 0.6 gather_fusion.1
  13.7 0.6 gather_fusion.1
  14.4 0.6 gather_fusion.1
  15.2 0.7 copy-done.5
  15.9 0.1 copy.16
  16.0 0.1 reduce-window.8
  16.1 0.1 reduce
  16.3 0.1 select_reduce_fusion.2
  16.4 0.1 and_convert_fusion.1.m_ref
  16.6 1.3 %rev.10.mr_ref = bf16[2,128,256]{2,1,0:T(8,128)(2,1)} reverse(bf16[2,128,256]{2,1,0:T(8,128)(2,1)S(1)} %slice.40), dimensions={1} | reverse | bytes 262144 | tf_op jit(solution)/shard_map/rev | solution.py:105
  17.9 0.1 rev.9
  18.0 0.7 concatenate.7.fq_ref
  18.7 2.1 %while.63 = (s32[]{:T(128)}, u32[4]{0:T(128)S(1)}, u32[4]{0:T(128)S(1)}, s32[]{:T(128)}, s32[]{:T(128)}, /*index=5*/s32[]{:T(128)}, s32[]{}) while((s32[]{:T(128)}, u32[4]{0:T(128)S(1)}, u32[4]{0:T(128)S(1)}, s32[]{:T(128)}, s32[]{:T(128)}, /*index=5*/s32[]{:T(128)}, s32[]{}) %tuple.100), condition=%wide.region_9.11_spmd.clone, body=%wide.region_8.10_spmd.clone.sunk | while | flops 1084 | bytes 4408 | solution.py:43
  18.8 0.6 gather_fusion.2
  19.5 0.6 gather_fusion.2
  20.2 0.6 gather_fusion.2
  20.9 0.8 maximum_maximum_fusion.fp_ref
  21.6 0.9 and_convert_fusion.mt_ref
  22.5 0.8 copy-done.2
  23.3 0.2 copy-done.3
  23.5 23.0 %shard_map.128 = (bf16[256,2048]{1,0:T(8,128)(2,1)}, bf16[256,2048]{1,0:T(8,128)(2,1)}, bf16[256,2048]{1,0:T(8,128)(2,1)}, bf16[256,2048]{1,0:T(8,128)(2,1)}, f32[16,8,256]{2,1,0:T(8,128)}) custom-call(bf16[256,2048]{1,0:T(8,128)(2,1)} %bitcast.53, bf16[256,2048]{1,0:T(8,128)(2,1)} %bitcast.54, bf16[256,2048]{1,0:T(8,128)(2,1)} %bitcast.55, ...), custom_call_target="tpu_custom_call" | custom-call | tf_op jit(solution)/shard_map/pallas_call | solution.py:117
  46.5 0.8 slice.41
  47.5 5.5 %collective-permute-start.3 = (f32[128,128]{1,0:T(8,128)S(1)}, f32[128,128]{1,0:T(8,128)S(1)}, u32[]{:S(2)}, u32[]{:S(2)}) collective-permute-start(f32[128,128]{1,0:T(8,128)S(1)} %rev.11), channel_id=1, source_target_pairs={{0,8},{4,12},{8,0},{12,4},{16,24},{20,28},{24,16},{28,20},{32,40},... | collective-permute-start | bytes 196616 | tf_op jit(solution)/shard_map/ppermute | solution.py:40
  52.9 0.5 collective-permute-start.4
  53.5 4.0 %collective-permute-start.5 = (f32[128,128]{1,0:T(8,128)S(1)}, f32[128,128]{1,0:T(8,128)S(1)}, u32[]{:S(2)}, u32[]{:S(2)}) collective-permute-start(f32[128,128]{1,0:T(8,128)S(1)} %rev.11), channel_id=1, source_target_pairs={{0,16},{4,20},{8,24},{12,28},{16,0},{20,4},{24,8},{28,12},{32,48},... | collective-permute-start | bytes 196616 | tf_op jit(solution)/shard_map/ppermute | solution.py:40
  57.5 1.8 %collective-permute-start.6 = (f32[128,128]{1,0:T(8,128)S(1)}, f32[128,128]{1,0:T(8,128)S(1)}, u32[]{:S(2)}, u32[]{:S(2)}) collective-permute-start(f32[128,128]{1,0:T(8,128)S(1)} %rev.11), channel_id=1, source_target_pairs={{0,20},{4,16},{8,28},{12,24},{16,4},{20,0},{24,12},{28,8},{32,52},... | collective-permute-start | bytes 196616 | tf_op jit(solution)/shard_map/ppermute | solution.py:40
  59.3 2.5 %collective-permute-start.7 = (f32[128,128]{1,0:T(8,128)S(1)}, f32[128,128]{1,0:T(8,128)S(1)}, u32[]{:S(2)}, u32[]{:S(2)}) collective-permute-start(f32[128,128]{1,0:T(8,128)S(1)} %rev.11), channel_id=1, source_target_pairs={{0,24},{4,28},{8,16},{12,20},{16,8},{20,12},{24,0},{28,4},{32,56},... | collective-permute-start | bytes 196616 | tf_op jit(solution)/shard_map/ppermute | solution.py:40
  61.8 2.2 %collective-permute-start.8 = (f32[128,128]{1,0:T(8,128)S(1)}, f32[128,128]{1,0:T(8,128)S(1)}, u32[]{:S(2)}, u32[]{:S(2)}) collective-permute-start(f32[128,128]{1,0:T(8,128)S(1)} %rev.11), channel_id=1, source_target_pairs={{0,28},{4,24},{8,20},{12,16},{16,12},{20,8},{24,4},{28,0},{32,60},... | collective-permute-start | bytes 196616 | tf_op jit(solution)/shard_map/ppermute | solution.py:40
  64.1 4.9 %collective-permute-done.6 = f32[128,128]{1,0:T(8,128)S(1)} collective-permute-done((f32[128,128]{1,0:T(8,128)S(1)}, f32[128,128]{1,0:T(8,128)S(1)}, u32[]{:S(2)}, u32[]{:S(2)}) %collective-permute-start.6) | collective-permute-done | bytes 65568 | tf_op jit(solution)/shard_map/ppermute | solution.py:40
  69.0 0.8 collective-permute-done.7
  69.8 0.6 gather_fusion.4
  70.4 0.1 select_reduce_fusion.1
  70.5 2.3 %collective-permute-start.9 = (f32[128,128]{1,0:T(8,128)S(1)}, f32[128,128]{1,0:T(8,128)S(1)}, u32[]{:S(2)}, u32[]{:S(2)}) collective-permute-start(f32[128,128]{1,0:T(8,128)S(1)} %select_reduce_fusion.1), channel_id=1, source_target_pairs={{0,32},{4,36},{8,40},{12,44},{16,48},{20,52},{24,56},{28,60},{32,0... | collective-permute-start | bytes 196616 | tf_op jit(solution)/shard_map/ppermute | solution.py:40
  72.8 3.0 %collective-permute-start.10 = (f32[128,128]{1,0:T(8,128)S(1)}, f32[128,128]{1,0:T(8,128)S(1)}, u32[]{:S(2)}, u32[]{:S(2)}) collective-permute-start(f32[128,128]{1,0:T(8,128)S(1)} %select_reduce_fusion.1), channel_id=1, source_target_pairs={{0,64},{4,68},{8,72},{12,76},{16,80},{20,84},{24,88},{28,92},{32,9... | collective-permute-start | bytes 196616 | tf_op jit(solution)/shard_map/ppermute | solution.py:40
  75.8 0.6 collective-permute-start.13
  76.4 3.8 %collective-permute-start.14 = (f32[128,128]{1,0:T(8,128)S(1)}, f32[128,128]{1,0:T(8,128)S(1)}, u32[]{:S(2)}, u32[]{:S(2)}) collective-permute-start(f32[128,128]{1,0:T(8,128)S(1)} %select_reduce_fusion.1), channel_id=1, source_target_pairs={{0,192},{4,196},{8,200},{12,204},{16,208},{20,212},{24,216},{28,22... | collective-permute-start | bytes 196616 | tf_op jit(solution)/shard_map/ppermute | solution.py:40
  80.2 0.2 collective-permute-start.15
  80.4 0.8 collective-permute-done.11
  81.3 2.3 %collective-permute-done.14 = f32[128,128]{1,0:T(8,128)S(1)} collective-permute-done((f32[128,128]{1,0:T(8,128)S(1)}, f32[128,128]{1,0:T(8,128)S(1)}, u32[]{:S(2)}, u32[]{:S(2)}) %collective-permute-start.14) | collective-permute-done | bytes 65568 | tf_op jit(solution)/shard_map/ppermute | solution.py:40
  83.5 1.6 %collective-permute-done.15 = f32[128,128]{1,0:T(8,128)S(1)} collective-permute-done((f32[128,128]{1,0:T(8,128)S(1)}, f32[128,128]{1,0:T(8,128)S(1)}, u32[]{:S(2)}, u32[]{:S(2)}) %collective-permute-start.15) | collective-permute-done | bytes 65568 | tf_op jit(solution)/shard_map/ppermute | solution.py:40
  85.2 0.6 gather_fusion.5
  85.8 0.1 select_reduce_fusion
  85.9 0.6 multiply_reduce_fusion
  86.5 1.5 %collective-permute-start.16 = (f32[]{:T(128)}, f32[]{:T(128)}, u32[]{:S(2)}, u32[]{:S(2)}) collective-permute-start(f32[]{:T(128)} %multiply_reduce_fusion), channel_id=1, source_target_pairs={{0,1},{1,0},{2,3},{3,2},{4,5},{5,4},{6,7},{7,6},{8,9},{9,8},{10,11... | collective-permute-start | bytes 20 | tf_op jit(solution)/shard_map/ppermute | solution.py:40
  88.0 2.7 %collective-permute-start.17 = (f32[]{:T(128)}, f32[]{:T(128)}, u32[]{:S(2)}, u32[]{:S(2)}) collective-permute-start(f32[]{:T(128)} %multiply_reduce_fusion), channel_id=1, source_target_pairs={{0,2},{1,3},{2,0},{3,1},{4,6},{5,7},{6,4},{7,5},{8,10},{9,11},{10,... | collective-permute-start | bytes 20 | tf_op jit(solution)/shard_map/ppermute | solution.py:40
  90.7 0.5 collective-permute-start.18
  91.2 2.1 %collective-permute-done.17 = f32[]{:T(128)} collective-permute-done((f32[]{:T(128)}, f32[]{:T(128)}, u32[]{:S(2)}, u32[]{:S(2)}) %collective-permute-start.17) | collective-permute-done | bytes 36 | tf_op jit(solution)/shard_map/ppermute | solution.py:40
  93.3 2.4 %collective-permute-done.18 = f32[]{:T(128)} collective-permute-done((f32[]{:T(128)}, f32[]{:T(128)}, u32[]{:S(2)}, u32[]{:S(2)}) %collective-permute-start.18) | collective-permute-done | bytes 36 | tf_op jit(solution)/shard_map/ppermute | solution.py:40
  95.8 2.5 %pad_maximum_fusion = f32[4]{0:T(128)S(1)} fusion(f32[1]{0:T(128)} %bitcast.32, f32[1]{0:T(128)} %bitcast.31, f32[1]{0:T(128)} %bitcast.30, f32[1]{0:T(128)} %bitcast.29), kind=kLoop, calls=%fused_computation.81 | loop fusion | flops 12 | bytes 32 | tf_op jit(solution)/shard_map/stack | solution.py:44
  98.3 0.6 gather_fusion.3
  98.9 0.6 fusion.26
  100.2 0.6 broadcast_multiply_fusion
  (109 shorter events, 1.0 us)
Async XLA Ops:
  0.6 5.3 %copy-start = (bf16[1,256,2048]{2,1,0:T(8,128)(2,1)S(1)}, bf16[1,256,2048]{2,1,0:T(8,128)(2,1)}, u32[]{:S(2)}) copy-start(bf16[1,256,2048]{2,1,0:T(8,128)(2,1)} %param.17) | copy-start | bytes 3145732
  2.1 20.4 %collective-permute-start = (bf16[128,2048]{1,0:T(8,128)(2,1)S(1)}, bf16[128,2048]{1,0:T(8,128)(2,1)S(1)}, u32[]{:S(2)}, u32[]{:S(2)}) collective-permute-start(bf16[128,2048]{1,0:T(8,128)(2,1)S(1)} %fusion.18), channel_id=1, source_target_pairs={{0,4},{4,8},{8,12},{12,16},{16,20},{20,24},{24,28},{28,32},{32,36}... | collective-permute-start | bytes 1572872 | tf_op jit(solution)/shard_map/ppermute | solution.py:19
  7.1 15.5 %collective-permute-start.1 = (bf16[128,2048]{1,0:T(8,128)(2,1)S(1)}, bf16[128,2048]{1,0:T(8,128)(2,1)S(1)}, u32[]{:S(2)}, u32[]{:S(2)}) collective-permute-start(bf16[128,2048]{1,0:T(8,128)(2,1)S(1)} %fusion.19), channel_id=1, source_target_pairs={{4,0},{8,4},{12,8},{16,12},{20,16},{24,20},{28,24},{32,28},{36,32}... | collective-permute-start | bytes 1572872 | tf_op jit(solution)/shard_map/ppermute | solution.py:19
  15.2 0.7 copy-start.5
  16.5 1.4 %copy-start.1 = (bf16[3,128,256]{2,1,0:T(8,128)(2,1)}, bf16[3,128,256]{2,1,0:T(8,128)(2,1)S(1)}, u32[]{:S(2)}) copy-start(bf16[3,128,256]{2,1,0:T(8,128)(2,1)S(1)} %and_convert_fusion.1.m_ref) | copy-start | bytes 589828
  16.5 1.3 %copy-start.4 = (bf16[128,128]{1,0:T(8,128)(2,1)S(1)}, bf16[128,128]{1,0:T(8,128)(2,1)}, u32[]{:S(2)}) copy-start(bf16[128,128]{1,0:T(8,128)(2,1)} %param.22) | copy-start | bytes 98308
  22.5 0.8 copy-start.2
  22.5 0.9 copy-start.3
  47.4 11.9 %collective-permute-start.2 = (f32[128,128]{1,0:T(8,128)S(1)}, f32[128,128]{1,0:T(8,128)S(1)}, u32[]{:S(2)}, u32[]{:S(2)}) collective-permute-start(f32[128,128]{1,0:T(8,128)S(1)} %rev.11), channel_id=1, source_target_pairs={{0,4},{4,0},{8,12},{12,8},{16,20},{20,16},{24,28},{28,24},{32,36},... | collective-permute-start | bytes 196616 | tf_op jit(solution)/shard_map/ppermute | solution.py:40
  47.5 14.3 %collective-permute-start.3 = (f32[128,128]{1,0:T(8,128)S(1)}, f32[128,128]{1,0:T(8,128)S(1)}, u32[]{:S(2)}, u32[]{:S(2)}) collective-permute-start(f32[128,128]{1,0:T(8,128)S(1)} %rev.11), channel_id=1, source_target_pairs={{0,8},{4,12},{8,0},{12,4},{16,24},{20,28},{24,16},{28,20},{32,40},... | collective-permute-start | bytes 196616 | tf_op jit(solution)/shard_map/ppermute | solution.py:40
  52.9 11.1 %collective-permute-start.4 = (f32[128,128]{1,0:T(8,128)S(1)}, f32[128,128]{1,0:T(8,128)S(1)}, u32[]{:S(2)}, u32[]{:S(2)}) collective-permute-start(f32[128,128]{1,0:T(8,128)S(1)} %rev.11), channel_id=1, source_target_pairs={{0,12},{4,8},{8,4},{12,0},{16,28},{20,24},{24,20},{28,16},{32,44},... | collective-permute-start | bytes 196616 | tf_op jit(solution)/shard_map/ppermute | solution.py:40
  53.5 10.5 %collective-permute-start.5 = (f32[128,128]{1,0:T(8,128)S(1)}, f32[128,128]{1,0:T(8,128)S(1)}, u32[]{:S(2)}, u32[]{:S(2)}) collective-permute-start(f32[128,128]{1,0:T(8,128)S(1)} %rev.11), channel_id=1, source_target_pairs={{0,16},{4,20},{8,24},{12,28},{16,0},{20,4},{24,8},{28,12},{32,48},... | collective-permute-start | bytes 196616 | tf_op jit(solution)/shard_map/ppermute | solution.py:40
  57.5 11.5 %collective-permute-start.6 = (f32[128,128]{1,0:T(8,128)S(1)}, f32[128,128]{1,0:T(8,128)S(1)}, u32[]{:S(2)}, u32[]{:S(2)}) collective-permute-start(f32[128,128]{1,0:T(8,128)S(1)} %rev.11), channel_id=1, source_target_pairs={{0,20},{4,16},{8,28},{12,24},{16,4},{20,0},{24,12},{28,8},{32,52},... | collective-permute-start | bytes 196616 | tf_op jit(solution)/shard_map/ppermute | solution.py:40
  59.3 10.4 %collective-permute-start.7 = (f32[128,128]{1,0:T(8,128)S(1)}, f32[128,128]{1,0:T(8,128)S(1)}, u32[]{:S(2)}, u32[]{:S(2)}) collective-permute-start(f32[128,128]{1,0:T(8,128)S(1)} %rev.11), channel_id=1, source_target_pairs={{0,24},{4,28},{8,16},{12,20},{16,8},{20,12},{24,0},{28,4},{32,56},... | collective-permute-start | bytes 196616 | tf_op jit(solution)/shard_map/ppermute | solution.py:40
  61.8 8.0 %collective-permute-start.8 = (f32[128,128]{1,0:T(8,128)S(1)}, f32[128,128]{1,0:T(8,128)S(1)}, u32[]{:S(2)}, u32[]{:S(2)}) collective-permute-start(f32[128,128]{1,0:T(8,128)S(1)} %rev.11), channel_id=1, source_target_pairs={{0,28},{4,24},{8,20},{12,16},{16,12},{20,8},{24,4},{28,0},{32,60},... | collective-permute-start | bytes 196616 | tf_op jit(solution)/shard_map/ppermute | solution.py:40
  70.5 5.9 %collective-permute-start.9 = (f32[128,128]{1,0:T(8,128)S(1)}, f32[128,128]{1,0:T(8,128)S(1)}, u32[]{:S(2)}, u32[]{:S(2)}) collective-permute-start(f32[128,128]{1,0:T(8,128)S(1)} %select_reduce_fusion.1), channel_id=1, source_target_pairs={{0,32},{4,36},{8,40},{12,44},{16,48},{20,52},{24,56},{28,60},{32,0... | collective-permute-start | bytes 196616 | tf_op jit(solution)/shard_map/ppermute | solution.py:40
  72.8 7.4 %collective-permute-start.10 = (f32[128,128]{1,0:T(8,128)S(1)}, f32[128,128]{1,0:T(8,128)S(1)}, u32[]{:S(2)}, u32[]{:S(2)}) collective-permute-start(f32[128,128]{1,0:T(8,128)S(1)} %select_reduce_fusion.1), channel_id=1, source_target_pairs={{0,64},{4,68},{8,72},{12,76},{16,80},{20,84},{24,88},{28,92},{32,9... | collective-permute-start | bytes 196616 | tf_op jit(solution)/shard_map/ppermute | solution.py:40
  75.8 5.5 %collective-permute-start.11 = (f32[128,128]{1,0:T(8,128)S(1)}, f32[128,128]{1,0:T(8,128)S(1)}, u32[]{:S(2)}, u32[]{:S(2)}) collective-permute-start(f32[128,128]{1,0:T(8,128)S(1)} %select_reduce_fusion.1), channel_id=1, source_target_pairs={{0,96},{4,100},{8,104},{12,108},{16,112},{20,116},{24,120},{28,124... | collective-permute-start | bytes 196616 | tf_op jit(solution)/shard_map/ppermute | solution.py:40
  75.8 5.5 %collective-permute-start.12 = (f32[128,128]{1,0:T(8,128)S(1)}, f32[128,128]{1,0:T(8,128)S(1)}, u32[]{:S(2)}, u32[]{:S(2)}) collective-permute-start(f32[128,128]{1,0:T(8,128)S(1)} %select_reduce_fusion.1), channel_id=1, source_target_pairs={{0,128},{4,132},{8,136},{12,140},{16,144},{20,148},{24,152},{28,15... | collective-permute-start | bytes 196616 | tf_op jit(solution)/shard_map/ppermute | solution.py:40
  75.8 5.5 %collective-permute-start.13 = (f32[128,128]{1,0:T(8,128)S(1)}, f32[128,128]{1,0:T(8,128)S(1)}, u32[]{:S(2)}, u32[]{:S(2)}) collective-permute-start(f32[128,128]{1,0:T(8,128)S(1)} %select_reduce_fusion.1), channel_id=1, source_target_pairs={{0,160},{4,164},{8,168},{12,172},{16,176},{20,180},{24,184},{28,18... | collective-permute-start | bytes 196616 | tf_op jit(solution)/shard_map/ppermute | solution.py:40
  76.4 7.2 %collective-permute-start.14 = (f32[128,128]{1,0:T(8,128)S(1)}, f32[128,128]{1,0:T(8,128)S(1)}, u32[]{:S(2)}, u32[]{:S(2)}) collective-permute-start(f32[128,128]{1,0:T(8,128)S(1)} %select_reduce_fusion.1), channel_id=1, source_target_pairs={{0,192},{4,196},{8,200},{12,204},{16,208},{20,212},{24,216},{28,22... | collective-permute-start | bytes 196616 | tf_op jit(solution)/shard_map/ppermute | solution.py:40
  80.2 5.0 %collective-permute-start.15 = (f32[128,128]{1,0:T(8,128)S(1)}, f32[128,128]{1,0:T(8,128)S(1)}, u32[]{:S(2)}, u32[]{:S(2)}) collective-permute-start(f32[128,128]{1,0:T(8,128)S(1)} %select_reduce_fusion.1), channel_id=1, source_target_pairs={{0,224},{4,228},{8,232},{12,236},{16,240},{20,244},{24,248},{28,25... | collective-permute-start | bytes 196616 | tf_op jit(solution)/shard_map/ppermute | solution.py:40
  86.5 4.7 %collective-permute-start.16 = (f32[]{:T(128)}, f32[]{:T(128)}, u32[]{:S(2)}, u32[]{:S(2)}) collective-permute-start(f32[]{:T(128)} %multiply_reduce_fusion), channel_id=1, source_target_pairs={{0,1},{1,0},{2,3},{3,2},{4,5},{5,4},{6,7},{7,6},{8,9},{9,8},{10,11... | collective-permute-start | bytes 20 | tf_op jit(solution)/shard_map/ppermute | solution.py:40
  88.0 5.3 %collective-permute-start.17 = (f32[]{:T(128)}, f32[]{:T(128)}, u32[]{:S(2)}, u32[]{:S(2)}) collective-permute-start(f32[]{:T(128)} %multiply_reduce_fusion), channel_id=1, source_target_pairs={{0,2},{1,3},{2,0},{3,1},{4,6},{5,7},{6,4},{7,5},{8,10},{9,11},{10,... | collective-permute-start | bytes 20 | tf_op jit(solution)/shard_map/ppermute | solution.py:40
  90.7 5.0 %collective-permute-start.18 = (f32[]{:T(128)}, f32[]{:T(128)}, u32[]{:S(2)}, u32[]{:S(2)}) collective-permute-start(f32[]{:T(128)} %multiply_reduce_fusion), channel_id=1, source_target_pairs={{0,3},{1,2},{2,1},{3,0},{4,7},{5,6},{6,5},{7,4},{8,11},{9,10},{10,... | collective-permute-start | bytes 20 | tf_op jit(solution)/shard_map/ppermute | solution.py:40

commit v4 on v2

--- a/solution.py
+++ b/solution.py
@@ -29,8 +29,36 @@
     return value
 
 
-def conv_kernel(q_ref, k_ref, v_ref, go_ref, prev_ref, next_ref, fp_ref, fq_ref, m_ref, mt_ref, mr_ref,
-                mo_ref, gq_ref, gk_ref, gv_ref, raw_ref):
+def raw_kernel(q_ref, k_ref, v_ref, go_ref, prev_ref, mr_ref, raw_ref):
+    f32, bf16 = jnp.float32, jnp.bfloat16
+    rows = q_ref.shape[0]
+    blocks = rows // FLEN
+    gated = (k_ref[...].astype(f32) * v_ref[...].astype(f32)).astype(bf16)
+    cot = (go_ref[...].astype(f32) * q_ref[...].astype(f32)).astype(bf16)
+    u_all = jnp.concatenate([prev_ref[...], gated], axis=0)
+    lane_group = lax.broadcasted_iota(jnp.int32, (1, LANES), 1) // GROUP
+    windows = [u_all[b * FLEN:(b + 2) * FLEN] for b in range(blocks)]
+    masks_r = [mr_ref[b].astype(f32) for b in range(blocks)]
+    flip = (lax.broadcasted_iota(jnp.int32, (FLEN, FLEN), 0)
+            + lax.broadcasted_iota(jnp.int32, (FLEN, FLEN), 1) == FLEN - 1).astype(bf16)
+    cots_r = [jnp.dot(flip, cot[b * FLEN:(b + 1) * FLEN], preferred_element_type=f32).astype(bf16)
+              for b in range(blocks)]
+    nt = (((1,), (1,)), ((), ()))
+    sums = []
+    for k in range(LANES // GROUP):
+        in_group = lane_group == k
+        acc = jnp.zeros((FLEN, 2 * FLEN), f32)
+        for b in range(blocks):
+            group_cot = jnp.where(in_group, cots_r[b], jnp.zeros_like(cots_r[b]))
+            prods = lax.dot_general(group_cot, windows[b], nt, preferred_element_type=f32)
+            acc = acc + prods * masks_r[b]
+        skewed = pltpu.roll(acc, 0, 1, stride=1, stride_axis=0)
+        sums.append(jnp.sum(skewed, axis=0, keepdims=True))
+    raw_ref[0] = jnp.concatenate(sums, axis=0)
+
+
+def conv_kernel(q_ref, k_ref, v_ref, go_ref, prev_ref, next_ref, fp_ref, fq_ref, m_ref, mt_ref, *refs):
+    mo_ref, gq_ref, gk_ref, gv_ref = refs[-4:]
     f32, bf16 = jnp.float32, jnp.bfloat16
     rows = q_ref.shape[0]
     blocks = rows // FLEN
@@ -47,14 +75,8 @@
     cots = [c_all[b * FLEN:(b + 1) * FLEN] for b in range(blocks + 1)]
     masks = [m_ref[b] for b in range(blocks + 1)]
     masks_t = [mt_ref[b] for b in range(blocks + 1)]
-    masks_r = [mr_ref[b].astype(f32) for b in range(blocks)]
-    flip = (lax.broadcasted_iota(jnp.int32, (FLEN, FLEN), 0)
-            + lax.broadcasted_iota(jnp.int32, (FLEN, FLEN), 1) == FLEN - 1).astype(bf16)
-    cots_r = [jnp.dot(flip, cots[b], preferred_element_type=f32).astype(bf16) for b in range(blocks)]
     mixed = [jnp.zeros((FLEN, LANES), f32) for _ in range(blocks)]
     back = [jnp.zeros((FLEN, LANES), f32) for _ in range(blocks)]
-    nt = (((1,), (1,)), ((), ()))
-    sums = []
     for k in range(LANES // GROUP):
         prow = jnp.broadcast_to(fp_ref[k:k + 1, :], (FLEN, 2 * FLEN))
         taps = pltpu.roll(prow, 0, 1, stride=1, stride_axis=0).astype(bf16)
@@ -62,22 +84,15 @@
         taps_t = pltpu.roll(qrow, FLEN, 1, stride=1, stride_axis=0)[:, :FLEN].astype(bf16)
         in_group = lane_group == k
         group_cots = [jnp.where(in_group, c, jnp.zeros_like(c)) for c in cots]
-        group_cots_r = [jnp.where(in_group, c, jnp.zeros_like(c)) for c in cots_r]
-        acc = jnp.zeros((FLEN, 2 * FLEN), f32)
         for b in range(blocks):
             window = jnp.where(in_group, windows[b], jnp.zeros_like(windows[b]))
             mixed[b] = mixed[b] + jnp.dot(taps * masks[b], window, preferred_element_type=f32)
-            prods = lax.dot_general(group_cots_r[b], windows[b], nt, preferred_element_type=f32)
-            acc = acc + prods * masks_r[b]
         for b in range(blocks + 1):
             spread = jnp.dot(taps_t * masks_t[b], group_cots[b], preferred_element_type=f32)
             if b < blocks:
                 back[b] = back[b] + spread[FLEN:]
             if b > 0:
                 back[b - 1] = back[b - 1] + spread[:FLEN]
-        skewed = pltpu.roll(acc, 0, 1, stride=1, stride_axis=0)
-        sums.append(jnp.sum(skewed, axis=0, keepdims=True))
-    raw_ref[0] = jnp.concatenate(sums, axis=0)
     mixed_all = jnp.concatenate(mixed, axis=0)
     back_all = jnp.concatenate(back, axis=0)
     mo_ref[...] = (query * mixed_all).astype(bf16)
@@ -86,28 +101,64 @@
     gv_ref[...] = (back_all * keys).astype(bf16)
 
 
-def grouped_conv(q2, k2, v2, g2, prev_tail, next_head, fp, fq, mask, mask_t, interpret=False):
-    mask_r = mask[:-1, ::-1, :]
+def raw_terms(q2, k2, v2, g2, prev_tail, mask, interpret=False):
     rows, channels = q2.shape
     tiles = channels // LANES
     per_tile = LANES // GROUP
     nb = rows // FLEN
+    mask_r = mask[:-1, ::-1, :]
     tok = pl.BlockSpec((rows, LANES), lambda j: (0, j))
     halo = pl.BlockSpec((FLEN, LANES), lambda j: (0, j))
-    filt = pl.BlockSpec((per_tile, 2 * FLEN), lambda j: (j, 0))
+    mrspec = pl.BlockSpec((nb, FLEN, 2 * FLEN), lambda j: (0, 0, 0))
+    return pl.pallas_call(
+        raw_kernel,
+        grid=(tiles,),
+        in_specs=[tok, tok, tok, tok, halo, mrspec],
+        out_specs=pl.BlockSpec((1, per_tile, 2 * FLEN), lambda j: (j, 0, 0)),
+        out_shape=jax.ShapeDtypeStruct((tiles, per_tile, 2 * FLEN), jnp.float32),
+        interpret=interpret,
+    )(q2, k2, v2, g2, prev_tail, mask_r)
+
+
+def conv_part(args, first, count, outs=None, interpret=False):
+    q2 = args[0]
+    rows, channels = q2.shape
+    per_tile = LANES // GROUP
+    nb = rows // FLEN
+    tok = pl.BlockSpec((rows, LANES), lambda j: (0, j + first))
+    halo = pl.BlockSpec((FLEN, LANES), lambda j: (0, j + first))
+    filt = pl.BlockSpec((per_tile, 2 * FLEN), lambda j: (j + first, 0))
     mspec = pl.BlockSpec((nb + 1, FLEN, 2 * FLEN), lambda j: (0, 0, 0))
     mtspec = pl.BlockSpec((nb + 1, 2 * FLEN, FLEN), lambda j: (0, 0, 0))
-    mrspec = pl.BlockSpec((nb, FLEN, 2 * FLEN), lambda j: (0, 0, 0))
+    in_specs = [tok, tok, tok, tok, halo, halo, filt, filt, mspec, mtspec]
+    operands = list(args)
+    aliases = {}
+    if outs is not None:
+        for i, o in enumerate(outs):
+            aliases[len(operands)] = i
+            operands.append(o)
+            in_specs.append(pl.BlockSpec(memory_space=pl.ANY))
     out_tok = jax.ShapeDtypeStruct((rows, channels), jnp.bfloat16)
     return pl.pallas_call(
         conv_kernel,
-        grid=(tiles,),
-        in_specs=[tok, tok, tok, tok, halo, halo, filt, filt, mspec, mtspec, mrspec],
-        out_specs=[tok, tok, tok, tok, pl.BlockSpec((1, per_tile, 2 * FLEN), lambda j: (j, 0, 0))],
-        out_shape=[out_tok, out_tok, out_tok, out_tok,
-                   jax.ShapeDtypeStruct((tiles, per_tile, 2 * FLEN), jnp.float32)],
+        grid=(count,),
+        in_specs=in_specs,
+        out_specs=[tok, tok, tok, tok],
+        out_shape=[out_tok] * 4,
+        input_output_aliases=aliases,
         interpret=interpret,
-    )(q2, k2, v2, g2, prev_tail, next_head, fp, fq, mask, mask_t, mask_r)
+    )(*operands)
+
+
+def grouped_conv(q2, k2, v2, g2, prev_tail, next_head, fp, fq, mask, mask_t, parts=4, interpret=False):
+    tiles = q2.shape[1] // LANES
+    args = (q2, k2, v2, g2, prev_tail, next_head, fp, fq, mask, mask_t)
+    cols = raw_terms(q2, k2, v2, g2, prev_tail, mask, interpret=interpret)
+    outs = None
+    step = tiles // parts
+    for p in range(parts):
+        outs = conv_part(args, p * step, step, outs, interpret=interpret)
+    return (*outs, cols)
 
 
 def doc_masks(lengths, offset, rows):
@@ -132,21 +183,49 @@
     return fp, fq
 
 
+def exchange_round(value, axis, step):
+    count = lax.axis_size(axis)
+    partner = lax.ppermute(value, axis, [(i, i ^ step) for i in range(count)])
+    return value + partner
+
+
 def on_device(query_in, key_in, value_in, grad_out, seq_lengths, filters):
     f32, bf16 = jnp.float32, jnp.bfloat16
     q2, k2, v2, g2 = query_in[0], key_in[0], value_in[0], grad_out[0]
-    rows = q2.shape[0]
+    rows, channels = q2.shape
     tail = (k2[rows - FLEN:].astype(f32) * v2[rows - FLEN:].astype(f32)).astype(bf16)
     head = (g2[:FLEN].astype(f32) * q2[:FLEN].astype(f32)).astype(bf16)
     prev_tail = passed_along(tail, "ctx", 1)
     next_head = passed_along(head, "ctx", -1)
     mask, mask_t = doc_masks(seq_lengths[0], lax.axis_index("ctx") * rows, rows)
     fp, fq = filter_rows(filters)
-    mixed_out, grad_query, grad_key, grad_value, cols = grouped_conv(
-        q2, k2, v2, g2, prev_tail, next_head, fp, fq, mask, mask_t)
+    cols = raw_terms(q2, k2, v2, g2, prev_tail, mask)
     local_raw = cols.reshape(-1, 2 * FLEN)[:, 2 * FLEN - 1:FLEN - 1:-1]
-    summed = doubling_sum(doubling_sum(local_raw, "dp"), "ctx")
-    squares = doubling_sum(jnp.sum(summed * summed), "tensor")
+    rounds = [("dp", 1 << i) for i in range(lax.axis_size("dp").bit_length() - 1)]
+    rounds += [("ctx", 1 << i) for i in range(lax.axis_size("ctx").bit_length() - 1)]
+    tensor_rounds = [("tensor", 1 << i) for i in range(lax.axis_size("tensor").bit_length() - 1)]
+    stages = len(rounds) + len(tensor_rounds)
+    tiles = channels // LANES
+    parts = stages if tiles % stages == 0 else 1
+    step = tiles // parts
+    args = (q2, k2, v2, g2, prev_tail, next_head, fp, fq, mask, mask_t)
+    outs = None
+    summed = local_raw
+    squares = None
+    for stage in range(stages):
+        if stage < len(rounds):
+            summed = exchange_round(summed, *rounds[stage])
+            if stage == len(rounds) - 1:
+                squares = jnp.sum(summed * summed)
+        else:
+            squares = exchange_round(squares, *tensor_rounds[stage - len(rounds)])
+        if stage < parts:
+            outs = conv_part(args, stage * step, step, outs)
+        if squares is None:
+            summed, outs = lax.optimization_barrier((summed, outs))
+        else:
+            summed, squares, outs = lax.optimization_barrier((summed, squares, outs))
+    mixed_out, grad_query, grad_key, grad_value = outs
     factor = jnp.minimum(1.0, math.sqrt(GROUPS * FLEN) / jnp.sqrt(squares))
     grad_filters = summed * factor
     return (mixed_out[None], grad_query[None], grad_key[None], grad_value[None], grad_filters)

time: 93.2 us -> 94.2 us (1.011)
  waiting for transfers between devices: 29.2 us -> 4.45 us
  Pallas kernels: 23 us -> 45.9 us
  starting transfers between devices: 25.7 us -> 27.2 us
    pallas_call x1 -> x9, Pallas kernels: 23 us -> 45.9 us  [the longest x8 31.5 us: conv_part(): pl.pallas_call(conv_kernel, grid=(count,), in_specs=in_specs, out_specs=[...]
    ppermute x8, waiting for transfers between devices: 21.9 us -> 0.53 us  [exchange_round(): partner = lax.ppermute(value, axis, [(i, i ^ step) for i in range(count)])]
    ppermute x2, waiting for transfers between devices: 7.33 us -> 3.92 us  [passed_along(): lax.ppermute(value, axis, [(source, source + steps) for source in range(i...]
    ppermute x8, starting transfers between devices: 19.8 us -> 21.3 us  [exchange_round(): partner = lax.ppermute(value, axis, [(i, i ^ step) for i in range(count)])]
  transfers between devices with their start and end apart: 10 -> 10, of which waited for: 10 -> 2; matrix products, arithmetic and copies ran while one was open for 6% -> 7% of each run, Pallas kernels for 0% -> 50%
where the time goes in v4:
time: 94.2 us; the launch traced here: 92.7 us
  Pallas kernels  45.9 us (49%)
  starting transfers between devices  27.2 us (29%)
  other arithmetic  6.22 us (7%)
  local copies, waits for them, and re-layouts  6.07 us (6%)
  waiting for transfers between devices  4.45 us (5%)
  between operations  2.89 us (3%)
    pallas_call x8, Pallas kernels, conv_part(): pl.pallas_call(conv_kernel, grid=(count,), in_specs=in_specs, out_specs=[...  31.5 us
    ppermute x8, starting transfers between devices, exchange_round(): partner = lax.ppermute(value, axis, [(i, i ^ step) for i in range(count)])  21.3 us
    pallas_call x1, Pallas kernels, raw_terms(): pl.pallas_call(raw_kernel, grid=(tiles,), in_specs=[tok, tok, tok, tok, h...  14.4 us
    ppermute x2, starting transfers between devices, passed_along(): lax.ppermute(value, axis, [(source, source + steps) for source in range(i...  5.87 us
    ppermute x2, waiting for transfers between devices, passed_along(): lax.ppermute(value, axis, [(source, source + steps) for source in range(i...  3.92 us
    unnamed x12, local copies, waits for them, and re-layouts  2.9 us
  transfers between devices with their start and end apart: 10, of which 2 were waited for; matrix products, arithmetic and copies ran while one was open for 7% of the time, Pallas kernels for 50%

profile of v4, /device:TPU:32, one launch (start us, length us, event | category | flops | bytes accessed | tf_op | source)
XLA Modules:
  0.0 92.7 jit_solution(4318977877372681255)
XLA Ops:
  0.6 0.0 copy-start
  0.6 1.4 %fusion = bf16[128,2048]{1,0:T(8,128)(2,1)S(1)} fusion(bf16[1,256,2048]{2,1,0:T(8,128)(2,1)} %param.8, bf16[1,256,2048]{2,1,0:T(8,128)(2,1)} %param.7), kind=kLoop, calls=%fused_computation.2 | loop fusion | flops 1048576 | bytes 1572864 | tf_op jit(solution)/shard_map/convert_element_type | solution.py:196
  2.1 3.8 %collective-permute-start = (bf16[128,2048]{1,0:T(8,128)(2,1)S(1)}, bf16[128,2048]{1,0:T(8,128)(2,1)S(1)}, u32[]{:S(2)}, u32[]{:S(2)}) collective-permute-start(bf16[128,2048]{1,0:T(8,128)(2,1)S(1)} %fusion), channel_id=1, source_target_pairs={{0,4},{4,8},{8,12},{12,16},{16,20},{20,24},{24,28},{28,32},{32,36}... | collective-permute-start | bytes 1572872 | tf_op jit(solution)/shard_map/ppermute | solution.py:19
  5.9 0.0 copy-done
  5.9 1.2 %fusion.1 = bf16[128,2048]{1,0:T(8,128)(2,1)S(1)} fusion(bf16[1,256,2048]{2,1,0:T(8,128)(2,1)S(1)} %copy-done, bf16[1,256,2048]{2,1,0:T(8,128)(2,1)} %param.9), kind=kLoop, calls=%fused_computation.3 | loop fusion | flops 1048576 | bytes 1572864 | tf_op jit(solution)/shard_map/convert_element_type | solution.py:197
  7.1 2.0 %collective-permute-start.2 = (bf16[128,2048]{1,0:T(8,128)(2,1)S(1)}, bf16[128,2048]{1,0:T(8,128)(2,1)S(1)}, u32[]{:S(2)}, u32[]{:S(2)}) collective-permute-start(bf16[128,2048]{1,0:T(8,128)(2,1)S(1)} %fusion.1), channel_id=1, source_target_pairs={{4,0},{8,4},{12,8},{16,12},{20,16},{24,20},{28,24},{32,28},{36,32}... | collective-permute-start | bytes 1572872 | tf_op jit(solution)/shard_map/ppermute | solution.py:19
  9.2 0.1 iota_add_fusion.1
  9.2 0.1 iota_add_fusion
  9.3 0.1 fusion.6
  9.4 0.0 copy-start.5
  9.4 0.6 copy-done.5
  10.1 0.1 copy.41
  10.2 0.1 reduce-window.8
  10.3 0.1 reduce
  10.4 0.1 select_reduce_fusion
  10.5 0.1 and_convert_fusion.1.m_ref
  10.6 0.0 copy-start.3
  10.6 0.0 copy-start.4
  10.7 0.1 pad.3.clone
  10.8 0.6 copy-done.4
  11.4 0.1 rev.11
  11.5 0.0 copy-done.3
  11.5 1.3 %rev.9.mr_ref = bf16[2,128,256]{2,1,0:T(8,128)(2,1)} reverse(bf16[2,128,256]{2,1,0:T(8,128)(2,1)S(1)} %slice.28), dimensions={1} | reverse | bytes 262144 | tf_op jit(solution)/shard_map/rev | solution.py:109
  12.9 0.8 and_convert_fusion.mt_ref
  13.7 3.9 %collective-permute-done.prev_ref = bf16[128,2048]{1,0:T(8,128)(2,1)S(1)} collective-permute-done((bf16[128,2048]{1,0:T(8,128)(2,1)S(1)}, bf16[128,2048]{1,0:T(8,128)(2,1)S(1)}, u32[]{:S(2)}, u32[]{:S(2)}) %collective-permute-start) | collective-permute-done | bytes 524320 | tf_op jit(solution)/shard_map/ppermute | solution.py:19
  17.6 0.0 copy-start.1
  17.6 0.8 copy-done.1
  18.4 14.4 %shard_map.101 = f32[16,8,256]{2,1,0:T(8,128)} custom-call(bf16[256,2048]{1,0:T(8,128)(2,1)} %bitcast.17, bf16[256,2048]{1,0:T(8,128)(2,1)} %bitcast.26, bf16[256,2048]{1,0:T(8,128)(2,1)} %bitcast.35, bf16[256,2048]{1,0:T(8,128)(2,1)} %bitcast.44, bf16[128,2048]{1,0:T(8,128)(2,1)} %copy-done.1, bf16[2,128,256]{2,1,0:T(8,128)(2,1)} %rev.9.mr_ref), custom_call_target="tpu_custom_call" | custom-call | tf_op jit(solution)/shard_map/pallas_call | solution.py:113
  32.8 0.8 slice.29
  33.6 0.1 rev.10
  33.7 0.1 collective-permute-start.1
  33.8 0.8 maximum_maximum_fusion.fp_ref
  34.5 0.7 concatenate.7.fq_ref
  35.2 0.0 collective-permute-done.2.next_ref
  35.2 0.0 copy-start.2
  35.2 0.8 copy-done.2
  36.0 3.9 %shard_map.102 = (bf16[256,2048]{1,0:T(8,128)(2,1)}, bf16[256,2048]{1,0:T(8,128)(2,1)}, bf16[256,2048]{1,0:T(8,128)(2,1)}, bf16[256,2048]{1,0:T(8,128)(2,1)}) custom-call(bf16[256,2048]{1,0:T(8,128)(2,1)} %bitcast.18, bf16[256,2048]{1,0:T(8,128)(2,1)} %bitcast.27, bf16[256,2048]{1,0:T(8,128)(2,1)} %bitcast.36, bf16[256,2048]{1,0:T(8,128)(2,1)} %bitcast.45, ...), custom_call_target="tpu_custom_call" | custom-call | tf_op jit(solution)/shard_map/pallas_call | solution.py:142
  39.9 0.0 collective-permute-done.1
  40.0 0.1 collective-permute-start.3
  40.1 4.0 %shard_map.103 = (bf16[256,2048]{1,0:T(8,128)(2,1)}, bf16[256,2048]{1,0:T(8,128)(2,1)}, bf16[256,2048]{1,0:T(8,128)(2,1)}, bf16[256,2048]{1,0:T(8,128)(2,1)}) custom-call(bf16[256,2048]{1,0:T(8,128)(2,1)} %bitcast.19, bf16[256,2048]{1,0:T(8,128)(2,1)} %bitcast.28, ...), custom_call_target="tpu_custom_call", output_to_operand_aliasing={{0}: (10, {}), {1}: (11, {}), {2}: (12, {}), {3}: (13, {})} | custom-call | tf_op jit(solution)/shard_map/pallas_call | solution.py:142
  44.0 0.5 collective-permute-done.3
  44.6 4.0 %collective-permute-start.4 = (f32[128,128]{1,0:T(8,128)S(1)}, f32[128,128]{1,0:T(8,128)S(1)}, u32[]{:S(2)}, u32[]{:S(2)}) collective-permute-start(f32[128,128]{1,0:T(8,128)S(1)} %add.111), channel_id=1, source_target_pairs={{0,8},{4,12},{8,0},{12,4},{16,24},{20,28},{24,16},{28,20},{32,40},... | collective-permute-start | bytes 196616 | tf_op jit(solution)/shard_map/ppermute | solution.py:188
  48.6 3.9 %shard_map.104 = (bf16[256,2048]{1,0:T(8,128)(2,1)}, bf16[256,2048]{1,0:T(8,128)(2,1)}, bf16[256,2048]{1,0:T(8,128)(2,1)}, bf16[256,2048]{1,0:T(8,128)(2,1)}) custom-call(bf16[256,2048]{1,0:T(8,128)(2,1)} %bitcast.20, bf16[256,2048]{1,0:T(8,128)(2,1)} %bitcast.29, ...), custom_call_target="tpu_custom_call", output_to_operand_aliasing={{0}: (10, {}), {1}: (11, {}), {2}: (12, {}), {3}: (13, {})} | custom-call | tf_op jit(solution)/shard_map/pallas_call | solution.py:142
  52.5 0.0 collective-permute-done.4
  52.5 5.4 %collective-permute-start.5 = (f32[128,128]{1,0:T(8,128)S(1)}, f32[128,128]{1,0:T(8,128)S(1)}, u32[]{:S(2)}, u32[]{:S(2)}) collective-permute-start(f32[128,128]{1,0:T(8,128)S(1)} %add.112), channel_id=1, source_target_pairs={{0,16},{4,20},{8,24},{12,28},{16,0},{20,4},{24,8},{28,12},{32,48},... | collective-permute-start | bytes 196616 | tf_op jit(solution)/shard_map/ppermute | solution.py:188
  57.9 3.9 %shard_map.105 = (bf16[256,2048]{1,0:T(8,128)(2,1)}, bf16[256,2048]{1,0:T(8,128)(2,1)}, bf16[256,2048]{1,0:T(8,128)(2,1)}, bf16[256,2048]{1,0:T(8,128)(2,1)}) custom-call(bf16[256,2048]{1,0:T(8,128)(2,1)} %bitcast.21, bf16[256,2048]{1,0:T(8,128)(2,1)} %bitcast.30, ...), custom_call_target="tpu_custom_call", output_to_operand_aliasing={{0}: (10, {}), {1}: (11, {}), {2}: (12, {}), {3}: (13, {})} | custom-call | tf_op jit(solution)/shard_map/pallas_call | solution.py:142
  61.9 0.0 collective-permute-done.5
  61.9 2.9 %collective-permute-start.6 = (f32[128,128]{1,0:T(8,128)S(1)}, f32[128,128]{1,0:T(8,128)S(1)}, u32[]{:S(2)}, u32[]{:S(2)}) collective-permute-start(f32[128,128]{1,0:T(8,128)S(1)} %add.113), channel_id=1, source_target_pairs={{0,32},{4,36},{8,40},{12,44},{16,48},{20,52},{24,56},{28,60},{32,0... | collective-permute-start | bytes 196616 | tf_op jit(solution)/shard_map/ppermute | solution.py:188
  64.8 3.9 %shard_map.106 = (bf16[256,2048]{1,0:T(8,128)(2,1)}, bf16[256,2048]{1,0:T(8,128)(2,1)}, bf16[256,2048]{1,0:T(8,128)(2,1)}, bf16[256,2048]{1,0:T(8,128)(2,1)}) custom-call(bf16[256,2048]{1,0:T(8,128)(2,1)} %bitcast.22, bf16[256,2048]{1,0:T(8,128)(2,1)} %bitcast.31, ...), custom_call_target="tpu_custom_call", output_to_operand_aliasing={{0}: (10, {}), {1}: (11, {}), {2}: (12, {}), {3}: (13, {})} | custom-call | tf_op jit(solution)/shard_map/pallas_call | solution.py:142
  68.8 0.0 collective-permute-done.6
  68.8 3.2 %collective-permute-start.7 = (f32[128,128]{1,0:T(8,128)S(1)}, f32[128,128]{1,0:T(8,128)S(1)}, u32[]{:S(2)}, u32[]{:S(2)}) collective-permute-start(f32[128,128]{1,0:T(8,128)S(1)} %add.114), channel_id=1, source_target_pairs={{0,64},{4,68},{8,72},{12,76},{16,80},{20,84},{24,88},{28,92},{32,9... | collective-permute-start | bytes 196616 | tf_op jit(solution)/shard_map/ppermute | solution.py:188
  72.0 3.9 %shard_map.107 = (bf16[256,2048]{1,0:T(8,128)(2,1)}, bf16[256,2048]{1,0:T(8,128)(2,1)}, bf16[256,2048]{1,0:T(8,128)(2,1)}, bf16[256,2048]{1,0:T(8,128)(2,1)}) custom-call(bf16[256,2048]{1,0:T(8,128)(2,1)} %bitcast.23, bf16[256,2048]{1,0:T(8,128)(2,1)} %bitcast.32, ...), custom_call_target="tpu_custom_call", output_to_operand_aliasing={{0}: (10, {}), {1}: (11, {}), {2}: (12, {}), {3}: (13, {})} | custom-call | tf_op jit(solution)/shard_map/pallas_call | solution.py:142
  76.0 0.0 collective-permute-done.7
  76.0 0.6 multiply_reduce_fusion
  76.6 1.5 %collective-permute-start.8 = (f32[]{:T(128)}, f32[]{:T(128)}, u32[]{:S(2)}, u32[]{:S(2)}) collective-permute-start(f32[]{:T(128)} %get-tuple-element.130), channel_id=1, source_target_pairs={{0,1},{1,0},{2,3},{3,2},{4,5},{5,4},{6,7},{7,6},{8,9},{9,8},{10,11... | collective-permute-start | bytes 20 | tf_op jit(solution)/shard_map/ppermute | solution.py:188
  78.1 3.9 %shard_map.108 = (bf16[256,2048]{1,0:T(8,128)(2,1)}, bf16[256,2048]{1,0:T(8,128)(2,1)}, bf16[256,2048]{1,0:T(8,128)(2,1)}, bf16[256,2048]{1,0:T(8,128)(2,1)}) custom-call(bf16[256,2048]{1,0:T(8,128)(2,1)} %bitcast.24, bf16[256,2048]{1,0:T(8,128)(2,1)} %bitcast.33, ...), custom_call_target="tpu_custom_call", output_to_operand_aliasing={{0}: (10, {}), {1}: (11, {}), {2}: (12, {}), {3}: (13, {})} | custom-call | tf_op jit(solution)/shard_map/pallas_call | solution.py:142
  82.0 0.0 collective-permute-done.8
  83.3 4.1 %collective-permute-start.9 = (f32[]{:T(128)}, f32[]{:T(128)}, u32[]{:S(2)}, u32[]{:S(2)}) collective-permute-start(f32[]{:T(128)} %add.116), channel_id=1, source_target_pairs={{0,2},{1,3},{2,0},{3,1},{4,6},{5,7},{6,4},{7,5},{8,10},{9,11},{10,... | collective-permute-start | bytes 20 | tf_op jit(solution)/shard_map/ppermute | solution.py:188
  87.5 3.9 %shard_map.109 = (bf16[256,2048]{1,0:T(8,128)(2,1)}, bf16[256,2048]{1,0:T(8,128)(2,1)}, bf16[256,2048]{1,0:T(8,128)(2,1)}, bf16[256,2048]{1,0:T(8,128)(2,1)}) custom-call(bf16[256,2048]{1,0:T(8,128)(2,1)} %bitcast.25, bf16[256,2048]{1,0:T(8,128)(2,1)} %bitcast.34, ...), custom_call_target="tpu_custom_call", output_to_operand_aliasing={{0}: (10, {}), {1}: (11, {}), {2}: (12, {}), {3}: (13, {})} | custom-call | tf_op jit(solution)/shard_map/pallas_call | solution.py:142
  91.4 0.0 collective-permute-done.9
  92.1 0.6 broadcast_multiply_fusion
  (12 shorter events, 0.1 us)
Async XLA Ops:
  0.6 5.3 %copy-start = (bf16[1,256,2048]{2,1,0:T(8,128)(2,1)S(1)}, bf16[1,256,2048]{2,1,0:T(8,128)(2,1)}, u32[]{:S(2)}) copy-start(bf16[1,256,2048]{2,1,0:T(8,128)(2,1)} %param.6) | copy-start | bytes 3145732
  2.1 15.6 %collective-permute-start = (bf16[128,2048]{1,0:T(8,128)(2,1)S(1)}, bf16[128,2048]{1,0:T(8,128)(2,1)S(1)}, u32[]{:S(2)}, u32[]{:S(2)}) collective-permute-start(bf16[128,2048]{1,0:T(8,128)(2,1)S(1)} %fusion), channel_id=1, source_target_pairs={{0,4},{4,8},{8,12},{12,16},{16,20},{20,24},{24,28},{28,32},{32,36}... | collective-permute-start | bytes 1572872 | tf_op jit(solution)/shard_map/ppermute | solution.py:19
  7.1 28.1 %collective-permute-start.2 = (bf16[128,2048]{1,0:T(8,128)(2,1)S(1)}, bf16[128,2048]{1,0:T(8,128)(2,1)S(1)}, u32[]{:S(2)}, u32[]{:S(2)}) collective-permute-start(bf16[128,2048]{1,0:T(8,128)(2,1)S(1)} %fusion.1), channel_id=1, source_target_pairs={{4,0},{8,4},{12,8},{16,12},{20,16},{24,20},{28,24},{32,28},{36,32}... | collective-permute-start | bytes 1572872 | tf_op jit(solution)/shard_map/ppermute | solution.py:19
  9.4 0.7 copy-start.5
  10.6 0.9 copy-start.3
  10.6 0.8 copy-start.4
  17.6 0.8 copy-start.1
  33.7 6.2 %collective-permute-start.1 = (f32[128,128]{1,0:T(8,128)S(1)}, f32[128,128]{1,0:T(8,128)S(1)}, u32[]{:S(2)}, u32[]{:S(2)}) collective-permute-start(f32[128,128]{1,0:T(8,128)S(1)} %rev.10), channel_id=1, source_target_pairs={{0,128},{128,0},{1,129},{129,1},{2,130},{130,2},{3,131},{131,3},{4... | collective-permute-start | bytes 196616 | tf_op jit(solution)/shard_map/ppermute | solution.py:188
  35.2 0.8 copy-start.2
  40.0 4.6 %collective-permute-start.3 = (f32[128,128]{1,0:T(8,128)S(1)}, f32[128,128]{1,0:T(8,128)S(1)}, u32[]{:S(2)}, u32[]{:S(2)}) collective-permute-start(f32[128,128]{1,0:T(8,128)S(1)} %add.110), channel_id=1, source_target_pairs={{0,4},{4,0},{8,12},{12,8},{16,20},{20,16},{24,28},{28,24},{32,36},... | collective-permute-start | bytes 196616 | tf_op jit(solution)/shard_map/ppermute | solution.py:188
  44.6 7.9 %collective-permute-start.4 = (f32[128,128]{1,0:T(8,128)S(1)}, f32[128,128]{1,0:T(8,128)S(1)}, u32[]{:S(2)}, u32[]{:S(2)}) collective-permute-start(f32[128,128]{1,0:T(8,128)S(1)} %add.111), channel_id=1, source_target_pairs={{0,8},{4,12},{8,0},{12,4},{16,24},{20,28},{24,16},{28,20},{32,40},... | collective-permute-start | bytes 196616 | tf_op jit(solution)/shard_map/ppermute | solution.py:188
  52.5 9.4 %collective-permute-start.5 = (f32[128,128]{1,0:T(8,128)S(1)}, f32[128,128]{1,0:T(8,128)S(1)}, u32[]{:S(2)}, u32[]{:S(2)}) collective-permute-start(f32[128,128]{1,0:T(8,128)S(1)} %add.112), channel_id=1, source_target_pairs={{0,16},{4,20},{8,24},{12,28},{16,0},{20,4},{24,8},{28,12},{32,48},... | collective-permute-start | bytes 196616 | tf_op jit(solution)/shard_map/ppermute | solution.py:188
  61.9 6.8 %collective-permute-start.6 = (f32[128,128]{1,0:T(8,128)S(1)}, f32[128,128]{1,0:T(8,128)S(1)}, u32[]{:S(2)}, u32[]{:S(2)}) collective-permute-start(f32[128,128]{1,0:T(8,128)S(1)} %add.113), channel_id=1, source_target_pairs={{0,32},{4,36},{8,40},{12,44},{16,48},{20,52},{24,56},{28,60},{32,0... | collective-permute-start | bytes 196616 | tf_op jit(solution)/shard_map/ppermute | solution.py:188
  68.8 7.2 %collective-permute-start.7 = (f32[128,128]{1,0:T(8,128)S(1)}, f32[128,128]{1,0:T(8,128)S(1)}, u32[]{:S(2)}, u32[]{:S(2)}) collective-permute-start(f32[128,128]{1,0:T(8,128)S(1)} %add.114), channel_id=1, source_target_pairs={{0,64},{4,68},{8,72},{12,76},{16,80},{20,84},{24,88},{28,92},{32,9... | collective-permute-start | bytes 196616 | tf_op jit(solution)/shard_map/ppermute | solution.py:188
  76.6 5.4 %collective-permute-start.8 = (f32[]{:T(128)}, f32[]{:T(128)}, u32[]{:S(2)}, u32[]{:S(2)}) collective-permute-start(f32[]{:T(128)} %get-tuple-element.130), channel_id=1, source_target_pairs={{0,1},{1,0},{2,3},{3,2},{4,5},{5,4},{6,7},{7,6},{8,9},{9,8},{10,11... | collective-permute-start | bytes 20 | tf_op jit(solution)/shard_map/ppermute | solution.py:188
  83.3 8.1 %collective-permute-start.9 = (f32[]{:T(128)}, f32[]{:T(128)}, u32[]{:S(2)}, u32[]{:S(2)}) collective-permute-start(f32[]{:T(128)} %add.116), channel_id=1, source_target_pairs={{0,2},{1,3},{2,0},{3,1},{4,6},{5,7},{6,4},{7,5},{8,10},{9,11},{10,... | collective-permute-start | bytes 20 | tf_op jit(solution)/shard_map/ppermute | solution.py:188

commit v5 on v2

--- a/solution.py
+++ b/solution.py
@@ -53,31 +53,32 @@
     cots_r = [jnp.dot(flip, cots[b], preferred_element_type=f32).astype(bf16) for b in range(blocks)]
     mixed = [jnp.zeros((FLEN, LANES), f32) for _ in range(blocks)]
     back = [jnp.zeros((FLEN, LANES), f32) for _ in range(blocks)]
-    nt = (((1,), (1,)), ((), ()))
-    sums = []
-    for k in range(LANES // GROUP):
+    per_tile = LANES // GROUP
+    windows_t = [w.astype(f32).T.astype(bf16) for w in windows]
+    acc = jnp.zeros((per_tile, FLEN, 2 * FLEN), f32)
+    for b in range(blocks):
+        stacked = jnp.concatenate(
+            [jnp.where(lane_group == k, cots_r[b], jnp.zeros_like(cots_r[b])) for k in range(per_tile)], axis=0)
+        prods = jnp.dot(stacked, windows_t[b], preferred_element_type=f32)
+        acc = acc + prods.reshape(per_tile, FLEN, 2 * FLEN) * masks_r[b][None]
+    skewed = pltpu.roll(acc.reshape(per_tile * FLEN, 2 * FLEN), 0, 1, stride=1, stride_axis=0)
+    raw_ref[0] = jnp.sum(skewed.reshape(per_tile, FLEN, 2 * FLEN), axis=1)
+    for k in range(per_tile):
         prow = jnp.broadcast_to(fp_ref[k:k + 1, :], (FLEN, 2 * FLEN))
         taps = pltpu.roll(prow, 0, 1, stride=1, stride_axis=0).astype(bf16)
         qrow = jnp.broadcast_to(fq_ref[k:k + 1, :], (2 * FLEN, 2 * FLEN))
         taps_t = pltpu.roll(qrow, FLEN, 1, stride=1, stride_axis=0)[:, :FLEN].astype(bf16)
         in_group = lane_group == k
         group_cots = [jnp.where(in_group, c, jnp.zeros_like(c)) for c in cots]
-        group_cots_r = [jnp.where(in_group, c, jnp.zeros_like(c)) for c in cots_r]
-        acc = jnp.zeros((FLEN, 2 * FLEN), f32)
         for b in range(blocks):
             window = jnp.where(in_group, windows[b], jnp.zeros_like(windows[b]))
             mixed[b] = mixed[b] + jnp.dot(taps * masks[b], window, preferred_element_type=f32)
-            prods = lax.dot_general(group_cots_r[b], windows[b], nt, preferred_element_type=f32)
-            acc = acc + prods * masks_r[b]
         for b in range(blocks + 1):
             spread = jnp.dot(taps_t * masks_t[b], group_cots[b], preferred_element_type=f32)
             if b < blocks:
                 back[b] = back[b] + spread[FLEN:]
             if b > 0:
                 back[b - 1] = back[b - 1] + spread[:FLEN]
-        skewed = pltpu.roll(acc, 0, 1, stride=1, stride_axis=0)
-        sums.append(jnp.sum(skewed, axis=0, keepdims=True))
-    raw_ref[0] = jnp.concatenate(sums, axis=0)
     mixed_all = jnp.concatenate(mixed, axis=0)
     back_all = jnp.concatenate(back, axis=0)
     mo_ref[...] = (query * mixed_all).astype(bf16)
@@ -144,6 +145,8 @@
     fp, fq = filter_rows(filters)
     mixed_out, grad_query, grad_key, grad_value, cols = grouped_conv(
         q2, k2, v2, g2, prev_tail, next_head, fp, fq, mask, mask_t)
+    half_turn = jnp.arange(cols.shape[1]) % 2 == 1
+    cols = jnp.where(half_turn[None, :, None], jnp.roll(cols, FLEN, axis=2), cols)
     local_raw = cols.reshape(-1, 2 * FLEN)[:, 2 * FLEN - 1:FLEN - 1:-1]
     summed = doubling_sum(doubling_sum(local_raw, "dp"), "ctx")
     squares = doubling_sum(jnp.sum(summed * summed), "tensor")

time: 93.2 us -> 94.5 us (1.014)
  Pallas kernels: 23 us -> 24.4 us
    pallas_call x1, Pallas kernels: 23 us -> 24.4 us  [grouped_conv(): pl.pallas_call(conv_kernel, grid=(tiles,), in_specs=[tok, tok, tok, tok,...]
    unnamed x12 -> x14, local copies, waits for them, and re-layouts: 2.18 us -> 1.49 us
where the time goes in v5:
time: 94.5 us; the launch traced here: 93.6 us
  waiting for transfers between devices  29.7 us (31%)
  starting transfers between devices  25.7 us (27%)
  Pallas kernels  24.4 us (26%)
  other arithmetic  6.3 us (7%)
  local copies, waits for them, and re-layouts  4.74 us (5%)
  between operations  2.77 us (3%)
    pallas_call x1, Pallas kernels, grouped_conv(): pl.pallas_call(conv_kernel, grid=(tiles,), in_specs=[tok, tok, tok, tok,...  24.4 us
    ppermute x8, waiting for transfers between devices, doubling_sum(): partner = lax.ppermute(value, axis, [(i, i ^ step) for i in range(count)])  21.6 us
    ppermute x8, starting transfers between devices, doubling_sum(): partner = lax.ppermute(value, axis, [(i, i ^ step) for i in range(count)])  19.8 us
    ppermute x2, waiting for transfers between devices, passed_along(): lax.ppermute(value, axis, [(source, source + steps) for source in range(i...  8.06 us
    ppermute x2, starting transfers between devices, passed_along(): lax.ppermute(value, axis, [(source, source + steps) for source in range(i...  5.87 us
  transfers between devices with their start and end apart: 10, of which 10 were waited for; matrix products, arithmetic and copies ran while one was open for 6% of the time, Pallas kernels for 0%

profile of v5, /device:TPU:32, one launch (start us, length us, event | category | flops | bytes accessed | tf_op | source)
XLA Modules:
  0.0 93.6 jit_solution(14234186322021422265)
XLA Ops:
  0.6 0.0 copy-start
  0.6 1.4 %fusion = bf16[128,2048]{1,0:T(8,128)(2,1)S(1)} fusion(bf16[1,256,2048]{2,1,0:T(8,128)(2,1)} %param.8, bf16[1,256,2048]{2,1,0:T(8,128)(2,1)} %param.7), kind=kLoop, calls=%fused_computation.2 | loop fusion | flops 1048576 | bytes 1572864 | tf_op jit(solution)/shard_map/convert_element_type | solution.py:140
  2.1 3.8 %collective-permute-start = (bf16[128,2048]{1,0:T(8,128)(2,1)S(1)}, bf16[128,2048]{1,0:T(8,128)(2,1)S(1)}, u32[]{:S(2)}, u32[]{:S(2)}) collective-permute-start(bf16[128,2048]{1,0:T(8,128)(2,1)S(1)} %fusion), channel_id=1, source_target_pairs={{0,4},{4,8},{8,12},{12,16},{16,20},{20,24},{24,28},{28,32},{32,36}... | collective-permute-start | bytes 1572872 | tf_op jit(solution)/shard_map/ppermute | solution.py:19
  5.9 0.0 copy-done
  5.9 1.2 %fusion.1 = bf16[128,2048]{1,0:T(8,128)(2,1)S(1)} fusion(bf16[1,256,2048]{2,1,0:T(8,128)(2,1)S(1)} %copy-done, bf16[1,256,2048]{2,1,0:T(8,128)(2,1)} %param.9), kind=kLoop, calls=%fused_computation.3 | loop fusion | flops 1048576 | bytes 1572864 | tf_op jit(solution)/shard_map/convert_element_type | solution.py:141
  7.1 2.0 %collective-permute-start.1 = (bf16[128,2048]{1,0:T(8,128)(2,1)S(1)}, bf16[128,2048]{1,0:T(8,128)(2,1)S(1)}, u32[]{:S(2)}, u32[]{:S(2)}) collective-permute-start(bf16[128,2048]{1,0:T(8,128)(2,1)S(1)} %fusion.1), channel_id=1, source_target_pairs={{4,0},{8,4},{12,8},{16,12},{20,16},{24,20},{28,24},{32,28},{36,32}... | collective-permute-start | bytes 1572872 | tf_op jit(solution)/shard_map/ppermute | solution.py:19
  9.2 0.1 fusion.7
  9.3 0.1 iota_add_fusion.1
  9.4 0.0 copy-start.6
  9.4 0.7 copy-done.6
  10.1 0.1 copy.13
  10.1 0.1 reduce-window.8
  10.2 0.1 reduce
  10.4 0.1 iota_add_fusion
  10.4 0.1 select_reduce_fusion
  10.5 0.1 and_convert_fusion.1.m_ref
  10.7 0.0 copy-start.1
  10.7 0.0 copy-start.5
  10.7 1.3 %rev.10.mr_ref = bf16[2,128,256]{2,1,0:T(8,128)(2,1)} reverse(bf16[2,128,256]{2,1,0:T(8,128)(2,1)S(1)} %slice.38), dimensions={1} | reverse | bytes 262144 | tf_op jit(solution)/shard_map/rev | solution.py:91
  12.0 0.0 copy-done.1
  12.0 0.0 copy-done.5
  12.0 0.1 rev.9
  12.1 0.7 concatenate.11.fq_ref
  12.8 0.1 pad.5.clone
  12.9 0.8 maximum_maximum_fusion.fp_ref
  13.6 0.9 and_convert_fusion.mt_ref
  14.5 3.1 %collective-permute-done.prev_ref = bf16[128,2048]{1,0:T(8,128)(2,1)S(1)} collective-permute-done((bf16[128,2048]{1,0:T(8,128)(2,1)S(1)}, bf16[128,2048]{1,0:T(8,128)(2,1)S(1)}, u32[]{:S(2)}, u32[]{:S(2)}) %collective-permute-start) | collective-permute-done | bytes 524320 | tf_op jit(solution)/shard_map/ppermute | solution.py:19
  17.6 0.0 copy-start.2
  17.6 4.9 %collective-permute-done.1.next_ref = bf16[128,2048]{1,0:T(8,128)(2,1)S(1)} collective-permute-done((bf16[128,2048]{1,0:T(8,128)(2,1)S(1)}, bf16[128,2048]{1,0:T(8,128)(2,1)S(1)}, u32[]{:S(2)}, u32[]{:S(2)}) %collective-permute-start.1) | collective-permute-done | bytes 524320 | tf_op jit(solution)/shard_map/ppermute | solution.py:19
  22.5 0.0 copy-start.3
  22.5 0.0 copy-done.2
  22.5 0.8 copy-done.3
  23.3 24.4 %shard_map.101 = (bf16[256,2048]{1,0:T(8,128)(2,1)}, bf16[256,2048]{1,0:T(8,128)(2,1)}, bf16[256,2048]{1,0:T(8,128)(2,1)}, bf16[256,2048]{1,0:T(8,128)(2,1)}, f32[16,8,256]{2,1,0:T(8,128)}) custom-call(bf16[256,2048]{1,0:T(8,128)(2,1)} %bitcast.18, bf16[256,2048]{1,0:T(8,128)(2,1)} %bitcast.19, bf16[256,2048]{1,0:T(8,128)(2,1)} %bitcast.20, ...), custom_call_target="tpu_custom_call" | custom-call | tf_op jit(solution)/shard_map/pallas_call | solution.py:103
  47.7 0.0 copy-start.4
  47.7 0.9 fusion.10
  48.6 0.0 copy-done.4
  48.7 0.1 fusion.2
  48.8 0.1 rev.11
  48.8 0.1 collective-permute-start.2
  48.9 1.2 %collective-permute-done.2 = f32[128,128]{1,0:T(8,128)S(1)} collective-permute-done((f32[128,128]{1,0:T(8,128)S(1)}, f32[128,128]{1,0:T(8,128)S(1)}, u32[]{:S(2)}, u32[]{:S(2)}) %collective-permute-start.2) | collective-permute-done | bytes 65568 | tf_op jit(solution)/shard_map/ppermute | solution.py:26
  50.2 0.2 collective-permute-start.3
  50.4 4.2 %collective-permute-done.3 = f32[128,128]{1,0:T(8,128)S(1)} collective-permute-done((f32[128,128]{1,0:T(8,128)S(1)}, f32[128,128]{1,0:T(8,128)S(1)}, u32[]{:S(2)}, u32[]{:S(2)}) %collective-permute-start.3) | collective-permute-done | bytes 65568 | tf_op jit(solution)/shard_map/ppermute | solution.py:26
  54.5 5.6 %collective-permute-start.4 = (f32[128,128]{1,0:T(8,128)S(1)}, f32[128,128]{1,0:T(8,128)S(1)}, u32[]{:S(2)}, u32[]{:S(2)}) collective-permute-start(f32[128,128]{1,0:T(8,128)S(1)} %add.122), channel_id=1, source_target_pairs={{0,8},{4,12},{8,0},{12,4},{16,24},{20,28},{24,16},{28,20},{32,40},... | collective-permute-start | bytes 196616 | tf_op jit(solution)/shard_map/ppermute | solution.py:26
  60.1 2.2 %collective-permute-done.4 = f32[128,128]{1,0:T(8,128)S(1)} collective-permute-done((f32[128,128]{1,0:T(8,128)S(1)}, f32[128,128]{1,0:T(8,128)S(1)}, u32[]{:S(2)}, u32[]{:S(2)}) %collective-permute-start.4) | collective-permute-done | bytes 65568 | tf_op jit(solution)/shard_map/ppermute | solution.py:26
  62.4 2.8 %collective-permute-start.5 = (f32[128,128]{1,0:T(8,128)S(1)}, f32[128,128]{1,0:T(8,128)S(1)}, u32[]{:S(2)}, u32[]{:S(2)}) collective-permute-start(f32[128,128]{1,0:T(8,128)S(1)} %add.123), channel_id=1, source_target_pairs={{0,16},{4,20},{8,24},{12,28},{16,0},{20,4},{24,8},{28,12},{32,48},... | collective-permute-start | bytes 196616 | tf_op jit(solution)/shard_map/ppermute | solution.py:26
  65.2 6.1 %collective-permute-done.5 = f32[128,128]{1,0:T(8,128)S(1)} collective-permute-done((f32[128,128]{1,0:T(8,128)S(1)}, f32[128,128]{1,0:T(8,128)S(1)}, u32[]{:S(2)}, u32[]{:S(2)}) %collective-permute-start.5) | collective-permute-done | bytes 65568 | tf_op jit(solution)/shard_map/ppermute | solution.py:26
  71.4 1.7 %collective-permute-start.6 = (f32[128,128]{1,0:T(8,128)S(1)}, f32[128,128]{1,0:T(8,128)S(1)}, u32[]{:S(2)}, u32[]{:S(2)}) collective-permute-start(f32[128,128]{1,0:T(8,128)S(1)} %add.124), channel_id=1, source_target_pairs={{0,32},{4,36},{8,40},{12,44},{16,48},{20,52},{24,56},{28,60},{32,0... | collective-permute-start | bytes 196616 | tf_op jit(solution)/shard_map/ppermute | solution.py:26
  73.0 2.7 %collective-permute-done.6 = f32[128,128]{1,0:T(8,128)S(1)} collective-permute-done((f32[128,128]{1,0:T(8,128)S(1)}, f32[128,128]{1,0:T(8,128)S(1)}, u32[]{:S(2)}, u32[]{:S(2)}) %collective-permute-start.6) | collective-permute-done | bytes 65568 | tf_op jit(solution)/shard_map/ppermute | solution.py:26
  75.7 3.6 %collective-permute-start.7 = (f32[128,128]{1,0:T(8,128)S(1)}, f32[128,128]{1,0:T(8,128)S(1)}, u32[]{:S(2)}, u32[]{:S(2)}) collective-permute-start(f32[128,128]{1,0:T(8,128)S(1)} %add.125), channel_id=1, source_target_pairs={{0,64},{4,68},{8,72},{12,76},{16,80},{20,84},{24,88},{28,92},{32,9... | collective-permute-start | bytes 196616 | tf_op jit(solution)/shard_map/ppermute | solution.py:26
  79.3 2.2 %collective-permute-done.7 = f32[128,128]{1,0:T(8,128)S(1)} collective-permute-done((f32[128,128]{1,0:T(8,128)S(1)}, f32[128,128]{1,0:T(8,128)S(1)}, u32[]{:S(2)}, u32[]{:S(2)}) %collective-permute-start.7) | collective-permute-done | bytes 65568 | tf_op jit(solution)/shard_map/ppermute | solution.py:26
  81.6 0.6 multiply_reduce_fusion
  82.2 1.5 %collective-permute-start.8 = (f32[]{:T(128)}, f32[]{:T(128)}, u32[]{:S(2)}, u32[]{:S(2)}) collective-permute-start(f32[]{:T(128)} %get-tuple-element.15), channel_id=1, source_target_pairs={{0,1},{1,0},{2,3},{3,2},{4,5},{5,4},{6,7},{7,6},{8,9},{9,8},{10,11... | collective-permute-start | bytes 20 | tf_op jit(solution)/shard_map/ppermute | solution.py:26
  83.7 2.2 %collective-permute-done.8 = f32[]{:T(128)} collective-permute-done((f32[]{:T(128)}, f32[]{:T(128)}, u32[]{:S(2)}, u32[]{:S(2)}) %collective-permute-start.8) | collective-permute-done | bytes 36 | tf_op jit(solution)/shard_map/ppermute | solution.py:26
  87.1 4.4 %collective-permute-start.9 = (f32[]{:T(128)}, f32[]{:T(128)}, u32[]{:S(2)}, u32[]{:S(2)}) collective-permute-start(f32[]{:T(128)} %add.127), channel_id=1, source_target_pairs={{0,2},{1,3},{2,0},{3,1},{4,6},{5,7},{6,4},{7,5},{8,10},{9,11},{10,... | collective-permute-start | bytes 20 | tf_op jit(solution)/shard_map/ppermute | solution.py:26
  91.5 0.7 collective-permute-done.9
  92.9 0.6 broadcast_multiply_fusion
  (14 shorter events, 0.1 us)
Async XLA Ops:
  0.6 5.3 %copy-start = (bf16[1,256,2048]{2,1,0:T(8,128)(2,1)S(1)}, bf16[1,256,2048]{2,1,0:T(8,128)(2,1)}, u32[]{:S(2)}) copy-start(bf16[1,256,2048]{2,1,0:T(8,128)(2,1)} %param.6) | copy-start | bytes 3145732
  2.1 15.6 %collective-permute-start = (bf16[128,2048]{1,0:T(8,128)(2,1)S(1)}, bf16[128,2048]{1,0:T(8,128)(2,1)S(1)}, u32[]{:S(2)}, u32[]{:S(2)}) collective-permute-start(bf16[128,2048]{1,0:T(8,128)(2,1)S(1)} %fusion), channel_id=1, source_target_pairs={{0,4},{4,8},{8,12},{12,16},{16,20},{20,24},{24,28},{28,32},{32,36}... | collective-permute-start | bytes 1572872 | tf_op jit(solution)/shard_map/ppermute | solution.py:19
  7.1 15.5 %collective-permute-start.1 = (bf16[128,2048]{1,0:T(8,128)(2,1)S(1)}, bf16[128,2048]{1,0:T(8,128)(2,1)S(1)}, u32[]{:S(2)}, u32[]{:S(2)}) collective-permute-start(bf16[128,2048]{1,0:T(8,128)(2,1)S(1)} %fusion.1), channel_id=1, source_target_pairs={{4,0},{8,4},{12,8},{16,12},{20,16},{24,20},{28,24},{32,28},{36,32}... | collective-permute-start | bytes 1572872 | tf_op jit(solution)/shard_map/ppermute | solution.py:19
  9.4 0.7 copy-start.6
  10.7 1.4 %copy-start.1 = (bf16[3,128,256]{2,1,0:T(8,128)(2,1)}, bf16[3,128,256]{2,1,0:T(8,128)(2,1)S(1)}, u32[]{:S(2)}) copy-start(bf16[3,128,256]{2,1,0:T(8,128)(2,1)S(1)} %and_convert_fusion.1.m_ref) | copy-start | bytes 589828
  10.7 1.3 %copy-start.5 = (bf16[128,128]{1,0:T(8,128)(2,1)S(1)}, bf16[128,128]{1,0:T(8,128)(2,1)}, u32[]{:S(2)}) copy-start(bf16[128,128]{1,0:T(8,128)(2,1)} %param.11) | copy-start | bytes 98308
  17.6 4.9 %copy-start.2 = (bf16[128,2048]{1,0:T(8,128)(2,1)}, bf16[128,2048]{1,0:T(8,128)(2,1)S(1)}, u32[]{:S(2)}) copy-start(bf16[128,2048]{1,0:T(8,128)(2,1)S(1)} %collective-permute-done.prev_ref) | copy-start | bytes 1572868
  22.5 0.8 copy-start.3
  47.7 1.0 %copy-start.4 = (f32[16,8,256]{2,1,0:T(8,128)S(1)}, f32[16,8,256]{2,1,0:T(8,128)}, u32[]{:S(2)}) copy-start(f32[16,8,256]{2,1,0:T(8,128)} %get-tuple-element.14) | copy-start | bytes 393220
  48.8 1.3 %collective-permute-start.2 = (f32[128,128]{1,0:T(8,128)S(1)}, f32[128,128]{1,0:T(8,128)S(1)}, u32[]{:S(2)}, u32[]{:S(2)}) collective-permute-start(f32[128,128]{1,0:T(8,128)S(1)} %rev.11), channel_id=1, source_target_pairs={{0,128},{128,0},{1,129},{129,1},{2,130},{130,2},{3,131},{131,3},{4... | collective-permute-start | bytes 196616 | tf_op jit(solution)/shard_map/ppermute | solution.py:26
  50.2 4.4 %collective-permute-start.3 = (f32[128,128]{1,0:T(8,128)S(1)}, f32[128,128]{1,0:T(8,128)S(1)}, u32[]{:S(2)}, u32[]{:S(2)}) collective-permute-start(f32[128,128]{1,0:T(8,128)S(1)} %add.121), channel_id=1, source_target_pairs={{0,4},{4,0},{8,12},{12,8},{16,20},{20,16},{24,28},{28,24},{32,36},... | collective-permute-start | bytes 196616 | tf_op jit(solution)/shard_map/ppermute | solution.py:26
  54.5 7.8 %collective-permute-start.4 = (f32[128,128]{1,0:T(8,128)S(1)}, f32[128,128]{1,0:T(8,128)S(1)}, u32[]{:S(2)}, u32[]{:S(2)}) collective-permute-start(f32[128,128]{1,0:T(8,128)S(1)} %add.122), channel_id=1, source_target_pairs={{0,8},{4,12},{8,0},{12,4},{16,24},{20,28},{24,16},{28,20},{32,40},... | collective-permute-start | bytes 196616 | tf_op jit(solution)/shard_map/ppermute | solution.py:26
  62.4 9.0 %collective-permute-start.5 = (f32[128,128]{1,0:T(8,128)S(1)}, f32[128,128]{1,0:T(8,128)S(1)}, u32[]{:S(2)}, u32[]{:S(2)}) collective-permute-start(f32[128,128]{1,0:T(8,128)S(1)} %add.123), channel_id=1, source_target_pairs={{0,16},{4,20},{8,24},{12,28},{16,0},{20,4},{24,8},{28,12},{32,48},... | collective-permute-start | bytes 196616 | tf_op jit(solution)/shard_map/ppermute | solution.py:26
  71.4 4.4 %collective-permute-start.6 = (f32[128,128]{1,0:T(8,128)S(1)}, f32[128,128]{1,0:T(8,128)S(1)}, u32[]{:S(2)}, u32[]{:S(2)}) collective-permute-start(f32[128,128]{1,0:T(8,128)S(1)} %add.124), channel_id=1, source_target_pairs={{0,32},{4,36},{8,40},{12,44},{16,48},{20,52},{24,56},{28,60},{32,0... | collective-permute-start | bytes 196616 | tf_op jit(solution)/shard_map/ppermute | solution.py:26
  75.7 5.9 %collective-permute-start.7 = (f32[128,128]{1,0:T(8,128)S(1)}, f32[128,128]{1,0:T(8,128)S(1)}, u32[]{:S(2)}, u32[]{:S(2)}) collective-permute-start(f32[128,128]{1,0:T(8,128)S(1)} %add.125), channel_id=1, source_target_pairs={{0,64},{4,68},{8,72},{12,76},{16,80},{20,84},{24,88},{28,92},{32,9... | collective-permute-start | bytes 196616 | tf_op jit(solution)/shard_map/ppermute | solution.py:26
  82.2 3.7 %collective-permute-start.8 = (f32[]{:T(128)}, f32[]{:T(128)}, u32[]{:S(2)}, u32[]{:S(2)}) collective-permute-start(f32[]{:T(128)} %get-tuple-element.15), channel_id=1, source_target_pairs={{0,1},{1,0},{2,3},{3,2},{4,5},{5,4},{6,7},{7,6},{8,9},{9,8},{10,11... | collective-permute-start | bytes 20 | tf_op jit(solution)/shard_map/ppermute | solution.py:26
  87.1 5.1 %collective-permute-start.9 = (f32[]{:T(128)}, f32[]{:T(128)}, u32[]{:S(2)}, u32[]{:S(2)}) collective-permute-start(f32[]{:T(128)} %add.127), channel_id=1, source_target_pairs={{0,2},{1,3},{2,0},{3,1},{4,6},{5,7},{6,4},{7,5},{8,10},{9,11},{10,... | collective-permute-start | bytes 20 | tf_op jit(solution)/shard_map/ppermute | solution.py:26

commit v6 on v2

--- a/solution.py
+++ b/solution.py
@@ -52,34 +52,36 @@
             + lax.broadcasted_iota(jnp.int32, (FLEN, FLEN), 1) == FLEN - 1).astype(bf16)
     cots_r = [jnp.dot(flip, cots[b], preferred_element_type=f32).astype(bf16) for b in range(blocks)]
     mixed = [jnp.zeros((FLEN, LANES), f32) for _ in range(blocks)]
-    back = [jnp.zeros((FLEN, LANES), f32) for _ in range(blocks)]
+    cots_t = [c.astype(f32).T.astype(bf16) for c in cots]
+    row_group = lax.broadcasted_iota(jnp.int32, (LANES, 1), 0) // GROUP
+    own_t = [jnp.zeros((LANES, FLEN), f32) for _ in range(blocks)]
+    spill_t = [jnp.zeros((LANES, FLEN), f32) for _ in range(blocks)]
     nt = (((1,), (1,)), ((), ()))
     sums = []
     for k in range(LANES // GROUP):
         prow = jnp.broadcast_to(fp_ref[k:k + 1, :], (FLEN, 2 * FLEN))
         taps = pltpu.roll(prow, 0, 1, stride=1, stride_axis=0).astype(bf16)
-        qrow = jnp.broadcast_to(fq_ref[k:k + 1, :], (2 * FLEN, 2 * FLEN))
-        taps_t = pltpu.roll(qrow, FLEN, 1, stride=1, stride_axis=0)[:, :FLEN].astype(bf16)
         in_group = lane_group == k
-        group_cots = [jnp.where(in_group, c, jnp.zeros_like(c)) for c in cots]
-        group_cots_r = [jnp.where(in_group, c, jnp.zeros_like(c)) for c in cots_r]
+        in_rows = row_group == k
         acc = jnp.zeros((FLEN, 2 * FLEN), f32)
-        for b in range(blocks):
-            window = jnp.where(in_group, windows[b], jnp.zeros_like(windows[b]))
-            mixed[b] = mixed[b] + jnp.dot(taps * masks[b], window, preferred_element_type=f32)
-            prods = lax.dot_general(group_cots_r[b], windows[b], nt, preferred_element_type=f32)
-            acc = acc + prods * masks_r[b]
         for b in range(blocks + 1):
-            spread = jnp.dot(taps_t * masks_t[b], group_cots[b], preferred_element_type=f32)
+            group_cot_t = jnp.where(in_rows, cots_t[b], jnp.zeros_like(cots_t[b]))
             if b < blocks:
-                back[b] = back[b] + spread[FLEN:]
+                operator = taps * masks[b]
+                window = jnp.where(in_group, windows[b], jnp.zeros_like(windows[b]))
+                mixed[b] = mixed[b] + jnp.dot(operator, window, preferred_element_type=f32)
+                own_t[b] = own_t[b] + jnp.dot(group_cot_t, operator[:, FLEN:], preferred_element_type=f32)
+                group_cot = jnp.where(in_group, cots_r[b], jnp.zeros_like(cots_r[b]))
+                prods = lax.dot_general(group_cot, windows[b], nt, preferred_element_type=f32)
+                acc = acc + prods * masks_r[b]
             if b > 0:
-                back[b - 1] = back[b - 1] + spread[:FLEN]
+                lead = taps[:, :FLEN] * masks[b][:, :FLEN]
+                spill_t[b - 1] = spill_t[b - 1] + jnp.dot(group_cot_t, lead, preferred_element_type=f32)
         skewed = pltpu.roll(acc, 0, 1, stride=1, stride_axis=0)
         sums.append(jnp.sum(skewed, axis=0, keepdims=True))
     raw_ref[0] = jnp.concatenate(sums, axis=0)
     mixed_all = jnp.concatenate(mixed, axis=0)
-    back_all = jnp.concatenate(back, axis=0)
+    back_all = jnp.concatenate([(own_t[b] + spill_t[b]).T for b in range(blocks)], axis=0)
     mo_ref[...] = (query * mixed_all).astype(bf16)
     gq_ref[...] = (upstream * mixed_all).astype(bf16)
     gk_ref[...] = (back_all * values).astype(bf16)

time: 93.2 us -> 93.1 us (level)
  no operation moved by 1% of the time
where the time goes in v6:
time: 93.1 us; the launch traced here: 92 us
  waiting for transfers between devices  29.2 us (31%)
  starting transfers between devices  25.7 us (28%)
  Pallas kernels  22.8 us (24%)
  other arithmetic  6.22 us (7%)
  local copies, waits for them, and re-layouts  5.35 us (6%)
  between operations  2.63 us (3%)
    pallas_call x1, Pallas kernels, grouped_conv(): pl.pallas_call(conv_kernel, grid=(tiles,), in_specs=[tok, tok, tok, tok,...  22.8 us
    ppermute x8, waiting for transfers between devices, doubling_sum(): partner = lax.ppermute(value, axis, [(i, i ^ step) for i in range(count)])  21.9 us
    ppermute x8, starting transfers between devices, doubling_sum(): partner = lax.ppermute(value, axis, [(i, i ^ step) for i in range(count)])  19.8 us
    ppermute x2, waiting for transfers between devices, passed_along(): lax.ppermute(value, axis, [(source, source + steps) for source in range(i...  7.33 us
    ppermute x2, starting transfers between devices, passed_along(): lax.ppermute(value, axis, [(source, source + steps) for source in range(i...  5.87 us
    unnamed x12, local copies, waits for them, and re-layouts  2.18 us
  transfers between devices with their start and end apart: 10, of which 10 were waited for; matrix products, arithmetic and copies ran while one was open for 6% of the time, Pallas kernels for 0%

profile of v6, /device:TPU:32, one launch (start us, length us, event | category | flops | bytes accessed | tf_op | source)
XLA Modules:
  0.0 92.0 jit_solution(9291498271889287216)
XLA Ops:
  0.6 0.0 copy-start
  0.6 1.4 %fusion = bf16[128,2048]{1,0:T(8,128)(2,1)S(1)} fusion(bf16[1,256,2048]{2,1,0:T(8,128)(2,1)} %param.8, bf16[1,256,2048]{2,1,0:T(8,128)(2,1)} %param.7), kind=kLoop, calls=%fused_computation.2 | loop fusion | flops 1048576 | bytes 1572864 | tf_op jit(solution)/shard_map/convert_element_type | solution.py:141
  2.1 3.8 %collective-permute-start = (bf16[128,2048]{1,0:T(8,128)(2,1)S(1)}, bf16[128,2048]{1,0:T(8,128)(2,1)S(1)}, u32[]{:S(2)}, u32[]{:S(2)}) collective-permute-start(bf16[128,2048]{1,0:T(8,128)(2,1)S(1)} %fusion), channel_id=1, source_target_pairs={{0,4},{4,8},{8,12},{12,16},{16,20},{20,24},{24,28},{28,32},{32,36}... | collective-permute-start | bytes 1572872 | tf_op jit(solution)/shard_map/ppermute | solution.py:19
  5.9 0.0 copy-done
  5.9 1.2 %fusion.1 = bf16[128,2048]{1,0:T(8,128)(2,1)S(1)} fusion(bf16[1,256,2048]{2,1,0:T(8,128)(2,1)S(1)} %copy-done, bf16[1,256,2048]{2,1,0:T(8,128)(2,1)} %param.9), kind=kLoop, calls=%fused_computation.3 | loop fusion | flops 1048576 | bytes 1572864 | tf_op jit(solution)/shard_map/convert_element_type | solution.py:142
  7.1 2.0 %collective-permute-start.1 = (bf16[128,2048]{1,0:T(8,128)(2,1)S(1)}, bf16[128,2048]{1,0:T(8,128)(2,1)S(1)}, u32[]{:S(2)}, u32[]{:S(2)}) collective-permute-start(bf16[128,2048]{1,0:T(8,128)(2,1)S(1)} %fusion.1), channel_id=1, source_target_pairs={{4,0},{8,4},{12,8},{16,12},{20,16},{24,20},{28,24},{32,28},{36,32}... | collective-permute-start | bytes 1572872 | tf_op jit(solution)/shard_map/ppermute | solution.py:19
  9.2 0.1 iota_add_fusion.1
  9.2 0.1 iota_add_fusion
  9.3 0.1 fusion.6
  9.4 0.0 copy-start.5
  9.4 0.6 copy-done.5
  10.1 0.1 copy.13
  10.2 0.1 reduce-window.8
  10.3 0.1 reduce
  10.4 0.1 select_reduce_fusion
  10.5 0.1 and_convert_fusion.1.m_ref
  10.6 0.0 copy-start.1
  10.6 0.0 copy-start.4
  10.7 0.7 copy-done.4
  11.4 0.1 rev.9
  11.5 0.7 concatenate.7.fq_ref
  12.2 0.1 pad.3.clone
  12.3 0.0 copy-done.1
  12.3 1.3 %rev.10.mr_ref = bf16[2,128,256]{2,1,0:T(8,128)(2,1)} reverse(bf16[2,128,256]{2,1,0:T(8,128)(2,1)S(1)} %slice.28), dimensions={1} | reverse | bytes 262144 | tf_op jit(solution)/shard_map/rev | solution.py:92
  13.6 0.7 maximum_maximum_fusion.fp_ref
  14.3 0.9 and_convert_fusion.mt_ref
  15.2 2.4 %collective-permute-done.prev_ref = bf16[128,2048]{1,0:T(8,128)(2,1)S(1)} collective-permute-done((bf16[128,2048]{1,0:T(8,128)(2,1)S(1)}, bf16[128,2048]{1,0:T(8,128)(2,1)S(1)}, u32[]{:S(2)}, u32[]{:S(2)}) %collective-permute-start) | collective-permute-done | bytes 524320 | tf_op jit(solution)/shard_map/ppermute | solution.py:19
  17.6 0.0 copy-start.2
  17.6 4.9 %collective-permute-done.1.next_ref = bf16[128,2048]{1,0:T(8,128)(2,1)S(1)} collective-permute-done((bf16[128,2048]{1,0:T(8,128)(2,1)S(1)}, bf16[128,2048]{1,0:T(8,128)(2,1)S(1)}, u32[]{:S(2)}, u32[]{:S(2)}) %collective-permute-start.1) | collective-permute-done | bytes 524320 | tf_op jit(solution)/shard_map/ppermute | solution.py:19
  22.5 0.0 copy-start.3
  22.5 0.0 copy-done.2
  22.5 0.8 copy-done.3
  23.3 22.8 %shard_map.101 = (bf16[256,2048]{1,0:T(8,128)(2,1)}, bf16[256,2048]{1,0:T(8,128)(2,1)}, bf16[256,2048]{1,0:T(8,128)(2,1)}, bf16[256,2048]{1,0:T(8,128)(2,1)}, f32[16,8,256]{2,1,0:T(8,128)}) custom-call(bf16[256,2048]{1,0:T(8,128)(2,1)} %bitcast.17, bf16[256,2048]{1,0:T(8,128)(2,1)} %bitcast.18, bf16[256,2048]{1,0:T(8,128)(2,1)} %bitcast.19, ...), custom_call_target="tpu_custom_call" | custom-call | tf_op jit(solution)/shard_map/pallas_call | solution.py:104
  46.2 0.8 slice.29
  47.0 0.1 rev.11
  47.1 0.1 collective-permute-start.2
  47.2 1.2 %collective-permute-done.2 = f32[128,128]{1,0:T(8,128)S(1)} collective-permute-done((f32[128,128]{1,0:T(8,128)S(1)}, f32[128,128]{1,0:T(8,128)S(1)}, u32[]{:S(2)}, u32[]{:S(2)}) %collective-permute-start.2) | collective-permute-done | bytes 65568 | tf_op jit(solution)/shard_map/ppermute | solution.py:26
  48.4 0.2 collective-permute-start.3
  48.6 4.2 %collective-permute-done.3 = f32[128,128]{1,0:T(8,128)S(1)} collective-permute-done((f32[128,128]{1,0:T(8,128)S(1)}, f32[128,128]{1,0:T(8,128)S(1)}, u32[]{:S(2)}, u32[]{:S(2)}) %collective-permute-start.3) | collective-permute-done | bytes 65568 | tf_op jit(solution)/shard_map/ppermute | solution.py:26
  52.8 5.6 %collective-permute-start.4 = (f32[128,128]{1,0:T(8,128)S(1)}, f32[128,128]{1,0:T(8,128)S(1)}, u32[]{:S(2)}, u32[]{:S(2)}) collective-permute-start(f32[128,128]{1,0:T(8,128)S(1)} %add.111), channel_id=1, source_target_pairs={{0,8},{4,12},{8,0},{12,4},{16,24},{20,28},{24,16},{28,20},{32,40},... | collective-permute-start | bytes 196616 | tf_op jit(solution)/shard_map/ppermute | solution.py:26
  58.4 2.2 %collective-permute-done.4 = f32[128,128]{1,0:T(8,128)S(1)} collective-permute-done((f32[128,128]{1,0:T(8,128)S(1)}, f32[128,128]{1,0:T(8,128)S(1)}, u32[]{:S(2)}, u32[]{:S(2)}) %collective-permute-start.4) | collective-permute-done | bytes 65568 | tf_op jit(solution)/shard_map/ppermute | solution.py:26
  60.6 2.8 %collective-permute-start.5 = (f32[128,128]{1,0:T(8,128)S(1)}, f32[128,128]{1,0:T(8,128)S(1)}, u32[]{:S(2)}, u32[]{:S(2)}) collective-permute-start(f32[128,128]{1,0:T(8,128)S(1)} %add.112), channel_id=1, source_target_pairs={{0,16},{4,20},{8,24},{12,28},{16,0},{20,4},{24,8},{28,12},{32,48},... | collective-permute-start | bytes 196616 | tf_op jit(solution)/shard_map/ppermute | solution.py:26
  63.5 6.2 %collective-permute-done.5 = f32[128,128]{1,0:T(8,128)S(1)} collective-permute-done((f32[128,128]{1,0:T(8,128)S(1)}, f32[128,128]{1,0:T(8,128)S(1)}, u32[]{:S(2)}, u32[]{:S(2)}) %collective-permute-start.5) | collective-permute-done | bytes 65568 | tf_op jit(solution)/shard_map/ppermute | solution.py:26
  69.6 1.7 %collective-permute-start.6 = (f32[128,128]{1,0:T(8,128)S(1)}, f32[128,128]{1,0:T(8,128)S(1)}, u32[]{:S(2)}, u32[]{:S(2)}) collective-permute-start(f32[128,128]{1,0:T(8,128)S(1)} %add.113), channel_id=1, source_target_pairs={{0,32},{4,36},{8,40},{12,44},{16,48},{20,52},{24,56},{28,60},{32,0... | collective-permute-start | bytes 196616 | tf_op jit(solution)/shard_map/ppermute | solution.py:26
  71.3 2.7 %collective-permute-done.6 = f32[128,128]{1,0:T(8,128)S(1)} collective-permute-done((f32[128,128]{1,0:T(8,128)S(1)}, f32[128,128]{1,0:T(8,128)S(1)}, u32[]{:S(2)}, u32[]{:S(2)}) %collective-permute-start.6) | collective-permute-done | bytes 65568 | tf_op jit(solution)/shard_map/ppermute | solution.py:26
  74.0 3.6 %collective-permute-start.7 = (f32[128,128]{1,0:T(8,128)S(1)}, f32[128,128]{1,0:T(8,128)S(1)}, u32[]{:S(2)}, u32[]{:S(2)}) collective-permute-start(f32[128,128]{1,0:T(8,128)S(1)} %add.114), channel_id=1, source_target_pairs={{0,64},{4,68},{8,72},{12,76},{16,80},{20,84},{24,88},{28,92},{32,9... | collective-permute-start | bytes 196616 | tf_op jit(solution)/shard_map/ppermute | solution.py:26
  77.6 2.2 %collective-permute-done.7 = f32[128,128]{1,0:T(8,128)S(1)} collective-permute-done((f32[128,128]{1,0:T(8,128)S(1)}, f32[128,128]{1,0:T(8,128)S(1)}, u32[]{:S(2)}, u32[]{:S(2)}) %collective-permute-start.7) | collective-permute-done | bytes 65568 | tf_op jit(solution)/shard_map/ppermute | solution.py:26
  79.9 0.6 multiply_reduce_fusion
  80.5 1.5 %collective-permute-start.8 = (f32[]{:T(128)}, f32[]{:T(128)}, u32[]{:S(2)}, u32[]{:S(2)}) collective-permute-start(f32[]{:T(128)} %get-tuple-element.15), channel_id=1, source_target_pairs={{0,1},{1,0},{2,3},{3,2},{4,5},{5,4},{6,7},{7,6},{8,9},{9,8},{10,11... | collective-permute-start | bytes 20 | tf_op jit(solution)/shard_map/ppermute | solution.py:26
  82.0 2.3 %collective-permute-done.8 = f32[]{:T(128)} collective-permute-done((f32[]{:T(128)}, f32[]{:T(128)}, u32[]{:S(2)}, u32[]{:S(2)}) %collective-permute-start.8) | collective-permute-done | bytes 36 | tf_op jit(solution)/shard_map/ppermute | solution.py:26
  85.5 4.4 %collective-permute-start.9 = (f32[]{:T(128)}, f32[]{:T(128)}, u32[]{:S(2)}, u32[]{:S(2)}) collective-permute-start(f32[]{:T(128)} %add.116), channel_id=1, source_target_pairs={{0,2},{1,3},{2,0},{3,1},{4,6},{5,7},{6,4},{7,5},{8,10},{9,11},{10,... | collective-permute-start | bytes 20 | tf_op jit(solution)/shard_map/ppermute | solution.py:26
  89.9 0.9 collective-permute-done.9
  91.4 0.6 broadcast_multiply_fusion
  (12 shorter events, 0.1 us)
Async XLA Ops:
  0.6 5.3 %copy-start = (bf16[1,256,2048]{2,1,0:T(8,128)(2,1)S(1)}, bf16[1,256,2048]{2,1,0:T(8,128)(2,1)}, u32[]{:S(2)}) copy-start(bf16[1,256,2048]{2,1,0:T(8,128)(2,1)} %param.6) | copy-start | bytes 3145732
  2.1 15.6 %collective-permute-start = (bf16[128,2048]{1,0:T(8,128)(2,1)S(1)}, bf16[128,2048]{1,0:T(8,128)(2,1)S(1)}, u32[]{:S(2)}, u32[]{:S(2)}) collective-permute-start(bf16[128,2048]{1,0:T(8,128)(2,1)S(1)} %fusion), channel_id=1, source_target_pairs={{0,4},{4,8},{8,12},{12,16},{16,20},{20,24},{24,28},{28,32},{32,36}... | collective-permute-start | bytes 1572872 | tf_op jit(solution)/shard_map/ppermute | solution.py:19
  7.1 15.5 %collective-permute-start.1 = (bf16[128,2048]{1,0:T(8,128)(2,1)S(1)}, bf16[128,2048]{1,0:T(8,128)(2,1)S(1)}, u32[]{:S(2)}, u32[]{:S(2)}) collective-permute-start(bf16[128,2048]{1,0:T(8,128)(2,1)S(1)} %fusion.1), channel_id=1, source_target_pairs={{4,0},{8,4},{12,8},{16,12},{20,16},{24,20},{28,24},{32,28},{36,32}... | collective-permute-start | bytes 1572872 | tf_op jit(solution)/shard_map/ppermute | solution.py:19
  9.4 0.7 copy-start.5
  10.6 1.6 %copy-start.1 = (bf16[3,128,256]{2,1,0:T(8,128)(2,1)}, bf16[3,128,256]{2,1,0:T(8,128)(2,1)S(1)}, u32[]{:S(2)}) copy-start(bf16[3,128,256]{2,1,0:T(8,128)(2,1)S(1)} %and_convert_fusion.1.m_ref) | copy-start | bytes 589828
  10.6 0.8 copy-start.4
  17.6 4.9 %copy-start.2 = (bf16[128,2048]{1,0:T(8,128)(2,1)}, bf16[128,2048]{1,0:T(8,128)(2,1)S(1)}, u32[]{:S(2)}) copy-start(bf16[128,2048]{1,0:T(8,128)(2,1)S(1)} %collective-permute-done.prev_ref) | copy-start | bytes 1572868
  22.5 0.8 copy-start.3
  47.1 1.3 %collective-permute-start.2 = (f32[128,128]{1,0:T(8,128)S(1)}, f32[128,128]{1,0:T(8,128)S(1)}, u32[]{:S(2)}, u32[]{:S(2)}) collective-permute-start(f32[128,128]{1,0:T(8,128)S(1)} %rev.11), channel_id=1, source_target_pairs={{0,128},{128,0},{1,129},{129,1},{2,130},{130,2},{3,131},{131,3},{4... | collective-permute-start | bytes 196616 | tf_op jit(solution)/shard_map/ppermute | solution.py:26
  48.4 4.4 %collective-permute-start.3 = (f32[128,128]{1,0:T(8,128)S(1)}, f32[128,128]{1,0:T(8,128)S(1)}, u32[]{:S(2)}, u32[]{:S(2)}) collective-permute-start(f32[128,128]{1,0:T(8,128)S(1)} %add.110), channel_id=1, source_target_pairs={{0,4},{4,0},{8,12},{12,8},{16,20},{20,16},{24,28},{28,24},{32,36},... | collective-permute-start | bytes 196616 | tf_op jit(solution)/shard_map/ppermute | solution.py:26
  52.8 7.8 %collective-permute-start.4 = (f32[128,128]{1,0:T(8,128)S(1)}, f32[128,128]{1,0:T(8,128)S(1)}, u32[]{:S(2)}, u32[]{:S(2)}) collective-permute-start(f32[128,128]{1,0:T(8,128)S(1)} %add.111), channel_id=1, source_target_pairs={{0,8},{4,12},{8,0},{12,4},{16,24},{20,28},{24,16},{28,20},{32,40},... | collective-permute-start | bytes 196616 | tf_op jit(solution)/shard_map/ppermute | solution.py:26
  60.6 9.0 %collective-permute-start.5 = (f32[128,128]{1,0:T(8,128)S(1)}, f32[128,128]{1,0:T(8,128)S(1)}, u32[]{:S(2)}, u32[]{:S(2)}) collective-permute-start(f32[128,128]{1,0:T(8,128)S(1)} %add.112), channel_id=1, source_target_pairs={{0,16},{4,20},{8,24},{12,28},{16,0},{20,4},{24,8},{28,12},{32,48},... | collective-permute-start | bytes 196616 | tf_op jit(solution)/shard_map/ppermute | solution.py:26
  69.6 4.4 %collective-permute-start.6 = (f32[128,128]{1,0:T(8,128)S(1)}, f32[128,128]{1,0:T(8,128)S(1)}, u32[]{:S(2)}, u32[]{:S(2)}) collective-permute-start(f32[128,128]{1,0:T(8,128)S(1)} %add.113), channel_id=1, source_target_pairs={{0,32},{4,36},{8,40},{12,44},{16,48},{20,52},{24,56},{28,60},{32,0... | collective-permute-start | bytes 196616 | tf_op jit(solution)/shard_map/ppermute | solution.py:26
  74.0 5.9 %collective-permute-start.7 = (f32[128,128]{1,0:T(8,128)S(1)}, f32[128,128]{1,0:T(8,128)S(1)}, u32[]{:S(2)}, u32[]{:S(2)}) collective-permute-start(f32[128,128]{1,0:T(8,128)S(1)} %add.114), channel_id=1, source_target_pairs={{0,64},{4,68},{8,72},{12,76},{16,80},{20,84},{24,88},{28,92},{32,9... | collective-permute-start | bytes 196616 | tf_op jit(solution)/shard_map/ppermute | solution.py:26
  80.5 3.8 %collective-permute-start.8 = (f32[]{:T(128)}, f32[]{:T(128)}, u32[]{:S(2)}, u32[]{:S(2)}) collective-permute-start(f32[]{:T(128)} %get-tuple-element.15), channel_id=1, source_target_pairs={{0,1},{1,0},{2,3},{3,2},{4,5},{5,4},{6,7},{7,6},{8,9},{9,8},{10,11... | collective-permute-start | bytes 20 | tf_op jit(solution)/shard_map/ppermute | solution.py:26
  85.5 5.3 %collective-permute-start.9 = (f32[]{:T(128)}, f32[]{:T(128)}, u32[]{:S(2)}, u32[]{:S(2)}) collective-permute-start(f32[]{:T(128)} %add.116), channel_id=1, source_target_pairs={{0,2},{1,3},{2,0},{3,1},{4,6},{5,7},{6,4},{7,5},{8,10},{9,11},{10,... | collective-permute-start | bytes 20 | tf_op jit(solution)/shard_map/ppermute | solution.py:26

commit v7 on v6

--- a/solution.py
+++ b/solution.py
@@ -51,37 +51,37 @@
     flip = (lax.broadcasted_iota(jnp.int32, (FLEN, FLEN), 0)
             + lax.broadcasted_iota(jnp.int32, (FLEN, FLEN), 1) == FLEN - 1).astype(bf16)
     cots_r = [jnp.dot(flip, cots[b], preferred_element_type=f32).astype(bf16) for b in range(blocks)]
-    mixed = [jnp.zeros((FLEN, LANES), f32) for _ in range(blocks)]
     cots_t = [c.astype(f32).T.astype(bf16) for c in cots]
-    row_group = lax.broadcasted_iota(jnp.int32, (LANES, 1), 0) // GROUP
-    own_t = [jnp.zeros((LANES, FLEN), f32) for _ in range(blocks)]
-    spill_t = [jnp.zeros((LANES, FLEN), f32) for _ in range(blocks)]
+    windows_t = [w.astype(f32).T.astype(bf16) for w in windows]
+    mixed_t = [[] for _ in range(blocks)]
+    own_t = [[] for _ in range(blocks)]
+    spill_t = [[] for _ in range(blocks)]
     nt = (((1,), (1,)), ((), ()))
     sums = []
     for k in range(LANES // GROUP):
         prow = jnp.broadcast_to(fp_ref[k:k + 1, :], (FLEN, 2 * FLEN))
         taps = pltpu.roll(prow, 0, 1, stride=1, stride_axis=0).astype(bf16)
+        rows_k = slice(k * GROUP, (k + 1) * GROUP)
         in_group = lane_group == k
-        in_rows = row_group == k
         acc = jnp.zeros((FLEN, 2 * FLEN), f32)
         for b in range(blocks + 1):
-            group_cot_t = jnp.where(in_rows, cots_t[b], jnp.zeros_like(cots_t[b]))
+            group_cot_t = cots_t[b][rows_k]
             if b < blocks:
                 operator = taps * masks[b]
-                window = jnp.where(in_group, windows[b], jnp.zeros_like(windows[b]))
-                mixed[b] = mixed[b] + jnp.dot(operator, window, preferred_element_type=f32)
-                own_t[b] = own_t[b] + jnp.dot(group_cot_t, operator[:, FLEN:], preferred_element_type=f32)
+                mixed_t[b].append(lax.dot_general(windows_t[b][rows_k], operator, nt, preferred_element_type=f32))
+                own_t[b].append(jnp.dot(group_cot_t, operator[:, FLEN:], preferred_element_type=f32))
                 group_cot = jnp.where(in_group, cots_r[b], jnp.zeros_like(cots_r[b]))
                 prods = lax.dot_general(group_cot, windows[b], nt, preferred_element_type=f32)
                 acc = acc + prods * masks_r[b]
             if b > 0:
                 lead = taps[:, :FLEN] * masks[b][:, :FLEN]
-                spill_t[b - 1] = spill_t[b - 1] + jnp.dot(group_cot_t, lead, preferred_element_type=f32)
+                spill_t[b - 1].append(jnp.dot(group_cot_t, lead, preferred_element_type=f32))
         skewed = pltpu.roll(acc, 0, 1, stride=1, stride_axis=0)
         sums.append(jnp.sum(skewed, axis=0, keepdims=True))
     raw_ref[0] = jnp.concatenate(sums, axis=0)
-    mixed_all = jnp.concatenate(mixed, axis=0)
-    back_all = jnp.concatenate([(own_t[b] + spill_t[b]).T for b in range(blocks)], axis=0)
+    mixed_all = jnp.concatenate([jnp.concatenate(m, axis=0).T for m in mixed_t], axis=0)
+    back_all = jnp.concatenate(
+        [(jnp.concatenate(own_t[b], axis=0) + jnp.concatenate(spill_t[b], axis=0)).T for b in range(blocks)], axis=0)
     mo_ref[...] = (query * mixed_all).astype(bf16)
     gq_ref[...] = (upstream * mixed_all).astype(bf16)
     gk_ref[...] = (back_all * values).astype(bf16)

time: 93.1 us -> 92.7 us (level)
  no operation moved by 1% of the time
where the time goes in v7:
time: 92.7 us; the launch traced here: 91.6 us
  waiting for transfers between devices  29.2 us (31%)
  starting transfers between devices  25.7 us (28%)
  Pallas kernels  22.5 us (24%)
  other arithmetic  6.22 us (7%)
  local copies, waits for them, and re-layouts  5.35 us (6%)
  between operations  2.63 us (3%)
    pallas_call x1, Pallas kernels, grouped_conv(): pl.pallas_call(conv_kernel, grid=(tiles,), in_specs=[tok, tok, tok, tok,...  22.5 us
    ppermute x8, waiting for transfers between devices, doubling_sum(): partner = lax.ppermute(value, axis, [(i, i ^ step) for i in range(count)])  21.9 us
    ppermute x8, starting transfers between devices, doubling_sum(): partner = lax.ppermute(value, axis, [(i, i ^ step) for i in range(count)])  19.8 us
    ppermute x2, waiting for transfers between devices, passed_along(): lax.ppermute(value, axis, [(source, source + steps) for source in range(i...  7.33 us
    ppermute x2, starting transfers between devices, passed_along(): lax.ppermute(value, axis, [(source, source + steps) for source in range(i...  5.87 us
    unnamed x12, local copies, waits for them, and re-layouts  2.18 us
  transfers between devices with their start and end apart: 10, of which 10 were waited for; matrix products, arithmetic and copies ran while one was open for 6% of the time, Pallas kernels for 0%

profile of v7, /device:TPU:32, one launch (start us, length us, event | category | flops | bytes accessed | tf_op | source)
XLA Modules:
  0.0 91.6 jit_solution(12298039150423859675)
XLA Ops:
  0.6 0.0 copy-start
  0.6 1.4 %fusion = bf16[128,2048]{1,0:T(8,128)(2,1)S(1)} fusion(bf16[1,256,2048]{2,1,0:T(8,128)(2,1)} %param.8, bf16[1,256,2048]{2,1,0:T(8,128)(2,1)} %param.7), kind=kLoop, calls=%fused_computation.2 | loop fusion | flops 1048576 | bytes 1572864 | tf_op jit(solution)/shard_map/convert_element_type | solution.py:141
  2.1 3.8 %collective-permute-start = (bf16[128,2048]{1,0:T(8,128)(2,1)S(1)}, bf16[128,2048]{1,0:T(8,128)(2,1)S(1)}, u32[]{:S(2)}, u32[]{:S(2)}) collective-permute-start(bf16[128,2048]{1,0:T(8,128)(2,1)S(1)} %fusion), channel_id=1, source_target_pairs={{0,4},{4,8},{8,12},{12,16},{16,20},{20,24},{24,28},{28,32},{32,36}... | collective-permute-start | bytes 1572872 | tf_op jit(solution)/shard_map/ppermute | solution.py:19
  5.9 0.0 copy-done
  5.9 1.2 %fusion.1 = bf16[128,2048]{1,0:T(8,128)(2,1)S(1)} fusion(bf16[1,256,2048]{2,1,0:T(8,128)(2,1)S(1)} %copy-done, bf16[1,256,2048]{2,1,0:T(8,128)(2,1)} %param.9), kind=kLoop, calls=%fused_computation.3 | loop fusion | flops 1048576 | bytes 1572864 | tf_op jit(solution)/shard_map/convert_element_type | solution.py:142
  7.1 2.0 %collective-permute-start.1 = (bf16[128,2048]{1,0:T(8,128)(2,1)S(1)}, bf16[128,2048]{1,0:T(8,128)(2,1)S(1)}, u32[]{:S(2)}, u32[]{:S(2)}) collective-permute-start(bf16[128,2048]{1,0:T(8,128)(2,1)S(1)} %fusion.1), channel_id=1, source_target_pairs={{4,0},{8,4},{12,8},{16,12},{20,16},{24,20},{28,24},{32,28},{36,32}... | collective-permute-start | bytes 1572872 | tf_op jit(solution)/shard_map/ppermute | solution.py:19
  9.2 0.1 iota_add_fusion.1
  9.2 0.1 iota_add_fusion
  9.3 0.1 fusion.6
  9.4 0.0 copy-start.5
  9.4 0.6 copy-done.5
  10.1 0.1 copy.13
  10.2 0.1 reduce-window.8
  10.3 0.1 reduce
  10.4 0.1 select_reduce_fusion
  10.5 0.1 and_convert_fusion.1.m_ref
  10.6 0.0 copy-start.1
  10.6 0.0 copy-start.4
  10.7 0.7 copy-done.4
  11.4 0.1 rev.9
  11.5 0.7 concatenate.7.fq_ref
  12.2 0.1 pad.3.clone
  12.3 0.0 copy-done.1
  12.3 1.3 %rev.10.mr_ref = bf16[2,128,256]{2,1,0:T(8,128)(2,1)} reverse(bf16[2,128,256]{2,1,0:T(8,128)(2,1)S(1)} %slice.28), dimensions={1} | reverse | bytes 262144 | tf_op jit(solution)/shard_map/rev | solution.py:92
  13.6 0.7 maximum_maximum_fusion.fp_ref
  14.3 0.9 and_convert_fusion.mt_ref
  15.2 2.4 %collective-permute-done.prev_ref = bf16[128,2048]{1,0:T(8,128)(2,1)S(1)} collective-permute-done((bf16[128,2048]{1,0:T(8,128)(2,1)S(1)}, bf16[128,2048]{1,0:T(8,128)(2,1)S(1)}, u32[]{:S(2)}, u32[]{:S(2)}) %collective-permute-start) | collective-permute-done | bytes 524320 | tf_op jit(solution)/shard_map/ppermute | solution.py:19
  17.6 0.0 copy-start.2
  17.6 4.9 %collective-permute-done.1.next_ref = bf16[128,2048]{1,0:T(8,128)(2,1)S(1)} collective-permute-done((bf16[128,2048]{1,0:T(8,128)(2,1)S(1)}, bf16[128,2048]{1,0:T(8,128)(2,1)S(1)}, u32[]{:S(2)}, u32[]{:S(2)}) %collective-permute-start.1) | collective-permute-done | bytes 524320 | tf_op jit(solution)/shard_map/ppermute | solution.py:19
  22.5 0.0 copy-start.3
  22.5 0.0 copy-done.2
  22.5 0.8 copy-done.3
  23.3 22.5 %shard_map.101 = (bf16[256,2048]{1,0:T(8,128)(2,1)}, bf16[256,2048]{1,0:T(8,128)(2,1)}, bf16[256,2048]{1,0:T(8,128)(2,1)}, bf16[256,2048]{1,0:T(8,128)(2,1)}, f32[16,8,256]{2,1,0:T(8,128)}) custom-call(bf16[256,2048]{1,0:T(8,128)(2,1)} %bitcast.17, bf16[256,2048]{1,0:T(8,128)(2,1)} %bitcast.18, bf16[256,2048]{1,0:T(8,128)(2,1)} %bitcast.19, ...), custom_call_target="tpu_custom_call" | custom-call | tf_op jit(solution)/shard_map/pallas_call | solution.py:104
  45.8 0.8 slice.29
  46.7 0.1 rev.11
  46.7 0.1 collective-permute-start.2
  46.8 1.2 %collective-permute-done.2 = f32[128,128]{1,0:T(8,128)S(1)} collective-permute-done((f32[128,128]{1,0:T(8,128)S(1)}, f32[128,128]{1,0:T(8,128)S(1)}, u32[]{:S(2)}, u32[]{:S(2)}) %collective-permute-start.2) | collective-permute-done | bytes 65568 | tf_op jit(solution)/shard_map/ppermute | solution.py:26
  48.1 0.2 collective-permute-start.3
  48.3 4.2 %collective-permute-done.3 = f32[128,128]{1,0:T(8,128)S(1)} collective-permute-done((f32[128,128]{1,0:T(8,128)S(1)}, f32[128,128]{1,0:T(8,128)S(1)}, u32[]{:S(2)}, u32[]{:S(2)}) %collective-permute-start.3) | collective-permute-done | bytes 65568 | tf_op jit(solution)/shard_map/ppermute | solution.py:26
  52.4 5.6 %collective-permute-start.4 = (f32[128,128]{1,0:T(8,128)S(1)}, f32[128,128]{1,0:T(8,128)S(1)}, u32[]{:S(2)}, u32[]{:S(2)}) collective-permute-start(f32[128,128]{1,0:T(8,128)S(1)} %add.111), channel_id=1, source_target_pairs={{0,8},{4,12},{8,0},{12,4},{16,24},{20,28},{24,16},{28,20},{32,40},... | collective-permute-start | bytes 196616 | tf_op jit(solution)/shard_map/ppermute | solution.py:26
  58.0 2.2 %collective-permute-done.4 = f32[128,128]{1,0:T(8,128)S(1)} collective-permute-done((f32[128,128]{1,0:T(8,128)S(1)}, f32[128,128]{1,0:T(8,128)S(1)}, u32[]{:S(2)}, u32[]{:S(2)}) %collective-permute-start.4) | collective-permute-done | bytes 65568 | tf_op jit(solution)/shard_map/ppermute | solution.py:26
  60.3 2.8 %collective-permute-start.5 = (f32[128,128]{1,0:T(8,128)S(1)}, f32[128,128]{1,0:T(8,128)S(1)}, u32[]{:S(2)}, u32[]{:S(2)}) collective-permute-start(f32[128,128]{1,0:T(8,128)S(1)} %add.112), channel_id=1, source_target_pairs={{0,16},{4,20},{8,24},{12,28},{16,0},{20,4},{24,8},{28,12},{32,48},... | collective-permute-start | bytes 196616 | tf_op jit(solution)/shard_map/ppermute | solution.py:26
  63.1 6.2 %collective-permute-done.5 = f32[128,128]{1,0:T(8,128)S(1)} collective-permute-done((f32[128,128]{1,0:T(8,128)S(1)}, f32[128,128]{1,0:T(8,128)S(1)}, u32[]{:S(2)}, u32[]{:S(2)}) %collective-permute-start.5) | collective-permute-done | bytes 65568 | tf_op jit(solution)/shard_map/ppermute | solution.py:26
  69.3 1.7 %collective-permute-start.6 = (f32[128,128]{1,0:T(8,128)S(1)}, f32[128,128]{1,0:T(8,128)S(1)}, u32[]{:S(2)}, u32[]{:S(2)}) collective-permute-start(f32[128,128]{1,0:T(8,128)S(1)} %add.113), channel_id=1, source_target_pairs={{0,32},{4,36},{8,40},{12,44},{16,48},{20,52},{24,56},{28,60},{32,0... | collective-permute-start | bytes 196616 | tf_op jit(solution)/shard_map/ppermute | solution.py:26
  70.9 2.7 %collective-permute-done.6 = f32[128,128]{1,0:T(8,128)S(1)} collective-permute-done((f32[128,128]{1,0:T(8,128)S(1)}, f32[128,128]{1,0:T(8,128)S(1)}, u32[]{:S(2)}, u32[]{:S(2)}) %collective-permute-start.6) | collective-permute-done | bytes 65568 | tf_op jit(solution)/shard_map/ppermute | solution.py:26
  73.6 3.6 %collective-permute-start.7 = (f32[128,128]{1,0:T(8,128)S(1)}, f32[128,128]{1,0:T(8,128)S(1)}, u32[]{:S(2)}, u32[]{:S(2)}) collective-permute-start(f32[128,128]{1,0:T(8,128)S(1)} %add.114), channel_id=1, source_target_pairs={{0,64},{4,68},{8,72},{12,76},{16,80},{20,84},{24,88},{28,92},{32,9... | collective-permute-start | bytes 196616 | tf_op jit(solution)/shard_map/ppermute | solution.py:26
  77.2 2.2 %collective-permute-done.7 = f32[128,128]{1,0:T(8,128)S(1)} collective-permute-done((f32[128,128]{1,0:T(8,128)S(1)}, f32[128,128]{1,0:T(8,128)S(1)}, u32[]{:S(2)}, u32[]{:S(2)}) %collective-permute-start.7) | collective-permute-done | bytes 65568 | tf_op jit(solution)/shard_map/ppermute | solution.py:26
  79.5 0.6 multiply_reduce_fusion
  80.1 1.5 %collective-permute-start.8 = (f32[]{:T(128)}, f32[]{:T(128)}, u32[]{:S(2)}, u32[]{:S(2)}) collective-permute-start(f32[]{:T(128)} %get-tuple-element.15), channel_id=1, source_target_pairs={{0,1},{1,0},{2,3},{3,2},{4,5},{5,4},{6,7},{7,6},{8,9},{9,8},{10,11... | collective-permute-start | bytes 20 | tf_op jit(solution)/shard_map/ppermute | solution.py:26
  81.6 2.3 %collective-permute-done.8 = f32[]{:T(128)} collective-permute-done((f32[]{:T(128)}, f32[]{:T(128)}, u32[]{:S(2)}, u32[]{:S(2)}) %collective-permute-start.8) | collective-permute-done | bytes 36 | tf_op jit(solution)/shard_map/ppermute | solution.py:26
  85.1 4.4 %collective-permute-start.9 = (f32[]{:T(128)}, f32[]{:T(128)}, u32[]{:S(2)}, u32[]{:S(2)}) collective-permute-start(f32[]{:T(128)} %add.116), channel_id=1, source_target_pairs={{0,2},{1,3},{2,0},{3,1},{4,6},{5,7},{6,4},{7,5},{8,10},{9,11},{10,... | collective-permute-start | bytes 20 | tf_op jit(solution)/shard_map/ppermute | solution.py:26
  89.5 0.9 collective-permute-done.9
  91.0 0.6 broadcast_multiply_fusion
  (12 shorter events, 0.1 us)
Async XLA Ops:
  0.6 5.3 %copy-start = (bf16[1,256,2048]{2,1,0:T(8,128)(2,1)S(1)}, bf16[1,256,2048]{2,1,0:T(8,128)(2,1)}, u32[]{:S(2)}) copy-start(bf16[1,256,2048]{2,1,0:T(8,128)(2,1)} %param.6) | copy-start | bytes 3145732
  2.1 15.6 %collective-permute-start = (bf16[128,2048]{1,0:T(8,128)(2,1)S(1)}, bf16[128,2048]{1,0:T(8,128)(2,1)S(1)}, u32[]{:S(2)}, u32[]{:S(2)}) collective-permute-start(bf16[128,2048]{1,0:T(8,128)(2,1)S(1)} %fusion), channel_id=1, source_target_pairs={{0,4},{4,8},{8,12},{12,16},{16,20},{20,24},{24,28},{28,32},{32,36}... | collective-permute-start | bytes 1572872 | tf_op jit(solution)/shard_map/ppermute | solution.py:19
  7.1 15.5 %collective-permute-start.1 = (bf16[128,2048]{1,0:T(8,128)(2,1)S(1)}, bf16[128,2048]{1,0:T(8,128)(2,1)S(1)}, u32[]{:S(2)}, u32[]{:S(2)}) collective-permute-start(bf16[128,2048]{1,0:T(8,128)(2,1)S(1)} %fusion.1), channel_id=1, source_target_pairs={{4,0},{8,4},{12,8},{16,12},{20,16},{24,20},{28,24},{32,28},{36,32}... | collective-permute-start | bytes 1572872 | tf_op jit(solution)/shard_map/ppermute | solution.py:19
  9.4 0.7 copy-start.5
  10.6 1.6 %copy-start.1 = (bf16[3,128,256]{2,1,0:T(8,128)(2,1)}, bf16[3,128,256]{2,1,0:T(8,128)(2,1)S(1)}, u32[]{:S(2)}) copy-start(bf16[3,128,256]{2,1,0:T(8,128)(2,1)S(1)} %and_convert_fusion.1.m_ref) | copy-start | bytes 589828
  10.6 0.8 copy-start.4
  17.6 4.9 %copy-start.2 = (bf16[128,2048]{1,0:T(8,128)(2,1)}, bf16[128,2048]{1,0:T(8,128)(2,1)S(1)}, u32[]{:S(2)}) copy-start(bf16[128,2048]{1,0:T(8,128)(2,1)S(1)} %collective-permute-done.prev_ref) | copy-start | bytes 1572868
  22.5 0.8 copy-start.3
  46.7 1.3 %collective-permute-start.2 = (f32[128,128]{1,0:T(8,128)S(1)}, f32[128,128]{1,0:T(8,128)S(1)}, u32[]{:S(2)}, u32[]{:S(2)}) collective-permute-start(f32[128,128]{1,0:T(8,128)S(1)} %rev.11), channel_id=1, source_target_pairs={{0,128},{128,0},{1,129},{129,1},{2,130},{130,2},{3,131},{131,3},{4... | collective-permute-start | bytes 196616 | tf_op jit(solution)/shard_map/ppermute | solution.py:26
  48.1 4.4 %collective-permute-start.3 = (f32[128,128]{1,0:T(8,128)S(1)}, f32[128,128]{1,0:T(8,128)S(1)}, u32[]{:S(2)}, u32[]{:S(2)}) collective-permute-start(f32[128,128]{1,0:T(8,128)S(1)} %add.110), channel_id=1, source_target_pairs={{0,4},{4,0},{8,12},{12,8},{16,20},{20,16},{24,28},{28,24},{32,36},... | collective-permute-start | bytes 196616 | tf_op jit(solution)/shard_map/ppermute | solution.py:26
  52.4 7.8 %collective-permute-start.4 = (f32[128,128]{1,0:T(8,128)S(1)}, f32[128,128]{1,0:T(8,128)S(1)}, u32[]{:S(2)}, u32[]{:S(2)}) collective-permute-start(f32[128,128]{1,0:T(8,128)S(1)} %add.111), channel_id=1, source_target_pairs={{0,8},{4,12},{8,0},{12,4},{16,24},{20,28},{24,16},{28,20},{32,40},... | collective-permute-start | bytes 196616 | tf_op jit(solution)/shard_map/ppermute | solution.py:26
  60.3 9.0 %collective-permute-start.5 = (f32[128,128]{1,0:T(8,128)S(1)}, f32[128,128]{1,0:T(8,128)S(1)}, u32[]{:S(2)}, u32[]{:S(2)}) collective-permute-start(f32[128,128]{1,0:T(8,128)S(1)} %add.112), channel_id=1, source_target_pairs={{0,16},{4,20},{8,24},{12,28},{16,0},{20,4},{24,8},{28,12},{32,48},... | collective-permute-start | bytes 196616 | tf_op jit(solution)/shard_map/ppermute | solution.py:26
  69.3 4.4 %collective-permute-start.6 = (f32[128,128]{1,0:T(8,128)S(1)}, f32[128,128]{1,0:T(8,128)S(1)}, u32[]{:S(2)}, u32[]{:S(2)}) collective-permute-start(f32[128,128]{1,0:T(8,128)S(1)} %add.113), channel_id=1, source_target_pairs={{0,32},{4,36},{8,40},{12,44},{16,48},{20,52},{24,56},{28,60},{32,0... | collective-permute-start | bytes 196616 | tf_op jit(solution)/shard_map/ppermute | solution.py:26
  73.6 5.9 %collective-permute-start.7 = (f32[128,128]{1,0:T(8,128)S(1)}, f32[128,128]{1,0:T(8,128)S(1)}, u32[]{:S(2)}, u32[]{:S(2)}) collective-permute-start(f32[128,128]{1,0:T(8,128)S(1)} %add.114), channel_id=1, source_target_pairs={{0,64},{4,68},{8,72},{12,76},{16,80},{20,84},{24,88},{28,92},{32,9... | collective-permute-start | bytes 196616 | tf_op jit(solution)/shard_map/ppermute | solution.py:26
  80.1 3.8 %collective-permute-start.8 = (f32[]{:T(128)}, f32[]{:T(128)}, u32[]{:S(2)}, u32[]{:S(2)}) collective-permute-start(f32[]{:T(128)} %get-tuple-element.15), channel_id=1, source_target_pairs={{0,1},{1,0},{2,3},{3,2},{4,5},{5,4},{6,7},{7,6},{8,9},{9,8},{10,11... | collective-permute-start | bytes 20 | tf_op jit(solution)/shard_map/ppermute | solution.py:26
  85.1 5.3 %collective-permute-start.9 = (f32[]{:T(128)}, f32[]{:T(128)}, u32[]{:S(2)}, u32[]{:S(2)}) collective-permute-start(f32[]{:T(128)} %add.116), channel_id=1, source_target_pairs={{0,2},{1,3},{2,0},{3,1},{4,6},{5,7},{6,4},{7,5},{8,10},{9,11},{10,... | collective-permute-start | bytes 20 | tf_op jit(solution)/shard_map/ppermute | solution.py:26

commit v8 on v7

--- a/solution.py
+++ b/solution.py
@@ -1,3 +1,4 @@
+import functools
 import math
 
 import jax
@@ -29,8 +30,8 @@
     return value
 
 
-def conv_kernel(q_ref, k_ref, v_ref, go_ref, prev_ref, next_ref, fp_ref, fq_ref, m_ref, mt_ref, mr_ref,
-                mo_ref, gq_ref, gk_ref, gv_ref, raw_ref):
+def conv_kernel(q_ref, k_ref, v_ref, go_ref, prev_ref, next_ref, fp_ref, fq_ref, m_ref, mt_ref, mr_ref, *refs, extra):
+    mo_ref, gq_ref, gk_ref, gv_ref, raw_ref = refs[extra:]
     f32, bf16 = jnp.float32, jnp.bfloat16
     rows = q_ref.shape[0]
     blocks = rows // FLEN
@@ -88,28 +89,37 @@
     gv_ref[...] = (back_all * keys).astype(bf16)
 
 
-def grouped_conv(q2, k2, v2, g2, prev_tail, next_head, fp, fq, mask, mask_t, interpret=False):
+def grouped_conv(q2, k2, v2, g2, prev_tail, next_head, fp, fq, mask, mask_t, first=0, outs=None, interpret=False):
     mask_r = mask[:-1, ::-1, :]
     rows, channels = q2.shape
-    tiles = channels // LANES
+    tiles = prev_tail.shape[1] // LANES
     per_tile = LANES // GROUP
     nb = rows // FLEN
-    tok = pl.BlockSpec((rows, LANES), lambda j: (0, j))
+    tok = pl.BlockSpec((rows, LANES), lambda j: (0, j + first))
     halo = pl.BlockSpec((FLEN, LANES), lambda j: (0, j))
-    filt = pl.BlockSpec((per_tile, 2 * FLEN), lambda j: (j, 0))
+    filt = pl.BlockSpec((per_tile, 2 * FLEN), lambda j: (j + first, 0))
     mspec = pl.BlockSpec((nb + 1, FLEN, 2 * FLEN), lambda j: (0, 0, 0))
     mtspec = pl.BlockSpec((nb + 1, 2 * FLEN, FLEN), lambda j: (0, 0, 0))
     mrspec = pl.BlockSpec((nb, FLEN, 2 * FLEN), lambda j: (0, 0, 0))
+    in_specs = [tok, tok, tok, tok, halo, halo, filt, filt, mspec, mtspec, mrspec]
+    operands = [q2, k2, v2, g2, prev_tail, next_head, fp, fq, mask, mask_t, mask_r]
+    aliases = {}
+    if outs is not None:
+        for i, o in enumerate(outs):
+            aliases[len(operands)] = i
+            operands.append(o)
+            in_specs.append(pl.BlockSpec(memory_space=pl.ANY))
     out_tok = jax.ShapeDtypeStruct((rows, channels), jnp.bfloat16)
     return pl.pallas_call(
-        conv_kernel,
+        functools.partial(conv_kernel, extra=len(aliases)),
         grid=(tiles,),
-        in_specs=[tok, tok, tok, tok, halo, halo, filt, filt, mspec, mtspec, mrspec],
+        in_specs=in_specs,
         out_specs=[tok, tok, tok, tok, pl.BlockSpec((1, per_tile, 2 * FLEN), lambda j: (j, 0, 0))],
         out_shape=[out_tok, out_tok, out_tok, out_tok,
                    jax.ShapeDtypeStruct((tiles, per_tile, 2 * FLEN), jnp.float32)],
+        input_output_aliases=aliases,
         interpret=interpret,
-    )(q2, k2, v2, g2, prev_tail, next_head, fp, fq, mask, mask_t, mask_r)
+    )(*operands)
 
 
 def doc_masks(lengths, offset, rows):
@@ -137,15 +147,23 @@
 def on_device(query_in, key_in, value_in, grad_out, seq_lengths, filters):
     f32, bf16 = jnp.float32, jnp.bfloat16
     q2, k2, v2, g2 = query_in[0], key_in[0], value_in[0], grad_out[0]
-    rows = q2.shape[0]
+    rows, channels = q2.shape
     tail = (k2[rows - FLEN:].astype(f32) * v2[rows - FLEN:].astype(f32)).astype(bf16)
     head = (g2[:FLEN].astype(f32) * q2[:FLEN].astype(f32)).astype(bf16)
-    prev_tail = passed_along(tail, "ctx", 1)
-    next_head = passed_along(head, "ctx", -1)
+    half = channels // 2
+    prev_tails = [passed_along(tail[:, :half], "ctx", 1), passed_along(tail[:, half:], "ctx", 1)]
+    next_heads = [passed_along(head[:, :half], "ctx", -1), passed_along(head[:, half:], "ctx", -1)]
     mask, mask_t = doc_masks(seq_lengths[0], lax.axis_index("ctx") * rows, rows)
     fp, fq = filter_rows(filters)
-    mixed_out, grad_query, grad_key, grad_value, cols = grouped_conv(
-        q2, k2, v2, g2, prev_tail, next_head, fp, fq, mask, mask_t)
+    outs = None
+    parts = []
+    for p in range(2):
+        result = grouped_conv(q2, k2, v2, g2, prev_tails[p], next_heads[p], fp, fq, mask, mask_t,
+                              first=p * (half // LANES), outs=outs)
+        outs = result[:4]
+        parts.append(result[4])
+    mixed_out, grad_query, grad_key, grad_value = outs
+    cols = jnp.concatenate(parts, axis=0)
     local_raw = cols.reshape(-1, 2 * FLEN)[:, 2 * FLEN - 1:FLEN - 1:-1]
     summed = doubling_sum(doubling_sum(local_raw, "dp"), "ctx")
     squares = doubling_sum(jnp.sum(summed * summed), "tensor")

time: 92.7 us -> 96.2 us (1.038)
  the two profiles are of different devices: /device:TPU:32 before, /device:TPU:16 now
where the time goes in v8:
time: 96.2 us; the launch traced here: 95.8 us
  waiting for transfers between devices  31.5 us (33%)
  starting transfers between devices  25.7 us (27%)
  Pallas kernels  24.6 us (26%)
  other arithmetic  6.08 us (6%)
  local copies, waits for them, and re-layouts  5.17 us (5%)
  between operations  2.91 us (3%)
    ppermute x8, waiting for transfers between devices, doubling_sum(): partner = lax.ppermute(value, axis, [(i, i ^ step) for i in range(count)])  29.1 us
    pallas_call x2, Pallas kernels, grouped_conv(): pl.pallas_call(functools.partial(conv_kernel, extra=len(aliases)), grid=(...  24.6 us
    ppermute x4, starting transfers between devices, passed_along(): lax.ppermute(value, axis, [(source, source + steps) for source in range(i...  15.4 us
    ppermute x8, starting transfers between devices, doubling_sum(): partner = lax.ppermute(value, axis, [(i, i ^ step) for i in range(count)])  10.2 us
    unnamed x20, local copies, waits for them, and re-layouts  2.76 us
    ppermute x4, waiting for transfers between devices, passed_along(): lax.ppermute(value, axis, [(source, source + steps) for source in range(i...  2.35 us
  transfers between devices with their start and end apart: 12, of which 9 were waited for; matrix products, arithmetic and copies ran while one was open for 5% of the time, Pallas kernels for 13%

profile of v8, /device:TPU:16, one launch (start us, length us, event | category | flops | bytes accessed | tf_op | source)
XLA Modules:
  0.0 95.8 jit_solution(17403880288772862608)
XLA Ops:
  0.6 0.0 copy-start.1
  0.6 0.0 copy-start
  0.7 1.5 %fusion.1 = bf16[128,2048]{1,0:T(8,128)(2,1)S(1)} fusion(bf16[1,256,2048]{2,1,0:T(8,128)(2,1)} %param.6, bf16[1,256,2048]{2,1,0:T(8,128)(2,1)} %param.9), kind=kLoop, calls=%fused_computation.3 | loop fusion | flops 1048576 | bytes 1572864 | tf_op jit(solution)/shard_map/convert_element_type | solution.py:152
  2.2 7.7 %collective-permute-start.3 = (bf16[128,1024]{1,0:T(8,128)(2,1)S(1)}, bf16[128,1024]{1,0:T(8,128)(2,1)S(1)}, u32[]{:S(2)}, u32[]{:S(2)}) collective-permute-start(bf16[128,1024]{1,0:T(8,128)(2,1)S(1)} %get-tuple-element.27), channel_id=1, source_target_pairs={{4,0},{8,4},{12,8},{16,12},{20,16},{24,20},{28,24},{32,28},{36,32}... | collective-permute-start | bytes 786440 | tf_op jit(solution)/shard_map/ppermute | solution.py:20
  9.8 2.9 %collective-permute-start.1 = (bf16[128,1024]{1,0:T(8,128)(2,1)S(1)}, bf16[128,1024]{1,0:T(8,128)(2,1)S(1)}, u32[]{:S(2)}, u32[]{:S(2)}) collective-permute-start(bf16[128,1024]{1,0:T(8,128)(2,1)S(1)} %get-tuple-element.28), channel_id=1, source_target_pairs={{4,0},{8,4},{12,8},{16,12},{20,16},{24,20},{28,24},{32,28},{36,32}... | collective-permute-start | bytes 786440 | tf_op jit(solution)/shard_map/ppermute | solution.py:20
  12.8 0.0 copy-done.1
  12.8 0.0 copy-done
  12.8 0.1 fusion
  13.0 2.9 %collective-permute-start.2 = (bf16[128,1024]{1,0:T(8,128)(2,1)S(1)}, bf16[128,1024]{1,0:T(8,128)(2,1)S(1)}, u32[]{:S(2)}, u32[]{:S(2)}) collective-permute-start(bf16[128,1024]{1,0:T(8,128)(2,1)S(1)} %get-tuple-element.29), channel_id=1, source_target_pairs={{0,4},{4,8},{8,12},{12,16},{16,20},{20,24},{24,28},{28,32},{32,36}... | collective-permute-start | bytes 786440 | tf_op jit(solution)/shard_map/ppermute | solution.py:20
  15.9 1.9 %collective-permute-start = (bf16[128,1024]{1,0:T(8,128)(2,1)S(1)}, bf16[128,1024]{1,0:T(8,128)(2,1)S(1)}, u32[]{:S(2)}, u32[]{:S(2)}) collective-permute-start(bf16[128,1024]{1,0:T(8,128)(2,1)S(1)} %get-tuple-element.30), channel_id=1, source_target_pairs={{0,4},{4,8},{8,12},{12,16},{16,20},{20,24},{24,28},{28,32},{32,36}... | collective-permute-start | bytes 786440 | tf_op jit(solution)/shard_map/ppermute | solution.py:20
  17.9 0.1 pad.5.clone
  17.9 0.1 iota_add_fusion.1
  18.0 0.1 iota_add_fusion
  18.1 0.1 fusion.6
  18.2 0.0 copy-start.9
  18.2 0.6 copy-done.9
  18.8 0.1 copy.17
  18.9 0.1 reduce-window.8
  19.0 0.0 copy-start.7
  19.0 0.1 reduce
  19.2 0.6 copy-done.7
  19.8 0.1 rev.10
  19.9 0.1 select_reduce_fusion
  20.0 0.8 maximum_maximum_fusion.fp_ref
  20.7 0.1 and_convert_fusion.1.m_ref
  20.9 0.0 copy-start.2
  20.9 0.7 concatenate.10.fq_ref
  21.6 0.0 copy-done.2
  21.6 1.3 %rev.11.mr_ref = bf16[2,128,256]{2,1,0:T(8,128)(2,1)} reverse(bf16[2,128,256]{2,1,0:T(8,128)(2,1)S(1)} %slice.47), dimensions={1} | reverse | bytes 262144 | tf_op jit(solution)/shard_map/rev | solution.py:93
  22.9 0.8 and_convert_fusion.mt_ref
  23.8 0.0 collective-permute-done.3.next_ref
  23.8 0.0 copy-start.5
  23.8 2.3 %collective-permute-done.2.prev_ref = bf16[128,1024]{1,0:T(8,128)(2,1)S(1)} collective-permute-done((bf16[128,1024]{1,0:T(8,128)(2,1)S(1)}, bf16[128,1024]{1,0:T(8,128)(2,1)S(1)}, u32[]{:S(2)}, u32[]{:S(2)}) %collective-permute-start.2) | collective-permute-done | bytes 262176 | tf_op jit(solution)/shard_map/ppermute | solution.py:20
  26.1 0.0 copy-done.5
  26.1 0.7 copy-done.6
  26.8 12.2 %shard_map.101 = (bf16[256,2048]{1,0:T(8,128)(2,1)}, bf16[256,2048]{1,0:T(8,128)(2,1)}, bf16[256,2048]{1,0:T(8,128)(2,1)}, bf16[256,2048]{1,0:T(8,128)(2,1)}, f32[8,8,256]{2,1,0:T(8,128)}) custom-call(bf16[256,2048]{1,0:T(8,128)(2,1)} %bitcast.18, bf16[256,2048]{1,0:T(8,128)(2,1)} %bitcast.20, bf16[256,2048]{1,0:T(8,128)(2,1)} %bitcast.22, ...), custom_call_target="tpu_custom_call" | custom-call | tf_op jit(solution)/shard_map/pallas_call | solution.py:113
  39.1 0.0 collective-permute-done.1.next_ref
  39.1 0.0 copy-start.3
  39.1 0.0 collective-permute-done.prev_ref
  39.1 0.0 copy-start.4
  39.1 0.7 copy-done.3
  39.8 0.1 copy-done.4
  39.9 12.3 %shard_map.102 = (bf16[256,2048]{1,0:T(8,128)(2,1)}, bf16[256,2048]{1,0:T(8,128)(2,1)}, bf16[256,2048]{1,0:T(8,128)(2,1)}, bf16[256,2048]{1,0:T(8,128)(2,1)}, f32[8,8,256]{2,1,0:T(8,128)}) custom-call(bf16[256,2048]{1,0:T(8,128)(2,1)} %bitcast.19, ...), custom_call_target="tpu_custom_call", output_to_operand_aliasing={{0}: (11, {}), {1}: (12, {}), {2}: (13, {}), {3}: (14, {})} | custom-call | tf_op jit(solution)/shard_map/pallas_call | solution.py:113
  52.2 0.0 copy-done.8
  52.2 0.9 maximum_bitcast_fusion
  53.1 0.1 rev.12
  53.2 0.1 collective-permute-start.4
  53.2 1.2 %collective-permute-done.4 = f32[128,128]{1,0:T(8,128)S(1)} collective-permute-done((f32[128,128]{1,0:T(8,128)S(1)}, f32[128,128]{1,0:T(8,128)S(1)}, u32[]{:S(2)}, u32[]{:S(2)}) %collective-permute-start.4) | collective-permute-done | bytes 65568 | tf_op jit(solution)/shard_map/ppermute | solution.py:27
  54.5 0.1 collective-permute-start.5
  54.6 4.3 %collective-permute-done.5 = f32[128,128]{1,0:T(8,128)S(1)} collective-permute-done((f32[128,128]{1,0:T(8,128)S(1)}, f32[128,128]{1,0:T(8,128)S(1)}, u32[]{:S(2)}, u32[]{:S(2)}) %collective-permute-start.5) | collective-permute-done | bytes 65568 | tf_op jit(solution)/shard_map/ppermute | solution.py:27
  58.9 0.1 collective-permute-start.6
  59.0 5.5 %collective-permute-done.6 = f32[128,128]{1,0:T(8,128)S(1)} collective-permute-done((f32[128,128]{1,0:T(8,128)S(1)}, f32[128,128]{1,0:T(8,128)S(1)}, u32[]{:S(2)}, u32[]{:S(2)}) %collective-permute-start.6) | collective-permute-done | bytes 65568 | tf_op jit(solution)/shard_map/ppermute | solution.py:27
  64.4 2.3 %collective-permute-start.7 = (f32[128,128]{1,0:T(8,128)S(1)}, f32[128,128]{1,0:T(8,128)S(1)}, u32[]{:S(2)}, u32[]{:S(2)}) collective-permute-start(f32[128,128]{1,0:T(8,128)S(1)} %add.112), channel_id=1, source_target_pairs={{0,16},{4,20},{8,24},{12,28},{16,0},{20,4},{24,8},{28,12},{32,48},... | collective-permute-start | bytes 196616 | tf_op jit(solution)/shard_map/ppermute | solution.py:27
  66.8 5.9 %collective-permute-done.7 = f32[128,128]{1,0:T(8,128)S(1)} collective-permute-done((f32[128,128]{1,0:T(8,128)S(1)}, f32[128,128]{1,0:T(8,128)S(1)}, u32[]{:S(2)}, u32[]{:S(2)}) %collective-permute-start.7) | collective-permute-done | bytes 65568 | tf_op jit(solution)/shard_map/ppermute | solution.py:27
  72.7 1.7 %collective-permute-start.8 = (f32[128,128]{1,0:T(8,128)S(1)}, f32[128,128]{1,0:T(8,128)S(1)}, u32[]{:S(2)}, u32[]{:S(2)}) collective-permute-start(f32[128,128]{1,0:T(8,128)S(1)} %add.113), channel_id=1, source_target_pairs={{0,32},{4,36},{8,40},{12,44},{16,48},{20,52},{24,56},{28,60},{32,0... | collective-permute-start | bytes 196616 | tf_op jit(solution)/shard_map/ppermute | solution.py:27
  74.4 3.3 %collective-permute-done.8 = f32[128,128]{1,0:T(8,128)S(1)} collective-permute-done((f32[128,128]{1,0:T(8,128)S(1)}, f32[128,128]{1,0:T(8,128)S(1)}, u32[]{:S(2)}, u32[]{:S(2)}) %collective-permute-start.8) | collective-permute-done | bytes 65568 | tf_op jit(solution)/shard_map/ppermute | solution.py:27
  77.7 0.1 collective-permute-start.9
  77.8 5.8 %collective-permute-done.9 = f32[128,128]{1,0:T(8,128)S(1)} collective-permute-done((f32[128,128]{1,0:T(8,128)S(1)}, f32[128,128]{1,0:T(8,128)S(1)}, u32[]{:S(2)}, u32[]{:S(2)}) %collective-permute-start.9) | collective-permute-done | bytes 65568 | tf_op jit(solution)/shard_map/ppermute | solution.py:27
  83.5 0.6 multiply_reduce_fusion
  84.2 1.5 %collective-permute-start.10 = (f32[]{:T(128)}, f32[]{:T(128)}, u32[]{:S(2)}, u32[]{:S(2)}) collective-permute-start(f32[]{:T(128)} %get-tuple-element.25), channel_id=1, source_target_pairs={{0,1},{1,0},{2,3},{3,2},{4,5},{5,4},{6,7},{7,6},{8,9},{9,8},{10,11... | collective-permute-start | bytes 20 | tf_op jit(solution)/shard_map/ppermute | solution.py:27
  85.6 2.3 %collective-permute-done.10 = f32[]{:T(128)} collective-permute-done((f32[]{:T(128)}, f32[]{:T(128)}, u32[]{:S(2)}, u32[]{:S(2)}) %collective-permute-start.10) | collective-permute-done | bytes 36 | tf_op jit(solution)/shard_map/ppermute | solution.py:27
  89.3 4.4 %collective-permute-start.11 = (f32[]{:T(128)}, f32[]{:T(128)}, u32[]{:S(2)}, u32[]{:S(2)}) collective-permute-start(f32[]{:T(128)} %add.116), channel_id=1, source_target_pairs={{0,2},{1,3},{2,0},{3,1},{4,6},{5,7},{6,4},{7,5},{8,10},{9,11},{10,... | collective-permute-start | bytes 20 | tf_op jit(solution)/shard_map/ppermute | solution.py:27
  93.7 0.9 collective-permute-done.11
  95.2 0.6 broadcast_multiply_fusion
  (17 shorter events, 0.2 us)
Async XLA Ops:
  0.6 12.1 %copy-start.1 = (bf16[1,256,2048]{2,1,0:T(8,128)(2,1)S(1)}, bf16[1,256,2048]{2,1,0:T(8,128)(2,1)}, u32[]{:S(2)}) copy-start(bf16[1,256,2048]{2,1,0:T(8,128)(2,1)} %param.8) | copy-start | bytes 3145732
  0.6 12.1 %copy-start = (bf16[1,256,2048]{2,1,0:T(8,128)(2,1)S(1)}, bf16[1,256,2048]{2,1,0:T(8,128)(2,1)}, u32[]{:S(2)}) copy-start(bf16[1,256,2048]{2,1,0:T(8,128)(2,1)} %param.7) | copy-start | bytes 3145732
  2.2 21.6 %collective-permute-start.3 = (bf16[128,1024]{1,0:T(8,128)(2,1)S(1)}, bf16[128,1024]{1,0:T(8,128)(2,1)S(1)}, u32[]{:S(2)}, u32[]{:S(2)}) collective-permute-start(bf16[128,1024]{1,0:T(8,128)(2,1)S(1)} %get-tuple-element.27), channel_id=1, source_target_pairs={{4,0},{8,4},{12,8},{16,12},{20,16},{24,20},{28,24},{32,28},{36,32}... | collective-permute-start | bytes 786440 | tf_op jit(solution)/shard_map/ppermute | solution.py:20
  9.8 29.2 %collective-permute-start.1 = (bf16[128,1024]{1,0:T(8,128)(2,1)S(1)}, bf16[128,1024]{1,0:T(8,128)(2,1)S(1)}, u32[]{:S(2)}, u32[]{:S(2)}) collective-permute-start(bf16[128,1024]{1,0:T(8,128)(2,1)S(1)} %get-tuple-element.28), channel_id=1, source_target_pairs={{4,0},{8,4},{12,8},{16,12},{20,16},{24,20},{28,24},{32,28},{36,32}... | collective-permute-start | bytes 786440 | tf_op jit(solution)/shard_map/ppermute | solution.py:20
  13.0 13.2 %collective-permute-start.2 = (bf16[128,1024]{1,0:T(8,128)(2,1)S(1)}, bf16[128,1024]{1,0:T(8,128)(2,1)S(1)}, u32[]{:S(2)}, u32[]{:S(2)}) collective-permute-start(bf16[128,1024]{1,0:T(8,128)(2,1)S(1)} %get-tuple-element.29), channel_id=1, source_target_pairs={{0,4},{4,8},{8,12},{12,16},{16,20},{20,24},{24,28},{28,32},{32,36}... | collective-permute-start | bytes 786440 | tf_op jit(solution)/shard_map/ppermute | solution.py:20
  15.9 23.2 %collective-permute-start = (bf16[128,1024]{1,0:T(8,128)(2,1)S(1)}, bf16[128,1024]{1,0:T(8,128)(2,1)S(1)}, u32[]{:S(2)}, u32[]{:S(2)}) collective-permute-start(bf16[128,1024]{1,0:T(8,128)(2,1)S(1)} %get-tuple-element.30), channel_id=1, source_target_pairs={{0,4},{4,8},{8,12},{12,16},{16,20},{20,24},{24,28},{28,32},{32,36}... | collective-permute-start | bytes 786440 | tf_op jit(solution)/shard_map/ppermute | solution.py:20
  18.2 0.7 copy-start.9
  19.0 0.8 copy-start.7
  20.9 0.7 copy-start.2
  23.8 2.3 %copy-start.5 = (bf16[128,1024]{1,0:T(8,128)(2,1)}, bf16[128,1024]{1,0:T(8,128)(2,1)S(1)}, u32[]{:S(2)}) copy-start(bf16[128,1024]{1,0:T(8,128)(2,1)S(1)} %collective-permute-done.3.next_ref) | copy-start | bytes 786436
  26.1 0.7 copy-start.6
  39.1 0.7 copy-start.3
  39.1 0.8 copy-start.4
  39.9 12.4 %copy-start.8 = (f32[8,8,256]{2,1,0:T(8,128)S(1)}, f32[8,8,256]{2,1,0:T(8,128)}, u32[]{:S(2)}) copy-start(f32[8,8,256]{2,1,0:T(8,128)} %get-tuple-element.23) | copy-start | bytes 196612
  53.2 1.3 %collective-permute-start.4 = (f32[128,128]{1,0:T(8,128)S(1)}, f32[128,128]{1,0:T(8,128)S(1)}, u32[]{:S(2)}, u32[]{:S(2)}) collective-permute-start(f32[128,128]{1,0:T(8,128)S(1)} %rev.12), channel_id=1, source_target_pairs={{0,128},{128,0},{1,129},{129,1},{2,130},{130,2},{3,131},{131,3},{4... | collective-permute-start | bytes 196616 | tf_op jit(solution)/shard_map/ppermute | solution.py:27
  54.5 4.4 %collective-permute-start.5 = (f32[128,128]{1,0:T(8,128)S(1)}, f32[128,128]{1,0:T(8,128)S(1)}, u32[]{:S(2)}, u32[]{:S(2)}) collective-permute-start(f32[128,128]{1,0:T(8,128)S(1)} %add.110), channel_id=1, source_target_pairs={{0,4},{4,0},{8,12},{12,8},{16,20},{20,16},{24,28},{28,24},{32,36},... | collective-permute-start | bytes 196616 | tf_op jit(solution)/shard_map/ppermute | solution.py:27
  58.9 5.6 %collective-permute-start.6 = (f32[128,128]{1,0:T(8,128)S(1)}, f32[128,128]{1,0:T(8,128)S(1)}, u32[]{:S(2)}, u32[]{:S(2)}) collective-permute-start(f32[128,128]{1,0:T(8,128)S(1)} %add.111), channel_id=1, source_target_pairs={{0,8},{4,12},{8,0},{12,4},{16,24},{20,28},{24,16},{28,20},{32,40},... | collective-permute-start | bytes 196616 | tf_op jit(solution)/shard_map/ppermute | solution.py:27
  64.4 8.3 %collective-permute-start.7 = (f32[128,128]{1,0:T(8,128)S(1)}, f32[128,128]{1,0:T(8,128)S(1)}, u32[]{:S(2)}, u32[]{:S(2)}) collective-permute-start(f32[128,128]{1,0:T(8,128)S(1)} %add.112), channel_id=1, source_target_pairs={{0,16},{4,20},{8,24},{12,28},{16,0},{20,4},{24,8},{28,12},{32,48},... | collective-permute-start | bytes 196616 | tf_op jit(solution)/shard_map/ppermute | solution.py:27
  72.7 5.0 %collective-permute-start.8 = (f32[128,128]{1,0:T(8,128)S(1)}, f32[128,128]{1,0:T(8,128)S(1)}, u32[]{:S(2)}, u32[]{:S(2)}) collective-permute-start(f32[128,128]{1,0:T(8,128)S(1)} %add.113), channel_id=1, source_target_pairs={{0,32},{4,36},{8,40},{12,44},{16,48},{20,52},{24,56},{28,60},{32,0... | collective-permute-start | bytes 196616 | tf_op jit(solution)/shard_map/ppermute | solution.py:27
  77.7 5.9 %collective-permute-start.9 = (f32[128,128]{1,0:T(8,128)S(1)}, f32[128,128]{1,0:T(8,128)S(1)}, u32[]{:S(2)}, u32[]{:S(2)}) collective-permute-start(f32[128,128]{1,0:T(8,128)S(1)} %add.114), channel_id=1, source_target_pairs={{0,64},{4,68},{8,72},{12,76},{16,80},{20,84},{24,88},{28,92},{32,9... | collective-permute-start | bytes 196616 | tf_op jit(solution)/shard_map/ppermute | solution.py:27
  84.2 3.8 %collective-permute-start.10 = (f32[]{:T(128)}, f32[]{:T(128)}, u32[]{:S(2)}, u32[]{:S(2)}) collective-permute-start(f32[]{:T(128)} %get-tuple-element.25), channel_id=1, source_target_pairs={{0,1},{1,0},{2,3},{3,2},{4,5},{5,4},{6,7},{7,6},{8,9},{9,8},{10,11... | collective-permute-start | bytes 20 | tf_op jit(solution)/shard_map/ppermute | solution.py:27
  89.3 5.3 %collective-permute-start.11 = (f32[]{:T(128)}, f32[]{:T(128)}, u32[]{:S(2)}, u32[]{:S(2)}) collective-permute-start(f32[]{:T(128)} %add.116), channel_id=1, source_target_pairs={{0,2},{1,3},{2,0},{3,1},{4,6},{5,7},{6,4},{7,5},{8,10},{9,11},{10,... | collective-permute-start | bytes 20 | tf_op jit(solution)/shard_map/ppermute | solution.py:27

commit v9 on v7

--- a/solution.py
+++ b/solution.py
@@ -19,13 +19,11 @@
     return lax.ppermute(value, axis, [(source, source + steps) for source in range(initial, last)])
 
 
-def doubling_sum(value, axis):
+def doubling_sum(value, axis, masks):
     count = lax.axis_size(axis)
-    step = 1
-    while step < count:
-        partner = lax.ppermute(value, axis, [(i, i ^ step) for i in range(count)])
+    for mask in masks:
+        partner = lax.ppermute(value, axis, [(i, i ^ mask) for i in range(count)])
         value = value + partner
-        step *= 2
     return value
 
 
@@ -134,6 +132,21 @@
     return fp, fq
 
 
+def mirror_masks(count):
+    masks, width = [], 1
+    while width < count:
+        masks.append(2 * width - 1)
+        width *= 2
+    return masks
+
+
+def ctx_masks():
+    inner = 8 if lax.axis_size("ctx") % 8 == 0 else 1
+    outer = lax.axis_size("ctx") // inner
+    low = [1, 2, 7][: inner.bit_length() - 1]
+    return low + [m * inner for m in mirror_masks(outer)]
+
+
 def on_device(query_in, key_in, value_in, grad_out, seq_lengths, filters):
     f32, bf16 = jnp.float32, jnp.bfloat16
     q2, k2, v2, g2 = query_in[0], key_in[0], value_in[0], grad_out[0]
@@ -147,8 +160,8 @@
     mixed_out, grad_query, grad_key, grad_value, cols = grouped_conv(
         q2, k2, v2, g2, prev_tail, next_head, fp, fq, mask, mask_t)
     local_raw = cols.reshape(-1, 2 * FLEN)[:, 2 * FLEN - 1:FLEN - 1:-1]
-    summed = doubling_sum(doubling_sum(local_raw, "dp"), "ctx")
-    squares = doubling_sum(jnp.sum(summed * summed), "tensor")
+    summed = doubling_sum(doubling_sum(local_raw, "dp", mirror_masks(lax.axis_size("dp"))), "ctx", ctx_masks())
+    squares = doubling_sum(jnp.sum(summed * summed), "tensor", mirror_masks(lax.axis_size("tensor")))
     factor = jnp.minimum(1.0, math.sqrt(GROUPS * FLEN) / jnp.sqrt(squares))
     grad_filters = summed * factor
     return (mixed_out[None], grad_query[None], grad_key[None], grad_value[None], grad_filters)

time: 92.7 us -> 89.8 us (0.969)
  waiting for transfers between devices: 29.2 us -> 27.8 us
    ppermute x8, waiting for transfers between devices: 21.9 us -> 20.5 us  [doubling_sum(): partner = lax.ppermute(value, axis, [(i, i ^ mask) for i in range(count)])]
where the time goes in v9:
time: 89.8 us; the launch traced here: 89.4 us
  waiting for transfers between devices  27.8 us (31%)
  starting transfers between devices  25 us (28%)
  Pallas kernels  22.5 us (25%)
  other arithmetic  6.22 us (7%)
  local copies, waits for them, and re-layouts  5.35 us (6%)
  between operations  2.63 us (3%)
    pallas_call x1, Pallas kernels, grouped_conv(): pl.pallas_call(conv_kernel, grid=(tiles,), in_specs=[tok, tok, tok, tok,...  22.5 us
    ppermute x8, waiting for transfers between devices, doubling_sum(): partner = lax.ppermute(value, axis, [(i, i ^ mask) for i in range(count)])  20.5 us
    ppermute x8, starting transfers between devices, doubling_sum(): partner = lax.ppermute(value, axis, [(i, i ^ mask) for i in range(count)])  19.1 us
    ppermute x2, waiting for transfers between devices, passed_along(): lax.ppermute(value, axis, [(source, source + steps) for source in range(i...  7.33 us
    ppermute x2, starting transfers between devices, passed_along(): lax.ppermute(value, axis, [(source, source + steps) for source in range(i...  5.87 us
    unnamed x12, local copies, waits for them, and re-layouts  2.18 us
  transfers between devices with their start and end apart: 10, of which 10 were waited for; matrix products, arithmetic and copies ran while one was open for 6% of the time, Pallas kernels for 0%

profile of v9, /device:TPU:32, one launch (start us, length us, event | category | flops | bytes accessed | tf_op | source)
XLA Modules:
  0.0 89.4 jit_solution(3945972420098899428)
XLA Ops:
  0.6 0.0 copy-start
  0.6 1.4 %fusion = bf16[128,2048]{1,0:T(8,128)(2,1)S(1)} fusion(bf16[1,256,2048]{2,1,0:T(8,128)(2,1)} %param.8, bf16[1,256,2048]{2,1,0:T(8,128)(2,1)} %param.7), kind=kLoop, calls=%fused_computation.2 | loop fusion | flops 1048576 | bytes 1572864 | tf_op jit(solution)/shard_map/convert_element_type | solution.py:154
  2.1 3.8 %collective-permute-start = (bf16[128,2048]{1,0:T(8,128)(2,1)S(1)}, bf16[128,2048]{1,0:T(8,128)(2,1)S(1)}, u32[]{:S(2)}, u32[]{:S(2)}) collective-permute-start(bf16[128,2048]{1,0:T(8,128)(2,1)S(1)} %fusion), channel_id=1, source_target_pairs={{0,4},{4,8},{8,12},{12,16},{16,20},{20,24},{24,28},{28,32},{32,36}... | collective-permute-start | bytes 1572872 | tf_op jit(solution)/shard_map/ppermute | solution.py:19
  5.9 0.0 copy-done
  5.9 1.2 %fusion.1 = bf16[128,2048]{1,0:T(8,128)(2,1)S(1)} fusion(bf16[1,256,2048]{2,1,0:T(8,128)(2,1)S(1)} %copy-done, bf16[1,256,2048]{2,1,0:T(8,128)(2,1)} %param.9), kind=kLoop, calls=%fused_computation.3 | loop fusion | flops 1048576 | bytes 1572864 | tf_op jit(solution)/shard_map/convert_element_type | solution.py:155
  7.1 2.0 %collective-permute-start.1 = (bf16[128,2048]{1,0:T(8,128)(2,1)S(1)}, bf16[128,2048]{1,0:T(8,128)(2,1)S(1)}, u32[]{:S(2)}, u32[]{:S(2)}) collective-permute-start(bf16[128,2048]{1,0:T(8,128)(2,1)S(1)} %fusion.1), channel_id=1, source_target_pairs={{4,0},{8,4},{12,8},{16,12},{20,16},{24,20},{28,24},{32,28},{36,32}... | collective-permute-start | bytes 1572872 | tf_op jit(solution)/shard_map/ppermute | solution.py:19
  9.2 0.1 iota_add_fusion.1
  9.2 0.1 iota_add_fusion
  9.3 0.1 fusion.6
  9.4 0.0 copy-start.5
  9.4 0.6 copy-done.5
  10.1 0.1 copy.13
  10.2 0.1 reduce-window.8
  10.3 0.1 reduce
  10.4 0.1 select_reduce_fusion
  10.5 0.1 and_convert_fusion.1.m_ref
  10.6 0.0 copy-start.1
  10.6 0.0 copy-start.4
  10.7 0.7 copy-done.4
  11.4 0.1 rev.9
  11.5 0.7 concatenate.7.fq_ref
  12.2 0.1 pad.3.clone
  12.3 0.0 copy-done.1
  12.3 1.3 %rev.10.mr_ref = bf16[2,128,256]{2,1,0:T(8,128)(2,1)} reverse(bf16[2,128,256]{2,1,0:T(8,128)(2,1)S(1)} %slice.28), dimensions={1} | reverse | bytes 262144 | tf_op jit(solution)/shard_map/rev | solution.py:90
  13.6 0.7 maximum_maximum_fusion.fp_ref
  14.3 0.9 and_convert_fusion.mt_ref
  15.2 2.4 %collective-permute-done.prev_ref = bf16[128,2048]{1,0:T(8,128)(2,1)S(1)} collective-permute-done((bf16[128,2048]{1,0:T(8,128)(2,1)S(1)}, bf16[128,2048]{1,0:T(8,128)(2,1)S(1)}, u32[]{:S(2)}, u32[]{:S(2)}) %collective-permute-start) | collective-permute-done | bytes 524320 | tf_op jit(solution)/shard_map/ppermute | solution.py:19
  17.6 0.0 copy-start.2
  17.6 4.9 %collective-permute-done.1.next_ref = bf16[128,2048]{1,0:T(8,128)(2,1)S(1)} collective-permute-done((bf16[128,2048]{1,0:T(8,128)(2,1)S(1)}, bf16[128,2048]{1,0:T(8,128)(2,1)S(1)}, u32[]{:S(2)}, u32[]{:S(2)}) %collective-permute-start.1) | collective-permute-done | bytes 524320 | tf_op jit(solution)/shard_map/ppermute | solution.py:19
  22.5 0.0 copy-start.3
  22.5 0.0 copy-done.2
  22.5 0.8 copy-done.3
  23.3 22.5 %shard_map.101 = (bf16[256,2048]{1,0:T(8,128)(2,1)}, bf16[256,2048]{1,0:T(8,128)(2,1)}, bf16[256,2048]{1,0:T(8,128)(2,1)}, bf16[256,2048]{1,0:T(8,128)(2,1)}, f32[16,8,256]{2,1,0:T(8,128)}) custom-call(bf16[256,2048]{1,0:T(8,128)(2,1)} %bitcast.17, bf16[256,2048]{1,0:T(8,128)(2,1)} %bitcast.18, bf16[256,2048]{1,0:T(8,128)(2,1)} %bitcast.19, ...), custom_call_target="tpu_custom_call" | custom-call | tf_op jit(solution)/shard_map/pallas_call | solution.py:102
  45.8 0.8 slice.29
  46.7 0.1 rev.11
  46.7 0.1 collective-permute-start.2
  46.8 1.2 %collective-permute-done.2 = f32[128,128]{1,0:T(8,128)S(1)} collective-permute-done((f32[128,128]{1,0:T(8,128)S(1)}, f32[128,128]{1,0:T(8,128)S(1)}, u32[]{:S(2)}, u32[]{:S(2)}) %collective-permute-start.2) | collective-permute-done | bytes 65568 | tf_op jit(solution)/shard_map/ppermute | solution.py:25
  48.1 0.2 collective-permute-start.3
  48.3 4.2 %collective-permute-done.3 = f32[128,128]{1,0:T(8,128)S(1)} collective-permute-done((f32[128,128]{1,0:T(8,128)S(1)}, f32[128,128]{1,0:T(8,128)S(1)}, u32[]{:S(2)}, u32[]{:S(2)}) %collective-permute-start.3) | collective-permute-done | bytes 65568 | tf_op jit(solution)/shard_map/ppermute | solution.py:25
  52.4 5.6 %collective-permute-start.4 = (f32[128,128]{1,0:T(8,128)S(1)}, f32[128,128]{1,0:T(8,128)S(1)}, u32[]{:S(2)}, u32[]{:S(2)}) collective-permute-start(f32[128,128]{1,0:T(8,128)S(1)} %add.111), channel_id=1, source_target_pairs={{0,8},{4,12},{8,0},{12,4},{16,24},{20,28},{24,16},{28,20},{32,40},... | collective-permute-start | bytes 196616 | tf_op jit(solution)/shard_map/ppermute | solution.py:25
  58.0 2.2 %collective-permute-done.4 = f32[128,128]{1,0:T(8,128)S(1)} collective-permute-done((f32[128,128]{1,0:T(8,128)S(1)}, f32[128,128]{1,0:T(8,128)S(1)}, u32[]{:S(2)}, u32[]{:S(2)}) %collective-permute-start.4) | collective-permute-done | bytes 65568 | tf_op jit(solution)/shard_map/ppermute | solution.py:25
  60.3 2.8 %collective-permute-start.5 = (f32[128,128]{1,0:T(8,128)S(1)}, f32[128,128]{1,0:T(8,128)S(1)}, u32[]{:S(2)}, u32[]{:S(2)}) collective-permute-start(f32[128,128]{1,0:T(8,128)S(1)} %add.112), channel_id=1, source_target_pairs={{0,28},{4,24},{8,20},{12,16},{16,12},{20,8},{24,4},{28,0},{32,60},... | collective-permute-start | bytes 196616 | tf_op jit(solution)/shard_map/ppermute | solution.py:25
  63.1 4.5 %collective-permute-done.5 = f32[128,128]{1,0:T(8,128)S(1)} collective-permute-done((f32[128,128]{1,0:T(8,128)S(1)}, f32[128,128]{1,0:T(8,128)S(1)}, u32[]{:S(2)}, u32[]{:S(2)}) %collective-permute-start.5) | collective-permute-done | bytes 65568 | tf_op jit(solution)/shard_map/ppermute | solution.py:25
  67.7 1.7 %collective-permute-start.6 = (f32[128,128]{1,0:T(8,128)S(1)}, f32[128,128]{1,0:T(8,128)S(1)}, u32[]{:S(2)}, u32[]{:S(2)}) collective-permute-start(f32[128,128]{1,0:T(8,128)S(1)} %add.113), channel_id=1, source_target_pairs={{0,32},{4,36},{8,40},{12,44},{16,48},{20,52},{24,56},{28,60},{32,0... | collective-permute-start | bytes 196616 | tf_op jit(solution)/shard_map/ppermute | solution.py:25
  69.3 2.7 %collective-permute-done.6 = f32[128,128]{1,0:T(8,128)S(1)} collective-permute-done((f32[128,128]{1,0:T(8,128)S(1)}, f32[128,128]{1,0:T(8,128)S(1)}, u32[]{:S(2)}, u32[]{:S(2)}) %collective-permute-start.6) | collective-permute-done | bytes 65568 | tf_op jit(solution)/shard_map/ppermute | solution.py:25
  72.0 3.1 %collective-permute-start.7 = (f32[128,128]{1,0:T(8,128)S(1)}, f32[128,128]{1,0:T(8,128)S(1)}, u32[]{:S(2)}, u32[]{:S(2)}) collective-permute-start(f32[128,128]{1,0:T(8,128)S(1)} %add.114), channel_id=1, source_target_pairs={{0,96},{4,100},{8,104},{12,108},{16,112},{20,116},{24,120},{28,124... | collective-permute-start | bytes 196616 | tf_op jit(solution)/shard_map/ppermute | solution.py:25
  75.1 2.5 %collective-permute-done.7 = f32[128,128]{1,0:T(8,128)S(1)} collective-permute-done((f32[128,128]{1,0:T(8,128)S(1)}, f32[128,128]{1,0:T(8,128)S(1)}, u32[]{:S(2)}, u32[]{:S(2)}) %collective-permute-start.7) | collective-permute-done | bytes 65568 | tf_op jit(solution)/shard_map/ppermute | solution.py:25
  77.6 0.6 multiply_reduce_fusion
  78.2 1.5 %collective-permute-start.8 = (f32[]{:T(128)}, f32[]{:T(128)}, u32[]{:S(2)}, u32[]{:S(2)}) collective-permute-start(f32[]{:T(128)} %get-tuple-element.15), channel_id=1, source_target_pairs={{0,1},{1,0},{2,3},{3,2},{4,5},{5,4},{6,7},{7,6},{8,9},{9,8},{10,11... | collective-permute-start | bytes 20 | tf_op jit(solution)/shard_map/ppermute | solution.py:25
  79.7 2.3 %collective-permute-done.8 = f32[]{:T(128)} collective-permute-done((f32[]{:T(128)}, f32[]{:T(128)}, u32[]{:S(2)}, u32[]{:S(2)}) %collective-permute-start.8) | collective-permute-done | bytes 36 | tf_op jit(solution)/shard_map/ppermute | solution.py:25
  83.2 4.1 %collective-permute-start.9 = (f32[]{:T(128)}, f32[]{:T(128)}, u32[]{:S(2)}, u32[]{:S(2)}) collective-permute-start(f32[]{:T(128)} %add.116), channel_id=1, source_target_pairs={{0,3},{1,2},{2,1},{3,0},{4,7},{5,6},{6,5},{7,4},{8,11},{9,10},{10,... | collective-permute-start | bytes 20 | tf_op jit(solution)/shard_map/ppermute | solution.py:25
  87.4 0.8 collective-permute-done.9
  88.8 0.6 broadcast_multiply_fusion
  (12 shorter events, 0.1 us)
Async XLA Ops:
  0.6 5.3 %copy-start = (bf16[1,256,2048]{2,1,0:T(8,128)(2,1)S(1)}, bf16[1,256,2048]{2,1,0:T(8,128)(2,1)}, u32[]{:S(2)}) copy-start(bf16[1,256,2048]{2,1,0:T(8,128)(2,1)} %param.6) | copy-start | bytes 3145732
  2.1 15.6 %collective-permute-start = (bf16[128,2048]{1,0:T(8,128)(2,1)S(1)}, bf16[128,2048]{1,0:T(8,128)(2,1)S(1)}, u32[]{:S(2)}, u32[]{:S(2)}) collective-permute-start(bf16[128,2048]{1,0:T(8,128)(2,1)S(1)} %fusion), channel_id=1, source_target_pairs={{0,4},{4,8},{8,12},{12,16},{16,20},{20,24},{24,28},{28,32},{32,36}... | collective-permute-start | bytes 1572872 | tf_op jit(solution)/shard_map/ppermute | solution.py:19
  7.1 15.5 %collective-permute-start.1 = (bf16[128,2048]{1,0:T(8,128)(2,1)S(1)}, bf16[128,2048]{1,0:T(8,128)(2,1)S(1)}, u32[]{:S(2)}, u32[]{:S(2)}) collective-permute-start(bf16[128,2048]{1,0:T(8,128)(2,1)S(1)} %fusion.1), channel_id=1, source_target_pairs={{4,0},{8,4},{12,8},{16,12},{20,16},{24,20},{28,24},{32,28},{36,32}... | collective-permute-start | bytes 1572872 | tf_op jit(solution)/shard_map/ppermute | solution.py:19
  9.4 0.7 copy-start.5
  10.6 1.6 %copy-start.1 = (bf16[3,128,256]{2,1,0:T(8,128)(2,1)}, bf16[3,128,256]{2,1,0:T(8,128)(2,1)S(1)}, u32[]{:S(2)}) copy-start(bf16[3,128,256]{2,1,0:T(8,128)(2,1)S(1)} %and_convert_fusion.1.m_ref) | copy-start | bytes 589828
  10.6 0.8 copy-start.4
  17.6 4.9 %copy-start.2 = (bf16[128,2048]{1,0:T(8,128)(2,1)}, bf16[128,2048]{1,0:T(8,128)(2,1)S(1)}, u32[]{:S(2)}) copy-start(bf16[128,2048]{1,0:T(8,128)(2,1)S(1)} %collective-permute-done.prev_ref) | copy-start | bytes 1572868
  22.5 0.8 copy-start.3
  46.7 1.3 %collective-permute-start.2 = (f32[128,128]{1,0:T(8,128)S(1)}, f32[128,128]{1,0:T(8,128)S(1)}, u32[]{:S(2)}, u32[]{:S(2)}) collective-permute-start(f32[128,128]{1,0:T(8,128)S(1)} %rev.11), channel_id=1, source_target_pairs={{0,128},{128,0},{1,129},{129,1},{2,130},{130,2},{3,131},{131,3},{4... | collective-permute-start | bytes 196616 | tf_op jit(solution)/shard_map/ppermute | solution.py:25
  48.1 4.4 %collective-permute-start.3 = (f32[128,128]{1,0:T(8,128)S(1)}, f32[128,128]{1,0:T(8,128)S(1)}, u32[]{:S(2)}, u32[]{:S(2)}) collective-permute-start(f32[128,128]{1,0:T(8,128)S(1)} %add.110), channel_id=1, source_target_pairs={{0,4},{4,0},{8,12},{12,8},{16,20},{20,16},{24,28},{28,24},{32,36},... | collective-permute-start | bytes 196616 | tf_op jit(solution)/shard_map/ppermute | solution.py:25
  52.4 7.8 %collective-permute-start.4 = (f32[128,128]{1,0:T(8,128)S(1)}, f32[128,128]{1,0:T(8,128)S(1)}, u32[]{:S(2)}, u32[]{:S(2)}) collective-permute-start(f32[128,128]{1,0:T(8,128)S(1)} %add.111), channel_id=1, source_target_pairs={{0,8},{4,12},{8,0},{12,4},{16,24},{20,28},{24,16},{28,20},{32,40},... | collective-permute-start | bytes 196616 | tf_op jit(solution)/shard_map/ppermute | solution.py:25
  60.3 7.4 %collective-permute-start.5 = (f32[128,128]{1,0:T(8,128)S(1)}, f32[128,128]{1,0:T(8,128)S(1)}, u32[]{:S(2)}, u32[]{:S(2)}) collective-permute-start(f32[128,128]{1,0:T(8,128)S(1)} %add.112), channel_id=1, source_target_pairs={{0,28},{4,24},{8,20},{12,16},{16,12},{20,8},{24,4},{28,0},{32,60},... | collective-permute-start | bytes 196616 | tf_op jit(solution)/shard_map/ppermute | solution.py:25
  67.7 4.4 %collective-permute-start.6 = (f32[128,128]{1,0:T(8,128)S(1)}, f32[128,128]{1,0:T(8,128)S(1)}, u32[]{:S(2)}, u32[]{:S(2)}) collective-permute-start(f32[128,128]{1,0:T(8,128)S(1)} %add.113), channel_id=1, source_target_pairs={{0,32},{4,36},{8,40},{12,44},{16,48},{20,52},{24,56},{28,60},{32,0... | collective-permute-start | bytes 196616 | tf_op jit(solution)/shard_map/ppermute | solution.py:25
  72.0 5.6 %collective-permute-start.7 = (f32[128,128]{1,0:T(8,128)S(1)}, f32[128,128]{1,0:T(8,128)S(1)}, u32[]{:S(2)}, u32[]{:S(2)}) collective-permute-start(f32[128,128]{1,0:T(8,128)S(1)} %add.114), channel_id=1, source_target_pairs={{0,96},{4,100},{8,104},{12,108},{16,112},{20,116},{24,120},{28,124... | collective-permute-start | bytes 196616 | tf_op jit(solution)/shard_map/ppermute | solution.py:25
  78.2 3.8 %collective-permute-start.8 = (f32[]{:T(128)}, f32[]{:T(128)}, u32[]{:S(2)}, u32[]{:S(2)}) collective-permute-start(f32[]{:T(128)} %get-tuple-element.15), channel_id=1, source_target_pairs={{0,1},{1,0},{2,3},{3,2},{4,5},{5,4},{6,7},{7,6},{8,9},{9,8},{10,11... | collective-permute-start | bytes 20 | tf_op jit(solution)/shard_map/ppermute | solution.py:25
  83.2 5.0 %collective-permute-start.9 = (f32[]{:T(128)}, f32[]{:T(128)}, u32[]{:S(2)}, u32[]{:S(2)}) collective-permute-start(f32[]{:T(128)} %add.116), channel_id=1, source_target_pairs={{0,3},{1,2},{2,1},{3,0},{4,7},{5,6},{6,5},{7,4},{8,11},{9,10},{10,... | collective-permute-start | bytes 20 | tf_op jit(solution)/shard_map/ppermute | solution.py:25

commit v10 on v9

--- a/solution.py
+++ b/solution.py
@@ -143,7 +143,7 @@
 def ctx_masks():
     inner = 8 if lax.axis_size("ctx") % 8 == 0 else 1
     outer = lax.axis_size("ctx") // inner
-    low = [1, 2, 7][: inner.bit_length() - 1]
+    low = [1, 2, 6][: inner.bit_length() - 1]
     return low + [m * inner for m in mirror_masks(outer)]
 
 

time: 89.8 us -> 89.6 us (level)
  waiting for transfers between devices: 27.8 us -> 26.8 us
    ppermute x8, waiting for transfers between devices: 20.5 us -> 19.5 us  [doubling_sum(): partner = lax.ppermute(value, axis, [(i, i ^ mask) for i in range(count)])]
where the time goes in v10:
time: 89.6 us; the launch traced here: 89.2 us
  waiting for transfers between devices  26.8 us (30%)
  starting transfers between devices  25.6 us (29%)
  Pallas kernels  22.5 us (25%)
  other arithmetic  6.22 us (7%)
  local copies, waits for them, and re-layouts  5.35 us (6%)
  between operations  2.63 us (3%)
    pallas_call x1, Pallas kernels, grouped_conv(): pl.pallas_call(conv_kernel, grid=(tiles,), in_specs=[tok, tok, tok, tok,...  22.5 us
    ppermute x8, starting transfers between devices, doubling_sum(): partner = lax.ppermute(value, axis, [(i, i ^ mask) for i in range(count)])  19.8 us
    ppermute x8, waiting for transfers between devices, doubling_sum(): partner = lax.ppermute(value, axis, [(i, i ^ mask) for i in range(count)])  19.5 us
    ppermute x2, waiting for transfers between devices, passed_along(): lax.ppermute(value, axis, [(source, source + steps) for source in range(i...  7.33 us
    ppermute x2, starting transfers between devices, passed_along(): lax.ppermute(value, axis, [(source, source + steps) for source in range(i...  5.87 us
    unnamed x12, local copies, waits for them, and re-layouts  2.18 us
  transfers between devices with their start and end apart: 10, of which 10 were waited for; matrix products, arithmetic and copies ran while one was open for 6% of the time, Pallas kernels for 0%

profile of v10, /device:TPU:32, one launch (start us, length us, event | category | flops | bytes accessed | tf_op | source)
XLA Modules:
  0.0 89.2 jit_solution(7919823611163273692)
XLA Ops:
  0.6 0.0 copy-start
  0.6 1.4 %fusion = bf16[128,2048]{1,0:T(8,128)(2,1)S(1)} fusion(bf16[1,256,2048]{2,1,0:T(8,128)(2,1)} %param.8, bf16[1,256,2048]{2,1,0:T(8,128)(2,1)} %param.7), kind=kLoop, calls=%fused_computation.2 | loop fusion | flops 1048576 | bytes 1572864 | tf_op jit(solution)/shard_map/convert_element_type | solution.py:154
  2.1 3.8 %collective-permute-start = (bf16[128,2048]{1,0:T(8,128)(2,1)S(1)}, bf16[128,2048]{1,0:T(8,128)(2,1)S(1)}, u32[]{:S(2)}, u32[]{:S(2)}) collective-permute-start(bf16[128,2048]{1,0:T(8,128)(2,1)S(1)} %fusion), channel_id=1, source_target_pairs={{0,4},{4,8},{8,12},{12,16},{16,20},{20,24},{24,28},{28,32},{32,36}... | collective-permute-start | bytes 1572872 | tf_op jit(solution)/shard_map/ppermute | solution.py:19
  5.9 0.0 copy-done
  5.9 1.2 %fusion.1 = bf16[128,2048]{1,0:T(8,128)(2,1)S(1)} fusion(bf16[1,256,2048]{2,1,0:T(8,128)(2,1)S(1)} %copy-done, bf16[1,256,2048]{2,1,0:T(8,128)(2,1)} %param.9), kind=kLoop, calls=%fused_computation.3 | loop fusion | flops 1048576 | bytes 1572864 | tf_op jit(solution)/shard_map/convert_element_type | solution.py:155
  7.1 2.0 %collective-permute-start.1 = (bf16[128,2048]{1,0:T(8,128)(2,1)S(1)}, bf16[128,2048]{1,0:T(8,128)(2,1)S(1)}, u32[]{:S(2)}, u32[]{:S(2)}) collective-permute-start(bf16[128,2048]{1,0:T(8,128)(2,1)S(1)} %fusion.1), channel_id=1, source_target_pairs={{4,0},{8,4},{12,8},{16,12},{20,16},{24,20},{28,24},{32,28},{36,32}... | collective-permute-start | bytes 1572872 | tf_op jit(solution)/shard_map/ppermute | solution.py:19
  9.2 0.1 iota_add_fusion.1
  9.2 0.1 iota_add_fusion
  9.3 0.1 fusion.6
  9.4 0.0 copy-start.5
  9.4 0.6 copy-done.5
  10.1 0.1 copy.13
  10.2 0.1 reduce-window.8
  10.3 0.1 reduce
  10.4 0.1 select_reduce_fusion
  10.5 0.1 and_convert_fusion.1.m_ref
  10.6 0.0 copy-start.1
  10.6 0.0 copy-start.4
  10.7 0.7 copy-done.4
  11.4 0.1 rev.9
  11.5 0.7 concatenate.7.fq_ref
  12.2 0.1 pad.3.clone
  12.3 0.0 copy-done.1
  12.3 1.3 %rev.10.mr_ref = bf16[2,128,256]{2,1,0:T(8,128)(2,1)} reverse(bf16[2,128,256]{2,1,0:T(8,128)(2,1)S(1)} %slice.28), dimensions={1} | reverse | bytes 262144 | tf_op jit(solution)/shard_map/rev | solution.py:90
  13.6 0.7 maximum_maximum_fusion.fp_ref
  14.3 0.9 and_convert_fusion.mt_ref
  15.2 2.4 %collective-permute-done.prev_ref = bf16[128,2048]{1,0:T(8,128)(2,1)S(1)} collective-permute-done((bf16[128,2048]{1,0:T(8,128)(2,1)S(1)}, bf16[128,2048]{1,0:T(8,128)(2,1)S(1)}, u32[]{:S(2)}, u32[]{:S(2)}) %collective-permute-start) | collective-permute-done | bytes 524320 | tf_op jit(solution)/shard_map/ppermute | solution.py:19
  17.6 0.0 copy-start.2
  17.6 4.9 %collective-permute-done.1.next_ref = bf16[128,2048]{1,0:T(8,128)(2,1)S(1)} collective-permute-done((bf16[128,2048]{1,0:T(8,128)(2,1)S(1)}, bf16[128,2048]{1,0:T(8,128)(2,1)S(1)}, u32[]{:S(2)}, u32[]{:S(2)}) %collective-permute-start.1) | collective-permute-done | bytes 524320 | tf_op jit(solution)/shard_map/ppermute | solution.py:19
  22.5 0.0 copy-start.3
  22.5 0.0 copy-done.2
  22.5 0.8 copy-done.3
  23.3 22.5 %shard_map.101 = (bf16[256,2048]{1,0:T(8,128)(2,1)}, bf16[256,2048]{1,0:T(8,128)(2,1)}, bf16[256,2048]{1,0:T(8,128)(2,1)}, bf16[256,2048]{1,0:T(8,128)(2,1)}, f32[16,8,256]{2,1,0:T(8,128)}) custom-call(bf16[256,2048]{1,0:T(8,128)(2,1)} %bitcast.17, bf16[256,2048]{1,0:T(8,128)(2,1)} %bitcast.18, bf16[256,2048]{1,0:T(8,128)(2,1)} %bitcast.19, ...), custom_call_target="tpu_custom_call" | custom-call | tf_op jit(solution)/shard_map/pallas_call | solution.py:102
  45.8 0.8 slice.29
  46.7 0.1 rev.11
  46.7 0.1 collective-permute-start.2
  46.8 1.2 %collective-permute-done.2 = f32[128,128]{1,0:T(8,128)S(1)} collective-permute-done((f32[128,128]{1,0:T(8,128)S(1)}, f32[128,128]{1,0:T(8,128)S(1)}, u32[]{:S(2)}, u32[]{:S(2)}) %collective-permute-start.2) | collective-permute-done | bytes 65568 | tf_op jit(solution)/shard_map/ppermute | solution.py:25
  48.1 0.2 collective-permute-start.3
  48.3 4.2 %collective-permute-done.3 = f32[128,128]{1,0:T(8,128)S(1)} collective-permute-done((f32[128,128]{1,0:T(8,128)S(1)}, f32[128,128]{1,0:T(8,128)S(1)}, u32[]{:S(2)}, u32[]{:S(2)}) %collective-permute-start.3) | collective-permute-done | bytes 65568 | tf_op jit(solution)/shard_map/ppermute | solution.py:25
  52.4 5.6 %collective-permute-start.4 = (f32[128,128]{1,0:T(8,128)S(1)}, f32[128,128]{1,0:T(8,128)S(1)}, u32[]{:S(2)}, u32[]{:S(2)}) collective-permute-start(f32[128,128]{1,0:T(8,128)S(1)} %add.111), channel_id=1, source_target_pairs={{0,8},{4,12},{8,0},{12,4},{16,24},{20,28},{24,16},{28,20},{32,40},... | collective-permute-start | bytes 196616 | tf_op jit(solution)/shard_map/ppermute | solution.py:25
  58.0 2.2 %collective-permute-done.4 = f32[128,128]{1,0:T(8,128)S(1)} collective-permute-done((f32[128,128]{1,0:T(8,128)S(1)}, f32[128,128]{1,0:T(8,128)S(1)}, u32[]{:S(2)}, u32[]{:S(2)}) %collective-permute-start.4) | collective-permute-done | bytes 65568 | tf_op jit(solution)/shard_map/ppermute | solution.py:25
  60.3 3.5 %collective-permute-start.5 = (f32[128,128]{1,0:T(8,128)S(1)}, f32[128,128]{1,0:T(8,128)S(1)}, u32[]{:S(2)}, u32[]{:S(2)}) collective-permute-start(f32[128,128]{1,0:T(8,128)S(1)} %add.112), channel_id=1, source_target_pairs={{0,24},{4,28},{8,16},{12,20},{16,8},{20,12},{24,0},{28,4},{32,56},... | collective-permute-start | bytes 196616 | tf_op jit(solution)/shard_map/ppermute | solution.py:25
  63.8 3.6 %collective-permute-done.5 = f32[128,128]{1,0:T(8,128)S(1)} collective-permute-done((f32[128,128]{1,0:T(8,128)S(1)}, f32[128,128]{1,0:T(8,128)S(1)}, u32[]{:S(2)}, u32[]{:S(2)}) %collective-permute-start.5) | collective-permute-done | bytes 65568 | tf_op jit(solution)/shard_map/ppermute | solution.py:25
  67.4 1.7 %collective-permute-start.6 = (f32[128,128]{1,0:T(8,128)S(1)}, f32[128,128]{1,0:T(8,128)S(1)}, u32[]{:S(2)}, u32[]{:S(2)}) collective-permute-start(f32[128,128]{1,0:T(8,128)S(1)} %add.113), channel_id=1, source_target_pairs={{0,32},{4,36},{8,40},{12,44},{16,48},{20,52},{24,56},{28,60},{32,0... | collective-permute-start | bytes 196616 | tf_op jit(solution)/shard_map/ppermute | solution.py:25
  69.0 2.7 %collective-permute-done.6 = f32[128,128]{1,0:T(8,128)S(1)} collective-permute-done((f32[128,128]{1,0:T(8,128)S(1)}, f32[128,128]{1,0:T(8,128)S(1)}, u32[]{:S(2)}, u32[]{:S(2)}) %collective-permute-start.6) | collective-permute-done | bytes 65568 | tf_op jit(solution)/shard_map/ppermute | solution.py:25
  71.7 3.1 %collective-permute-start.7 = (f32[128,128]{1,0:T(8,128)S(1)}, f32[128,128]{1,0:T(8,128)S(1)}, u32[]{:S(2)}, u32[]{:S(2)}) collective-permute-start(f32[128,128]{1,0:T(8,128)S(1)} %add.114), channel_id=1, source_target_pairs={{0,96},{4,100},{8,104},{12,108},{16,112},{20,116},{24,120},{28,124... | collective-permute-start | bytes 196616 | tf_op jit(solution)/shard_map/ppermute | solution.py:25
  74.8 2.5 %collective-permute-done.7 = f32[128,128]{1,0:T(8,128)S(1)} collective-permute-done((f32[128,128]{1,0:T(8,128)S(1)}, f32[128,128]{1,0:T(8,128)S(1)}, u32[]{:S(2)}, u32[]{:S(2)}) %collective-permute-start.7) | collective-permute-done | bytes 65568 | tf_op jit(solution)/shard_map/ppermute | solution.py:25
  77.3 0.6 multiply_reduce_fusion
  77.9 1.5 %collective-permute-start.8 = (f32[]{:T(128)}, f32[]{:T(128)}, u32[]{:S(2)}, u32[]{:S(2)}) collective-permute-start(f32[]{:T(128)} %get-tuple-element.15), channel_id=1, source_target_pairs={{0,1},{1,0},{2,3},{3,2},{4,5},{5,4},{6,7},{7,6},{8,9},{9,8},{10,11... | collective-permute-start | bytes 20 | tf_op jit(solution)/shard_map/ppermute | solution.py:25
  79.4 2.3 %collective-permute-done.8 = f32[]{:T(128)} collective-permute-done((f32[]{:T(128)}, f32[]{:T(128)}, u32[]{:S(2)}, u32[]{:S(2)}) %collective-permute-start.8) | collective-permute-done | bytes 36 | tf_op jit(solution)/shard_map/ppermute | solution.py:25
  82.9 4.1 %collective-permute-start.9 = (f32[]{:T(128)}, f32[]{:T(128)}, u32[]{:S(2)}, u32[]{:S(2)}) collective-permute-start(f32[]{:T(128)} %add.116), channel_id=1, source_target_pairs={{0,3},{1,2},{2,1},{3,0},{4,7},{5,6},{6,5},{7,4},{8,11},{9,10},{10,... | collective-permute-start | bytes 20 | tf_op jit(solution)/shard_map/ppermute | solution.py:25
  87.1 0.8 collective-permute-done.9
  88.5 0.6 broadcast_multiply_fusion
  (12 shorter events, 0.1 us)
Async XLA Ops:
  0.6 5.3 %copy-start = (bf16[1,256,2048]{2,1,0:T(8,128)(2,1)S(1)}, bf16[1,256,2048]{2,1,0:T(8,128)(2,1)}, u32[]{:S(2)}) copy-start(bf16[1,256,2048]{2,1,0:T(8,128)(2,1)} %param.6) | copy-start | bytes 3145732
  2.1 15.6 %collective-permute-start = (bf16[128,2048]{1,0:T(8,128)(2,1)S(1)}, bf16[128,2048]{1,0:T(8,128)(2,1)S(1)}, u32[]{:S(2)}, u32[]{:S(2)}) collective-permute-start(bf16[128,2048]{1,0:T(8,128)(2,1)S(1)} %fusion), channel_id=1, source_target_pairs={{0,4},{4,8},{8,12},{12,16},{16,20},{20,24},{24,28},{28,32},{32,36}... | collective-permute-start | bytes 1572872 | tf_op jit(solution)/shard_map/ppermute | solution.py:19
  7.1 15.5 %collective-permute-start.1 = (bf16[128,2048]{1,0:T(8,128)(2,1)S(1)}, bf16[128,2048]{1,0:T(8,128)(2,1)S(1)}, u32[]{:S(2)}, u32[]{:S(2)}) collective-permute-start(bf16[128,2048]{1,0:T(8,128)(2,1)S(1)} %fusion.1), channel_id=1, source_target_pairs={{4,0},{8,4},{12,8},{16,12},{20,16},{24,20},{28,24},{32,28},{36,32}... | collective-permute-start | bytes 1572872 | tf_op jit(solution)/shard_map/ppermute | solution.py:19
  9.4 0.7 copy-start.5
  10.6 1.6 %copy-start.1 = (bf16[3,128,256]{2,1,0:T(8,128)(2,1)}, bf16[3,128,256]{2,1,0:T(8,128)(2,1)S(1)}, u32[]{:S(2)}) copy-start(bf16[3,128,256]{2,1,0:T(8,128)(2,1)S(1)} %and_convert_fusion.1.m_ref) | copy-start | bytes 589828
  10.6 0.8 copy-start.4
  17.6 4.9 %copy-start.2 = (bf16[128,2048]{1,0:T(8,128)(2,1)}, bf16[128,2048]{1,0:T(8,128)(2,1)S(1)}, u32[]{:S(2)}) copy-start(bf16[128,2048]{1,0:T(8,128)(2,1)S(1)} %collective-permute-done.prev_ref) | copy-start | bytes 1572868
  22.5 0.8 copy-start.3
  46.7 1.3 %collective-permute-start.2 = (f32[128,128]{1,0:T(8,128)S(1)}, f32[128,128]{1,0:T(8,128)S(1)}, u32[]{:S(2)}, u32[]{:S(2)}) collective-permute-start(f32[128,128]{1,0:T(8,128)S(1)} %rev.11), channel_id=1, source_target_pairs={{0,128},{128,0},{1,129},{129,1},{2,130},{130,2},{3,131},{131,3},{4... | collective-permute-start | bytes 196616 | tf_op jit(solution)/shard_map/ppermute | solution.py:25
  48.1 4.4 %collective-permute-start.3 = (f32[128,128]{1,0:T(8,128)S(1)}, f32[128,128]{1,0:T(8,128)S(1)}, u32[]{:S(2)}, u32[]{:S(2)}) collective-permute-start(f32[128,128]{1,0:T(8,128)S(1)} %add.110), channel_id=1, source_target_pairs={{0,4},{4,0},{8,12},{12,8},{16,20},{20,16},{24,28},{28,24},{32,36},... | collective-permute-start | bytes 196616 | tf_op jit(solution)/shard_map/ppermute | solution.py:25
  52.4 7.8 %collective-permute-start.4 = (f32[128,128]{1,0:T(8,128)S(1)}, f32[128,128]{1,0:T(8,128)S(1)}, u32[]{:S(2)}, u32[]{:S(2)}) collective-permute-start(f32[128,128]{1,0:T(8,128)S(1)} %add.111), channel_id=1, source_target_pairs={{0,8},{4,12},{8,0},{12,4},{16,24},{20,28},{24,16},{28,20},{32,40},... | collective-permute-start | bytes 196616 | tf_op jit(solution)/shard_map/ppermute | solution.py:25
  60.3 7.1 %collective-permute-start.5 = (f32[128,128]{1,0:T(8,128)S(1)}, f32[128,128]{1,0:T(8,128)S(1)}, u32[]{:S(2)}, u32[]{:S(2)}) collective-permute-start(f32[128,128]{1,0:T(8,128)S(1)} %add.112), channel_id=1, source_target_pairs={{0,24},{4,28},{8,16},{12,20},{16,8},{20,12},{24,0},{28,4},{32,56},... | collective-permute-start | bytes 196616 | tf_op jit(solution)/shard_map/ppermute | solution.py:25
  67.4 4.4 %collective-permute-start.6 = (f32[128,128]{1,0:T(8,128)S(1)}, f32[128,128]{1,0:T(8,128)S(1)}, u32[]{:S(2)}, u32[]{:S(2)}) collective-permute-start(f32[128,128]{1,0:T(8,128)S(1)} %add.113), channel_id=1, source_target_pairs={{0,32},{4,36},{8,40},{12,44},{16,48},{20,52},{24,56},{28,60},{32,0... | collective-permute-start | bytes 196616 | tf_op jit(solution)/shard_map/ppermute | solution.py:25
  71.7 5.6 %collective-permute-start.7 = (f32[128,128]{1,0:T(8,128)S(1)}, f32[128,128]{1,0:T(8,128)S(1)}, u32[]{:S(2)}, u32[]{:S(2)}) collective-permute-start(f32[128,128]{1,0:T(8,128)S(1)} %add.114), channel_id=1, source_target_pairs={{0,96},{4,100},{8,104},{12,108},{16,112},{20,116},{24,120},{28,124... | collective-permute-start | bytes 196616 | tf_op jit(solution)/shard_map/ppermute | solution.py:25
  77.9 3.8 %collective-permute-start.8 = (f32[]{:T(128)}, f32[]{:T(128)}, u32[]{:S(2)}, u32[]{:S(2)}) collective-permute-start(f32[]{:T(128)} %get-tuple-element.15), channel_id=1, source_target_pairs={{0,1},{1,0},{2,3},{3,2},{4,5},{5,4},{6,7},{7,6},{8,9},{9,8},{10,11... | collective-permute-start | bytes 20 | tf_op jit(solution)/shard_map/ppermute | solution.py:25
  82.9 5.0 %collective-permute-start.9 = (f32[]{:T(128)}, f32[]{:T(128)}, u32[]{:S(2)}, u32[]{:S(2)}) collective-permute-start(f32[]{:T(128)} %add.116), channel_id=1, source_target_pairs={{0,3},{1,2},{2,1},{3,0},{4,7},{5,6},{6,5},{7,4},{8,11},{9,10},{10,... | collective-permute-start | bytes 20 | tf_op jit(solution)/shard_map/ppermute | solution.py:25

commit v11 on v10

--- a/solution.py
+++ b/solution.py
@@ -144,7 +144,7 @@
     inner = 8 if lax.axis_size("ctx") % 8 == 0 else 1
     outer = lax.axis_size("ctx") // inner
     low = [1, 2, 6][: inner.bit_length() - 1]
-    return low + [m * inner for m in mirror_masks(outer)]
+    return [m * inner for m in mirror_masks(outer)] + low
 
 
 def on_device(query_in, key_in, value_in, grad_out, seq_lengths, filters):

time: 89.6 us -> 89.4 us (level)
  waiting for transfers between devices: 26.8 us -> 25 us
  starting transfers between devices: 25.6 us -> 27.3 us
    ppermute x8, waiting for transfers between devices: 19.5 us -> 17.6 us  [doubling_sum(): partner = lax.ppermute(value, axis, [(i, i ^ mask) for i in range(count)])]
    ppermute x8, starting transfers between devices: 19.8 us -> 21.4 us  [doubling_sum(): partner = lax.ppermute(value, axis, [(i, i ^ mask) for i in range(count)])]
where the time goes in v11:
time: 89.4 us; the launch traced here: 88.9 us
  starting transfers between devices  27.3 us (31%)
  waiting for transfers between devices  25 us (28%)
  Pallas kernels  22.5 us (25%)
  other arithmetic  6.22 us (7%)
  local copies, waits for them, and re-layouts  5.35 us (6%)
  between operations  2.63 us (3%)
    pallas_call x1, Pallas kernels, grouped_conv(): pl.pallas_call(conv_kernel, grid=(tiles,), in_specs=[tok, tok, tok, tok,...  22.5 us
    ppermute x8, starting transfers between devices, doubling_sum(): partner = lax.ppermute(value, axis, [(i, i ^ mask) for i in range(count)])  21.4 us
    ppermute x8, waiting for transfers between devices, doubling_sum(): partner = lax.ppermute(value, axis, [(i, i ^ mask) for i in range(count)])  17.6 us
    ppermute x2, waiting for transfers between devices, passed_along(): lax.ppermute(value, axis, [(source, source + steps) for source in range(i...  7.33 us
    ppermute x2, starting transfers between devices, passed_along(): lax.ppermute(value, axis, [(source, source + steps) for source in range(i...  5.87 us
    unnamed x12, local copies, waits for them, and re-layouts  2.18 us
  transfers between devices with their start and end apart: 10, of which 10 were waited for; matrix products, arithmetic and copies ran while one was open for 6% of the time, Pallas kernels for 0%

profile of v11, /device:TPU:32, one launch (start us, length us, event | category | flops | bytes accessed | tf_op | source)
XLA Modules:
  0.0 88.9 jit_solution(10438213252208866060)
XLA Ops:
  0.6 0.0 copy-start
  0.6 1.4 %fusion = bf16[128,2048]{1,0:T(8,128)(2,1)S(1)} fusion(bf16[1,256,2048]{2,1,0:T(8,128)(2,1)} %param.8, bf16[1,256,2048]{2,1,0:T(8,128)(2,1)} %param.7), kind=kLoop, calls=%fused_computation.2 | loop fusion | flops 1048576 | bytes 1572864 | tf_op jit(solution)/shard_map/convert_element_type | solution.py:154
  2.1 3.8 %collective-permute-start = (bf16[128,2048]{1,0:T(8,128)(2,1)S(1)}, bf16[128,2048]{1,0:T(8,128)(2,1)S(1)}, u32[]{:S(2)}, u32[]{:S(2)}) collective-permute-start(bf16[128,2048]{1,0:T(8,128)(2,1)S(1)} %fusion), channel_id=1, source_target_pairs={{0,4},{4,8},{8,12},{12,16},{16,20},{20,24},{24,28},{28,32},{32,36}... | collective-permute-start | bytes 1572872 | tf_op jit(solution)/shard_map/ppermute | solution.py:19
  5.9 0.0 copy-done
  5.9 1.2 %fusion.1 = bf16[128,2048]{1,0:T(8,128)(2,1)S(1)} fusion(bf16[1,256,2048]{2,1,0:T(8,128)(2,1)S(1)} %copy-done, bf16[1,256,2048]{2,1,0:T(8,128)(2,1)} %param.9), kind=kLoop, calls=%fused_computation.3 | loop fusion | flops 1048576 | bytes 1572864 | tf_op jit(solution)/shard_map/convert_element_type | solution.py:155
  7.1 2.0 %collective-permute-start.1 = (bf16[128,2048]{1,0:T(8,128)(2,1)S(1)}, bf16[128,2048]{1,0:T(8,128)(2,1)S(1)}, u32[]{:S(2)}, u32[]{:S(2)}) collective-permute-start(bf16[128,2048]{1,0:T(8,128)(2,1)S(1)} %fusion.1), channel_id=1, source_target_pairs={{4,0},{8,4},{12,8},{16,12},{20,16},{24,20},{28,24},{32,28},{36,32}... | collective-permute-start | bytes 1572872 | tf_op jit(solution)/shard_map/ppermute | solution.py:19
  9.2 0.1 iota_add_fusion.1
  9.2 0.1 iota_add_fusion
  9.3 0.1 fusion.6
  9.4 0.0 copy-start.5
  9.4 0.6 copy-done.5
  10.1 0.1 copy.13
  10.2 0.1 reduce-window.8
  10.3 0.1 reduce
  10.4 0.1 select_reduce_fusion
  10.5 0.1 and_convert_fusion.1.m_ref
  10.6 0.0 copy-start.1
  10.6 0.0 copy-start.4
  10.7 0.7 copy-done.4
  11.4 0.1 rev.9
  11.5 0.7 concatenate.7.fq_ref
  12.2 0.1 pad.3.clone
  12.3 0.0 copy-done.1
  12.3 1.3 %rev.10.mr_ref = bf16[2,128,256]{2,1,0:T(8,128)(2,1)} reverse(bf16[2,128,256]{2,1,0:T(8,128)(2,1)S(1)} %slice.28), dimensions={1} | reverse | bytes 262144 | tf_op jit(solution)/shard_map/rev | solution.py:90
  13.6 0.7 maximum_maximum_fusion.fp_ref
  14.3 0.9 and_convert_fusion.mt_ref
  15.2 2.4 %collective-permute-done.prev_ref = bf16[128,2048]{1,0:T(8,128)(2,1)S(1)} collective-permute-done((bf16[128,2048]{1,0:T(8,128)(2,1)S(1)}, bf16[128,2048]{1,0:T(8,128)(2,1)S(1)}, u32[]{:S(2)}, u32[]{:S(2)}) %collective-permute-start) | collective-permute-done | bytes 524320 | tf_op jit(solution)/shard_map/ppermute | solution.py:19
  17.6 0.0 copy-start.2
  17.6 4.9 %collective-permute-done.1.next_ref = bf16[128,2048]{1,0:T(8,128)(2,1)S(1)} collective-permute-done((bf16[128,2048]{1,0:T(8,128)(2,1)S(1)}, bf16[128,2048]{1,0:T(8,128)(2,1)S(1)}, u32[]{:S(2)}, u32[]{:S(2)}) %collective-permute-start.1) | collective-permute-done | bytes 524320 | tf_op jit(solution)/shard_map/ppermute | solution.py:19
  22.5 0.0 copy-start.3
  22.5 0.0 copy-done.2
  22.5 0.8 copy-done.3
  23.3 22.5 %shard_map.101 = (bf16[256,2048]{1,0:T(8,128)(2,1)}, bf16[256,2048]{1,0:T(8,128)(2,1)}, bf16[256,2048]{1,0:T(8,128)(2,1)}, bf16[256,2048]{1,0:T(8,128)(2,1)}, f32[16,8,256]{2,1,0:T(8,128)}) custom-call(bf16[256,2048]{1,0:T(8,128)(2,1)} %bitcast.17, bf16[256,2048]{1,0:T(8,128)(2,1)} %bitcast.18, bf16[256,2048]{1,0:T(8,128)(2,1)} %bitcast.19, ...), custom_call_target="tpu_custom_call" | custom-call | tf_op jit(solution)/shard_map/pallas_call | solution.py:102
  45.8 0.8 slice.29
  46.7 0.1 rev.11
  46.7 0.1 collective-permute-start.2
  46.8 1.2 %collective-permute-done.2 = f32[128,128]{1,0:T(8,128)S(1)} collective-permute-done((f32[128,128]{1,0:T(8,128)S(1)}, f32[128,128]{1,0:T(8,128)S(1)}, u32[]{:S(2)}, u32[]{:S(2)}) %collective-permute-start.2) | collective-permute-done | bytes 65568 | tf_op jit(solution)/shard_map/ppermute | solution.py:25
  48.1 1.7 %collective-permute-start.3 = (f32[128,128]{1,0:T(8,128)S(1)}, f32[128,128]{1,0:T(8,128)S(1)}, u32[]{:S(2)}, u32[]{:S(2)}) collective-permute-start(f32[128,128]{1,0:T(8,128)S(1)} %add.110), channel_id=1, source_target_pairs={{0,32},{4,36},{8,40},{12,44},{16,48},{20,52},{24,56},{28,60},{32,0... | collective-permute-start | bytes 196616 | tf_op jit(solution)/shard_map/ppermute | solution.py:25
  49.7 2.7 %collective-permute-done.3 = f32[128,128]{1,0:T(8,128)S(1)} collective-permute-done((f32[128,128]{1,0:T(8,128)S(1)}, f32[128,128]{1,0:T(8,128)S(1)}, u32[]{:S(2)}, u32[]{:S(2)}) %collective-permute-start.3) | collective-permute-done | bytes 65568 | tf_op jit(solution)/shard_map/ppermute | solution.py:25
  52.4 3.1 %collective-permute-start.4 = (f32[128,128]{1,0:T(8,128)S(1)}, f32[128,128]{1,0:T(8,128)S(1)}, u32[]{:S(2)}, u32[]{:S(2)}) collective-permute-start(f32[128,128]{1,0:T(8,128)S(1)} %add.111), channel_id=1, source_target_pairs={{0,96},{4,100},{8,104},{12,108},{16,112},{20,116},{24,120},{28,124... | collective-permute-start | bytes 196616 | tf_op jit(solution)/shard_map/ppermute | solution.py:25
  55.5 2.5 %collective-permute-done.4 = f32[128,128]{1,0:T(8,128)S(1)} collective-permute-done((f32[128,128]{1,0:T(8,128)S(1)}, f32[128,128]{1,0:T(8,128)S(1)}, u32[]{:S(2)}, u32[]{:S(2)}) %collective-permute-start.4) | collective-permute-done | bytes 65568 | tf_op jit(solution)/shard_map/ppermute | solution.py:25
  58.0 1.7 %collective-permute-start.5 = (f32[128,128]{1,0:T(8,128)S(1)}, f32[128,128]{1,0:T(8,128)S(1)}, u32[]{:S(2)}, u32[]{:S(2)}) collective-permute-start(f32[128,128]{1,0:T(8,128)S(1)} %add.112), channel_id=1, source_target_pairs={{0,4},{4,0},{8,12},{12,8},{16,20},{20,16},{24,28},{28,24},{32,36},... | collective-permute-start | bytes 196616 | tf_op jit(solution)/shard_map/ppermute | solution.py:25
  59.7 2.6 %collective-permute-done.5 = f32[128,128]{1,0:T(8,128)S(1)} collective-permute-done((f32[128,128]{1,0:T(8,128)S(1)}, f32[128,128]{1,0:T(8,128)S(1)}, u32[]{:S(2)}, u32[]{:S(2)}) %collective-permute-start.5) | collective-permute-done | bytes 65568 | tf_op jit(solution)/shard_map/ppermute | solution.py:25
  62.4 5.6 %collective-permute-start.6 = (f32[128,128]{1,0:T(8,128)S(1)}, f32[128,128]{1,0:T(8,128)S(1)}, u32[]{:S(2)}, u32[]{:S(2)}) collective-permute-start(f32[128,128]{1,0:T(8,128)S(1)} %add.113), channel_id=1, source_target_pairs={{0,8},{4,12},{8,0},{12,4},{16,24},{20,28},{24,16},{28,20},{32,40},... | collective-permute-start | bytes 196616 | tf_op jit(solution)/shard_map/ppermute | solution.py:25
  68.0 2.2 %collective-permute-done.6 = f32[128,128]{1,0:T(8,128)S(1)} collective-permute-done((f32[128,128]{1,0:T(8,128)S(1)}, f32[128,128]{1,0:T(8,128)S(1)}, u32[]{:S(2)}, u32[]{:S(2)}) %collective-permute-start.6) | collective-permute-done | bytes 65568 | tf_op jit(solution)/shard_map/ppermute | solution.py:25
  70.2 3.7 %collective-permute-start.7 = (f32[128,128]{1,0:T(8,128)S(1)}, f32[128,128]{1,0:T(8,128)S(1)}, u32[]{:S(2)}, u32[]{:S(2)}) collective-permute-start(f32[128,128]{1,0:T(8,128)S(1)} %add.114), channel_id=1, source_target_pairs={{0,24},{4,28},{8,16},{12,20},{16,8},{20,12},{24,0},{28,4},{32,56},... | collective-permute-start | bytes 196616 | tf_op jit(solution)/shard_map/ppermute | solution.py:25
  73.9 3.2 %collective-permute-done.7 = f32[128,128]{1,0:T(8,128)S(1)} collective-permute-done((f32[128,128]{1,0:T(8,128)S(1)}, f32[128,128]{1,0:T(8,128)S(1)}, u32[]{:S(2)}, u32[]{:S(2)}) %collective-permute-start.7) | collective-permute-done | bytes 65568 | tf_op jit(solution)/shard_map/ppermute | solution.py:25
  77.1 0.6 multiply_reduce_fusion
  77.7 1.5 %collective-permute-start.8 = (f32[]{:T(128)}, f32[]{:T(128)}, u32[]{:S(2)}, u32[]{:S(2)}) collective-permute-start(f32[]{:T(128)} %get-tuple-element.15), channel_id=1, source_target_pairs={{0,1},{1,0},{2,3},{3,2},{4,5},{5,4},{6,7},{7,6},{8,9},{9,8},{10,11... | collective-permute-start | bytes 20 | tf_op jit(solution)/shard_map/ppermute | solution.py:25
  79.2 2.3 %collective-permute-done.8 = f32[]{:T(128)} collective-permute-done((f32[]{:T(128)}, f32[]{:T(128)}, u32[]{:S(2)}, u32[]{:S(2)}) %collective-permute-start.8) | collective-permute-done | bytes 36 | tf_op jit(solution)/shard_map/ppermute | solution.py:25
  82.7 4.1 %collective-permute-start.9 = (f32[]{:T(128)}, f32[]{:T(128)}, u32[]{:S(2)}, u32[]{:S(2)}) collective-permute-start(f32[]{:T(128)} %add.116), channel_id=1, source_target_pairs={{0,3},{1,2},{2,1},{3,0},{4,7},{5,6},{6,5},{7,4},{8,11},{9,10},{10,... | collective-permute-start | bytes 20 | tf_op jit(solution)/shard_map/ppermute | solution.py:25
  86.9 0.8 collective-permute-done.9
  88.3 0.6 broadcast_multiply_fusion
  (12 shorter events, 0.1 us)
Async XLA Ops:
  0.6 5.3 %copy-start = (bf16[1,256,2048]{2,1,0:T(8,128)(2,1)S(1)}, bf16[1,256,2048]{2,1,0:T(8,128)(2,1)}, u32[]{:S(2)}) copy-start(bf16[1,256,2048]{2,1,0:T(8,128)(2,1)} %param.6) | copy-start | bytes 3145732
  2.1 15.6 %collective-permute-start = (bf16[128,2048]{1,0:T(8,128)(2,1)S(1)}, bf16[128,2048]{1,0:T(8,128)(2,1)S(1)}, u32[]{:S(2)}, u32[]{:S(2)}) collective-permute-start(bf16[128,2048]{1,0:T(8,128)(2,1)S(1)} %fusion), channel_id=1, source_target_pairs={{0,4},{4,8},{8,12},{12,16},{16,20},{20,24},{24,28},{28,32},{32,36}... | collective-permute-start | bytes 1572872 | tf_op jit(solution)/shard_map/ppermute | solution.py:19
  7.1 15.5 %collective-permute-start.1 = (bf16[128,2048]{1,0:T(8,128)(2,1)S(1)}, bf16[128,2048]{1,0:T(8,128)(2,1)S(1)}, u32[]{:S(2)}, u32[]{:S(2)}) collective-permute-start(bf16[128,2048]{1,0:T(8,128)(2,1)S(1)} %fusion.1), channel_id=1, source_target_pairs={{4,0},{8,4},{12,8},{16,12},{20,16},{24,20},{28,24},{32,28},{36,32}... | collective-permute-start | bytes 1572872 | tf_op jit(solution)/shard_map/ppermute | solution.py:19
  9.4 0.7 copy-start.5
  10.6 1.6 %copy-start.1 = (bf16[3,128,256]{2,1,0:T(8,128)(2,1)}, bf16[3,128,256]{2,1,0:T(8,128)(2,1)S(1)}, u32[]{:S(2)}) copy-start(bf16[3,128,256]{2,1,0:T(8,128)(2,1)S(1)} %and_convert_fusion.1.m_ref) | copy-start | bytes 589828
  10.6 0.8 copy-start.4
  17.6 4.9 %copy-start.2 = (bf16[128,2048]{1,0:T(8,128)(2,1)}, bf16[128,2048]{1,0:T(8,128)(2,1)S(1)}, u32[]{:S(2)}) copy-start(bf16[128,2048]{1,0:T(8,128)(2,1)S(1)} %collective-permute-done.prev_ref) | copy-start | bytes 1572868
  22.5 0.8 copy-start.3
  46.7 1.3 %collective-permute-start.2 = (f32[128,128]{1,0:T(8,128)S(1)}, f32[128,128]{1,0:T(8,128)S(1)}, u32[]{:S(2)}, u32[]{:S(2)}) collective-permute-start(f32[128,128]{1,0:T(8,128)S(1)} %rev.11), channel_id=1, source_target_pairs={{0,128},{128,0},{1,129},{129,1},{2,130},{130,2},{3,131},{131,3},{4... | collective-permute-start | bytes 196616 | tf_op jit(solution)/shard_map/ppermute | solution.py:25
  48.1 4.4 %collective-permute-start.3 = (f32[128,128]{1,0:T(8,128)S(1)}, f32[128,128]{1,0:T(8,128)S(1)}, u32[]{:S(2)}, u32[]{:S(2)}) collective-permute-start(f32[128,128]{1,0:T(8,128)S(1)} %add.110), channel_id=1, source_target_pairs={{0,32},{4,36},{8,40},{12,44},{16,48},{20,52},{24,56},{28,60},{32,0... | collective-permute-start | bytes 196616 | tf_op jit(solution)/shard_map/ppermute | solution.py:25
  52.4 5.6 %collective-permute-start.4 = (f32[128,128]{1,0:T(8,128)S(1)}, f32[128,128]{1,0:T(8,128)S(1)}, u32[]{:S(2)}, u32[]{:S(2)}) collective-permute-start(f32[128,128]{1,0:T(8,128)S(1)} %add.111), channel_id=1, source_target_pairs={{0,96},{4,100},{8,104},{12,108},{16,112},{20,116},{24,120},{28,124... | collective-permute-start | bytes 196616 | tf_op jit(solution)/shard_map/ppermute | solution.py:25
  58.0 4.4 %collective-permute-start.5 = (f32[128,128]{1,0:T(8,128)S(1)}, f32[128,128]{1,0:T(8,128)S(1)}, u32[]{:S(2)}, u32[]{:S(2)}) collective-permute-start(f32[128,128]{1,0:T(8,128)S(1)} %add.112), channel_id=1, source_target_pairs={{0,4},{4,0},{8,12},{12,8},{16,20},{20,16},{24,28},{28,24},{32,36},... | collective-permute-start | bytes 196616 | tf_op jit(solution)/shard_map/ppermute | solution.py:25
  62.4 7.8 %collective-permute-start.6 = (f32[128,128]{1,0:T(8,128)S(1)}, f32[128,128]{1,0:T(8,128)S(1)}, u32[]{:S(2)}, u32[]{:S(2)}) collective-permute-start(f32[128,128]{1,0:T(8,128)S(1)} %add.113), channel_id=1, source_target_pairs={{0,8},{4,12},{8,0},{12,4},{16,24},{20,28},{24,16},{28,20},{32,40},... | collective-permute-start | bytes 196616 | tf_op jit(solution)/shard_map/ppermute | solution.py:25
  70.2 6.9 %collective-permute-start.7 = (f32[128,128]{1,0:T(8,128)S(1)}, f32[128,128]{1,0:T(8,128)S(1)}, u32[]{:S(2)}, u32[]{:S(2)}) collective-permute-start(f32[128,128]{1,0:T(8,128)S(1)} %add.114), channel_id=1, source_target_pairs={{0,24},{4,28},{8,16},{12,20},{16,8},{20,12},{24,0},{28,4},{32,56},... | collective-permute-start | bytes 196616 | tf_op jit(solution)/shard_map/ppermute | solution.py:25
  77.7 3.8 %collective-permute-start.8 = (f32[]{:T(128)}, f32[]{:T(128)}, u32[]{:S(2)}, u32[]{:S(2)}) collective-permute-start(f32[]{:T(128)} %get-tuple-element.15), channel_id=1, source_target_pairs={{0,1},{1,0},{2,3},{3,2},{4,5},{5,4},{6,7},{7,6},{8,9},{9,8},{10,11... | collective-permute-start | bytes 20 | tf_op jit(solution)/shard_map/ppermute | solution.py:25
  82.7 5.0 %collective-permute-start.9 = (f32[]{:T(128)}, f32[]{:T(128)}, u32[]{:S(2)}, u32[]{:S(2)}) collective-permute-start(f32[]{:T(128)} %add.116), channel_id=1, source_target_pairs={{0,3},{1,2},{2,1},{3,0},{4,7},{5,6},{6,5},{7,4},{8,11},{9,10},{10,... | collective-permute-start | bytes 20 | tf_op jit(solution)/shard_map/ppermute | solution.py:25

commit v12 on v11

--- a/solution.py
+++ b/solution.py
@@ -153,6 +153,7 @@
     rows = q2.shape[0]
     tail = (k2[rows - FLEN:].astype(f32) * v2[rows - FLEN:].astype(f32)).astype(bf16)
     head = (g2[:FLEN].astype(f32) * q2[:FLEN].astype(f32)).astype(bf16)
+    tail, head = lax.optimization_barrier((tail, head))
     prev_tail = passed_along(tail, "ctx", 1)
     next_head = passed_along(head, "ctx", -1)
     mask, mask_t = doc_masks(seq_lengths[0], lax.axis_index("ctx") * rows, rows)

time: 89.4 us -> 88.6 us (level)
    convert_element_type x1 -> x0, other arithmetic: 1.17 us -> none  [on_device(): head = (g2[:FLEN].astype(f32) * q2[:FLEN].astype(f32)).astype(bf16)]
    unnamed x12 -> x10, local copies, waits for them, and re-layouts: 2.18 us -> 2.18 us
  transfers between devices with their start and end apart: 10 -> 10, of which waited for: 10 -> 10; matrix products, arithmetic and copies ran while one was open for 6% -> 5% of each run, Pallas kernels for 0% -> 0%
where the time goes in v12:
time: 88.6 us; the launch traced here: 88.2 us
  starting transfers between devices  27.3 us (31%)
  waiting for transfers between devices  24.9 us (28%)
  Pallas kernels  22.5 us (25%)
  other arithmetic  5.55 us (6%)
  local copies, waits for them, and re-layouts  5.35 us (6%)
  between operations  2.61 us (3%)
    pallas_call x1, Pallas kernels, grouped_conv(): pl.pallas_call(conv_kernel, grid=(tiles,), in_specs=[tok, tok, tok, tok,...  22.5 us
    ppermute x8, starting transfers between devices, doubling_sum(): partner = lax.ppermute(value, axis, [(i, i ^ mask) for i in range(count)])  21.4 us
    ppermute x8, waiting for transfers between devices, doubling_sum(): partner = lax.ppermute(value, axis, [(i, i ^ mask) for i in range(count)])  17.6 us
    ppermute x2, waiting for transfers between devices, passed_along(): lax.ppermute(value, axis, [(source, source + steps) for source in range(i...  7.34 us
    ppermute x2, starting transfers between devices, passed_along(): lax.ppermute(value, axis, [(source, source + steps) for source in range(i...  5.87 us
    unnamed x10, local copies, waits for them, and re-layouts  2.18 us
    convert_element_type x1, other arithmetic, on_device(): (k2[rows - FLEN:].astype(f32) * v2[rows - FLEN:].astype(f32)).astype(bf16)  1.91 us
  transfers between devices with their start and end apart: 10, of which 10 were waited for; matrix products, arithmetic and copies ran while one was open for 5% of the time, Pallas kernels for 0%

profile of v12, /device:TPU:32, one launch (start us, length us, event | category | flops | bytes accessed | tf_op | source)
XLA Modules:
  0.0 88.2 jit_solution(15047982152055435764)
XLA Ops:
  0.6 1.9 %fusion = (bf16[128,2048]{1,0:T(8,128)(2,1)S(1)}, bf16[128,2048]{1,0:T(8,128)(2,1)S(1)}) fusion(bf16[1,256,2048]{2,1,0:T(8,128)(2,1)} %param.8, bf16[1,256,2048]{2,1,0:T(8,128)(2,1)} %param.7, bf16[1,256,2048]{2,1,0:T(8,128)(2,1)} %param.6, bf16[1,256,2048]{2,1,0:T(8,128)(2,1)} %param.9), kind=kLoop, calls=%fused_computation.2 | loop fusion | flops 2097152 | bytes 3145728 | tf_op jit(solution)/shard_map/convert_element_type | solution.py:154
  2.5 3.8 %collective-permute-start = (bf16[128,2048]{1,0:T(8,128)(2,1)S(1)}, bf16[128,2048]{1,0:T(8,128)(2,1)S(1)}, u32[]{:S(2)}, u32[]{:S(2)}) collective-permute-start(bf16[128,2048]{1,0:T(8,128)(2,1)S(1)} %get-tuple-element.12), channel_id=1, source_target_pairs={{0,4},{4,8},{8,12},{12,16},{16,20},{20,24},{24,28},{28,32},{32,36}... | collective-permute-start | bytes 1572872 | tf_op jit(solution)/shard_map/ppermute | solution.py:19
  6.4 2.0 %collective-permute-start.1 = (bf16[128,2048]{1,0:T(8,128)(2,1)S(1)}, bf16[128,2048]{1,0:T(8,128)(2,1)S(1)}, u32[]{:S(2)}, u32[]{:S(2)}) collective-permute-start(bf16[128,2048]{1,0:T(8,128)(2,1)S(1)} %get-tuple-element.13), channel_id=1, source_target_pairs={{4,0},{8,4},{12,8},{16,12},{20,16},{24,20},{28,24},{32,28},{36,32}... | collective-permute-start | bytes 1572872 | tf_op jit(solution)/shard_map/ppermute | solution.py:19
  8.5 0.1 iota_add_fusion.1
  8.5 0.1 iota_add_fusion
  8.6 0.1 fusion.6
  8.7 0.0 copy-start.4
  8.7 0.6 copy-done.4
  9.4 0.1 copy.13
  9.5 0.1 reduce-window.8
  9.6 0.1 reduce
  9.7 0.1 select_reduce_fusion
  9.8 0.1 and_convert_fusion.1.m_ref
  9.9 0.0 copy-start
  9.9 0.0 copy-start.3
  10.0 0.7 copy-done.3
  10.7 0.1 rev.9
  10.8 0.7 concatenate.7.fq_ref
  11.5 0.1 pad.3.clone
  11.6 0.0 copy-done
  11.6 1.3 %rev.10.mr_ref = bf16[2,128,256]{2,1,0:T(8,128)(2,1)} reverse(bf16[2,128,256]{2,1,0:T(8,128)(2,1)S(1)} %slice.28), dimensions={1} | reverse | bytes 262144 | tf_op jit(solution)/shard_map/rev | solution.py:90
  12.9 0.7 maximum_maximum_fusion.fp_ref
  13.6 0.9 and_convert_fusion.mt_ref
  14.5 3.6 %collective-permute-done.prev_ref = bf16[128,2048]{1,0:T(8,128)(2,1)S(1)} collective-permute-done((bf16[128,2048]{1,0:T(8,128)(2,1)S(1)}, bf16[128,2048]{1,0:T(8,128)(2,1)S(1)}, u32[]{:S(2)}, u32[]{:S(2)}) %collective-permute-start) | collective-permute-done | bytes 524320 | tf_op jit(solution)/shard_map/ppermute | solution.py:19
  18.1 0.0 copy-start.1
  18.1 3.7 %collective-permute-done.1.next_ref = bf16[128,2048]{1,0:T(8,128)(2,1)S(1)} collective-permute-done((bf16[128,2048]{1,0:T(8,128)(2,1)S(1)}, bf16[128,2048]{1,0:T(8,128)(2,1)S(1)}, u32[]{:S(2)}, u32[]{:S(2)}) %collective-permute-start.1) | collective-permute-done | bytes 524320 | tf_op jit(solution)/shard_map/ppermute | solution.py:19
  21.8 0.0 copy-start.2
  21.8 0.0 copy-done.1
  21.8 0.8 copy-done.2
  22.6 22.5 %shard_map.101 = (bf16[256,2048]{1,0:T(8,128)(2,1)}, bf16[256,2048]{1,0:T(8,128)(2,1)}, bf16[256,2048]{1,0:T(8,128)(2,1)}, bf16[256,2048]{1,0:T(8,128)(2,1)}, f32[16,8,256]{2,1,0:T(8,128)}) custom-call(bf16[256,2048]{1,0:T(8,128)(2,1)} %bitcast.17, bf16[256,2048]{1,0:T(8,128)(2,1)} %bitcast.18, bf16[256,2048]{1,0:T(8,128)(2,1)} %bitcast.19, ...), custom_call_target="tpu_custom_call" | custom-call | tf_op jit(solution)/shard_map/pallas_call | solution.py:102
  45.1 0.8 slice.29
  46.0 0.1 rev.11
  46.0 0.1 collective-permute-start.2
  46.1 1.2 %collective-permute-done.2 = f32[128,128]{1,0:T(8,128)S(1)} collective-permute-done((f32[128,128]{1,0:T(8,128)S(1)}, f32[128,128]{1,0:T(8,128)S(1)}, u32[]{:S(2)}, u32[]{:S(2)}) %collective-permute-start.2) | collective-permute-done | bytes 65568 | tf_op jit(solution)/shard_map/ppermute | solution.py:25
  47.4 1.7 %collective-permute-start.3 = (f32[128,128]{1,0:T(8,128)S(1)}, f32[128,128]{1,0:T(8,128)S(1)}, u32[]{:S(2)}, u32[]{:S(2)}) collective-permute-start(f32[128,128]{1,0:T(8,128)S(1)} %add.110), channel_id=1, source_target_pairs={{0,32},{4,36},{8,40},{12,44},{16,48},{20,52},{24,56},{28,60},{32,0... | collective-permute-start | bytes 196616 | tf_op jit(solution)/shard_map/ppermute | solution.py:25
  49.0 2.7 %collective-permute-done.3 = f32[128,128]{1,0:T(8,128)S(1)} collective-permute-done((f32[128,128]{1,0:T(8,128)S(1)}, f32[128,128]{1,0:T(8,128)S(1)}, u32[]{:S(2)}, u32[]{:S(2)}) %collective-permute-start.3) | collective-permute-done | bytes 65568 | tf_op jit(solution)/shard_map/ppermute | solution.py:25
  51.7 3.1 %collective-permute-start.4 = (f32[128,128]{1,0:T(8,128)S(1)}, f32[128,128]{1,0:T(8,128)S(1)}, u32[]{:S(2)}, u32[]{:S(2)}) collective-permute-start(f32[128,128]{1,0:T(8,128)S(1)} %add.111), channel_id=1, source_target_pairs={{0,96},{4,100},{8,104},{12,108},{16,112},{20,116},{24,120},{28,124... | collective-permute-start | bytes 196616 | tf_op jit(solution)/shard_map/ppermute | solution.py:25
  54.8 2.5 %collective-permute-done.4 = f32[128,128]{1,0:T(8,128)S(1)} collective-permute-done((f32[128,128]{1,0:T(8,128)S(1)}, f32[128,128]{1,0:T(8,128)S(1)}, u32[]{:S(2)}, u32[]{:S(2)}) %collective-permute-start.4) | collective-permute-done | bytes 65568 | tf_op jit(solution)/shard_map/ppermute | solution.py:25
  57.3 1.7 %collective-permute-start.5 = (f32[128,128]{1,0:T(8,128)S(1)}, f32[128,128]{1,0:T(8,128)S(1)}, u32[]{:S(2)}, u32[]{:S(2)}) collective-permute-start(f32[128,128]{1,0:T(8,128)S(1)} %add.112), channel_id=1, source_target_pairs={{0,4},{4,0},{8,12},{12,8},{16,20},{20,16},{24,28},{28,24},{32,36},... | collective-permute-start | bytes 196616 | tf_op jit(solution)/shard_map/ppermute | solution.py:25
  59.0 2.6 %collective-permute-done.5 = f32[128,128]{1,0:T(8,128)S(1)} collective-permute-done((f32[128,128]{1,0:T(8,128)S(1)}, f32[128,128]{1,0:T(8,128)S(1)}, u32[]{:S(2)}, u32[]{:S(2)}) %collective-permute-start.5) | collective-permute-done | bytes 65568 | tf_op jit(solution)/shard_map/ppermute | solution.py:25
  61.7 5.6 %collective-permute-start.6 = (f32[128,128]{1,0:T(8,128)S(1)}, f32[128,128]{1,0:T(8,128)S(1)}, u32[]{:S(2)}, u32[]{:S(2)}) collective-permute-start(f32[128,128]{1,0:T(8,128)S(1)} %add.113), channel_id=1, source_target_pairs={{0,8},{4,12},{8,0},{12,4},{16,24},{20,28},{24,16},{28,20},{32,40},... | collective-permute-start | bytes 196616 | tf_op jit(solution)/shard_map/ppermute | solution.py:25
  67.3 2.2 %collective-permute-done.6 = f32[128,128]{1,0:T(8,128)S(1)} collective-permute-done((f32[128,128]{1,0:T(8,128)S(1)}, f32[128,128]{1,0:T(8,128)S(1)}, u32[]{:S(2)}, u32[]{:S(2)}) %collective-permute-start.6) | collective-permute-done | bytes 65568 | tf_op jit(solution)/shard_map/ppermute | solution.py:25
  69.5 3.7 %collective-permute-start.7 = (f32[128,128]{1,0:T(8,128)S(1)}, f32[128,128]{1,0:T(8,128)S(1)}, u32[]{:S(2)}, u32[]{:S(2)}) collective-permute-start(f32[128,128]{1,0:T(8,128)S(1)} %add.114), channel_id=1, source_target_pairs={{0,24},{4,28},{8,16},{12,20},{16,8},{20,12},{24,0},{28,4},{32,56},... | collective-permute-start | bytes 196616 | tf_op jit(solution)/shard_map/ppermute | solution.py:25
  73.2 3.2 %collective-permute-done.7 = f32[128,128]{1,0:T(8,128)S(1)} collective-permute-done((f32[128,128]{1,0:T(8,128)S(1)}, f32[128,128]{1,0:T(8,128)S(1)}, u32[]{:S(2)}, u32[]{:S(2)}) %collective-permute-start.7) | collective-permute-done | bytes 65568 | tf_op jit(solution)/shard_map/ppermute | solution.py:25
  76.4 0.6 multiply_reduce_fusion
  77.0 1.5 %collective-permute-start.8 = (f32[]{:T(128)}, f32[]{:T(128)}, u32[]{:S(2)}, u32[]{:S(2)}) collective-permute-start(f32[]{:T(128)} %get-tuple-element.19), channel_id=1, source_target_pairs={{0,1},{1,0},{2,3},{3,2},{4,5},{5,4},{6,7},{7,6},{8,9},{9,8},{10,11... | collective-permute-start | bytes 20 | tf_op jit(solution)/shard_map/ppermute | solution.py:25
  78.5 2.3 %collective-permute-done.8 = f32[]{:T(128)} collective-permute-done((f32[]{:T(128)}, f32[]{:T(128)}, u32[]{:S(2)}, u32[]{:S(2)}) %collective-permute-start.8) | collective-permute-done | bytes 36 | tf_op jit(solution)/shard_map/ppermute | solution.py:25
  82.0 4.1 %collective-permute-start.9 = (f32[]{:T(128)}, f32[]{:T(128)}, u32[]{:S(2)}, u32[]{:S(2)}) collective-permute-start(f32[]{:T(128)} %add.116), channel_id=1, source_target_pairs={{0,3},{1,2},{2,1},{3,0},{4,7},{5,6},{6,5},{7,4},{8,11},{9,10},{10,... | collective-permute-start | bytes 20 | tf_op jit(solution)/shard_map/ppermute | solution.py:25
  86.2 0.8 collective-permute-done.9
  87.6 0.6 broadcast_multiply_fusion
  (12 shorter events, 0.1 us)
Async XLA Ops:
  2.5 15.6 %collective-permute-start = (bf16[128,2048]{1,0:T(8,128)(2,1)S(1)}, bf16[128,2048]{1,0:T(8,128)(2,1)S(1)}, u32[]{:S(2)}, u32[]{:S(2)}) collective-permute-start(bf16[128,2048]{1,0:T(8,128)(2,1)S(1)} %get-tuple-element.12), channel_id=1, source_target_pairs={{0,4},{4,8},{8,12},{12,16},{16,20},{20,24},{24,28},{28,32},{32,36}... | collective-permute-start | bytes 1572872 | tf_op jit(solution)/shard_map/ppermute | solution.py:19
  6.4 15.5 %collective-permute-start.1 = (bf16[128,2048]{1,0:T(8,128)(2,1)S(1)}, bf16[128,2048]{1,0:T(8,128)(2,1)S(1)}, u32[]{:S(2)}, u32[]{:S(2)}) collective-permute-start(bf16[128,2048]{1,0:T(8,128)(2,1)S(1)} %get-tuple-element.13), channel_id=1, source_target_pairs={{4,0},{8,4},{12,8},{16,12},{20,16},{24,20},{28,24},{32,28},{36,32}... | collective-permute-start | bytes 1572872 | tf_op jit(solution)/shard_map/ppermute | solution.py:19
  8.7 0.7 copy-start.4
  9.9 1.6 %copy-start = (bf16[3,128,256]{2,1,0:T(8,128)(2,1)}, bf16[3,128,256]{2,1,0:T(8,128)(2,1)S(1)}, u32[]{:S(2)}) copy-start(bf16[3,128,256]{2,1,0:T(8,128)(2,1)S(1)} %and_convert_fusion.1.m_ref) | copy-start | bytes 589828
  9.9 0.8 copy-start.3
  18.1 3.7 %copy-start.1 = (bf16[128,2048]{1,0:T(8,128)(2,1)}, bf16[128,2048]{1,0:T(8,128)(2,1)S(1)}, u32[]{:S(2)}) copy-start(bf16[128,2048]{1,0:T(8,128)(2,1)S(1)} %collective-permute-done.prev_ref) | copy-start | bytes 1572868
  21.8 0.8 copy-start.2
  46.0 1.3 %collective-permute-start.2 = (f32[128,128]{1,0:T(8,128)S(1)}, f32[128,128]{1,0:T(8,128)S(1)}, u32[]{:S(2)}, u32[]{:S(2)}) collective-permute-start(f32[128,128]{1,0:T(8,128)S(1)} %rev.11), channel_id=1, source_target_pairs={{0,128},{128,0},{1,129},{129,1},{2,130},{130,2},{3,131},{131,3},{4... | collective-permute-start | bytes 196616 | tf_op jit(solution)/shard_map/ppermute | solution.py:25
  47.4 4.4 %collective-permute-start.3 = (f32[128,128]{1,0:T(8,128)S(1)}, f32[128,128]{1,0:T(8,128)S(1)}, u32[]{:S(2)}, u32[]{:S(2)}) collective-permute-start(f32[128,128]{1,0:T(8,128)S(1)} %add.110), channel_id=1, source_target_pairs={{0,32},{4,36},{8,40},{12,44},{16,48},{20,52},{24,56},{28,60},{32,0... | collective-permute-start | bytes 196616 | tf_op jit(solution)/shard_map/ppermute | solution.py:25
  51.7 5.6 %collective-permute-start.4 = (f32[128,128]{1,0:T(8,128)S(1)}, f32[128,128]{1,0:T(8,128)S(1)}, u32[]{:S(2)}, u32[]{:S(2)}) collective-permute-start(f32[128,128]{1,0:T(8,128)S(1)} %add.111), channel_id=1, source_target_pairs={{0,96},{4,100},{8,104},{12,108},{16,112},{20,116},{24,120},{28,124... | collective-permute-start | bytes 196616 | tf_op jit(solution)/shard_map/ppermute | solution.py:25
  57.3 4.4 %collective-permute-start.5 = (f32[128,128]{1,0:T(8,128)S(1)}, f32[128,128]{1,0:T(8,128)S(1)}, u32[]{:S(2)}, u32[]{:S(2)}) collective-permute-start(f32[128,128]{1,0:T(8,128)S(1)} %add.112), channel_id=1, source_target_pairs={{0,4},{4,0},{8,12},{12,8},{16,20},{20,16},{24,28},{28,24},{32,36},... | collective-permute-start | bytes 196616 | tf_op jit(solution)/shard_map/ppermute | solution.py:25
  61.7 7.8 %collective-permute-start.6 = (f32[128,128]{1,0:T(8,128)S(1)}, f32[128,128]{1,0:T(8,128)S(1)}, u32[]{:S(2)}, u32[]{:S(2)}) collective-permute-start(f32[128,128]{1,0:T(8,128)S(1)} %add.113), channel_id=1, source_target_pairs={{0,8},{4,12},{8,0},{12,4},{16,24},{20,28},{24,16},{28,20},{32,40},... | collective-permute-start | bytes 196616 | tf_op jit(solution)/shard_map/ppermute | solution.py:25
  69.5 6.9 %collective-permute-start.7 = (f32[128,128]{1,0:T(8,128)S(1)}, f32[128,128]{1,0:T(8,128)S(1)}, u32[]{:S(2)}, u32[]{:S(2)}) collective-permute-start(f32[128,128]{1,0:T(8,128)S(1)} %add.114), channel_id=1, source_target_pairs={{0,24},{4,28},{8,16},{12,20},{16,8},{20,12},{24,0},{28,4},{32,56},... | collective-permute-start | bytes 196616 | tf_op jit(solution)/shard_map/ppermute | solution.py:25
  77.0 3.8 %collective-permute-start.8 = (f32[]{:T(128)}, f32[]{:T(128)}, u32[]{:S(2)}, u32[]{:S(2)}) collective-permute-start(f32[]{:T(128)} %get-tuple-element.19), channel_id=1, source_target_pairs={{0,1},{1,0},{2,3},{3,2},{4,5},{5,4},{6,7},{7,6},{8,9},{9,8},{10,11... | collective-permute-start | bytes 20 | tf_op jit(solution)/shard_map/ppermute | solution.py:25
  82.0 5.0 %collective-permute-start.9 = (f32[]{:T(128)}, f32[]{:T(128)}, u32[]{:S(2)}, u32[]{:S(2)}) collective-permute-start(f32[]{:T(128)} %add.116), channel_id=1, source_target_pairs={{0,3},{1,2},{2,1},{3,0},{4,7},{5,6},{6,5},{7,4},{8,11},{9,10},{10,... | collective-permute-start | bytes 20 | tf_op jit(solution)/shard_map/ppermute | solution.py:25
